TPU v7x, 512 devices: a whole 4x8x8 slice. The times are simulated.
512 devices in a mesh: pool: 64 (over x, z, core), mp: 8 (over y).
Axes of the slice: x: 4, y: 8, z: 8, core: 2. Of those that a mesh axis runs over, the one named last changes fastest.
Arguments:
- residual_in: bfloat16 [16384, 2048], P('pool', 'mp'), may hold values from -6 to 6
- mlp_branch: bfloat16 [16384, 2048], P('pool'), may hold values from -6 to 6
- norm_gain: float32 [2048], replicated, may hold values from 0.5 to 1.5
- norm_bias: float32 [2048], replicated, may hold values from -3 to 3
- w_qkv: bfloat16 [2048, 3, 2048], P('pool', None, 'mp'), may hold values from -0.125 to 0.125
- qkv_bias: float32 [3, 2048], P(None, 'mp'), may hold values from -3 to 3
- cache_pool: bfloat16 [3072, 2, 32, 2048], P('pool', None, None, 'mp'), as said below
- w_dense: bfloat16 [2048, 2048], P('mp', 'pool'), may hold values from -0.125 to 0.125
- dense_bias: float32 [2048], replicated, may hold values from -3 to 3
- next_gain: float32 [2048], replicated, may hold values from 0.5 to 1.5
- next_bias: float32 [2048], replicated, may hold values from -3 to 3
- w_next: bfloat16 [2048, 3, 2048], P('pool', None, 'mp'), may hold values from -0.125 to 0.125
- next_qkv_bias: float32 [3, 2048], P(None, 'mp'), may hold values from -3 to 3
- token_request: int32 [16384], P('pool'), may hold values from 0 to 255, as said below
- cache_len: int32 [256], P('pool'), may hold values from 0 to 1024, as said below
- block_table: int32 [256, 32], P('pool'), may hold values from 0 to 3071, as said below
Outputs:
- hidden_out: bfloat16 [16384, 2048], P('pool', 'mp')
- next_qkv: bfloat16 [16384, 3, 2048], P('pool', None, 'mp')
Inputs may be any that keep to these rules, and one draw needn't show every extreme that they name: `token_request`: the 256 tokens of index i of pool belong to the requests i * 4 to (i+1) * 4 - 1, each request's tokens in one run, in increasing order, each request with at least one token. `cache_len`: 0 for a fresh prompt; some request has exactly 1024. `block_table`: block b is held by index b // 48 of pool; a block may appear in several lists; entries at or past a request's cached blocks are padding. Of the 128 entries of the requests of one index of pool, exactly 2 name blocks held by each index of pool. `cache_pool`: cached keys and values.
All inputs are finite; a program needn't handle non-finite values.
Results may differ from a plain program's by a relative error of at most 0.015.
Values may be sent and summed in bfloat16 or wider, within the bound.
No kernel may reach another device: no remote copies, remote signals or barrier semaphores. Data moves between devices by JAX's collectives and lax.ppermute only.
A program may use at most 128 MiB of HBM per device.

v0:
```python
import jax
import jax.numpy as jnp
from jax import lax
from jax.sharding import PartitionSpec as P

HEAD_DIM = 64
ROT = 32


epsilon = 1e-05


def layer_norm(row_data, gain_vec, bias_vec):
    values = row_data.astype(jnp.float32)
    row_mean = jnp.mean(values, axis=-1, keepdims=True)
    centered = values - row_mean
    spread = jnp.mean(centered * centered, axis=-1, keepdims=True)
    return centered * lax.rsqrt(spread + epsilon) * gain_vec + bias_vec


def rotate(head_rows, positions):
    half_rot = ROT // 2
    inverse = 10000.0 ** (-2.0 * jnp.arange(half_rot, dtype=jnp.float32) / ROT)
    angles = positions.astype(jnp.float32)[:, None] * inverse[None, :]
    cosine = jnp.cos(angles)[:, None, :]
    sine = jnp.sin(angles)[:, None, :]
    lower = head_rows[..., :half_rot]
    upper = head_rows[..., half_rot:ROT]
    return jnp.concatenate(
        [lower * cosine - upper * sine, upper * cosine + lower * sine, head_rows[..., ROT:]],
        axis=-1,
    )


def run_starts(token_request):
    tok_total = token_request.shape[0]
    token_index = jnp.arange(tok_total, dtype=jnp.int32)
    change = jnp.concatenate([jnp.ones((1,), dtype=bool), token_request[1:] != token_request[:-1]])
    return (token_index, lax.cummax(jnp.where(change, token_index, 0), axis=0))


def row_folder(left_rows, running, w_piece):
    columns_part = lax.slice_in_dim(left_rows, 0, w_piece.shape[0], axis=1)
    return running + jnp.dot(
        columns_part, w_piece.reshape(w_piece.shape[0], -1), preferred_element_type=jnp.float32
    )


def local(
    residual_in,
    mlp_branch,
    norm_gain,
    norm_bias,
    w_qkv,
    qkv_bias,
    cache_pool,
    w_dense,
    dense_bias,
    next_gain,
    next_bias,
    w_next,
    next_qkv_bias,
    token_request,
    cache_len,
    block_table,
):
    full_rows = lax.all_gather(residual_in, "mp", axis=1, tiled=True)
    tok_count = full_rows.shape[0]
    col_width = w_qkv.shape[2]
    head_count = col_width // HEAD_DIM
    normed = layer_norm(full_rows, norm_gain, norm_bias).astype(jnp.bfloat16)
    empty_sum = jnp.zeros((tok_count, 3 * col_width), jnp.float32)
    projected = row_folder(normed, empty_sum, lax.all_gather(w_qkv, "pool", axis=0, tiled=True))
    projected = (projected + qkv_bias.reshape(1, 3 * col_width)).reshape(tok_count, 3, col_width)
    token_index, starts = run_starts(token_request)
    request_count = cache_len.shape[0]
    local_req = token_request - request_count * lax.axis_index("pool")
    request_ids = jnp.arange(request_count, dtype=jnp.int32)
    request_match = local_req[:, None] == request_ids[None, :]
    cached_here = jnp.sum(jnp.where(request_match, cache_len[None, :], 0), axis=1)
    positions = cached_here + token_index - starts
    query = rotate(projected[:, 0].reshape(tok_count, head_count, HEAD_DIM), positions).astype(
        jnp.bfloat16
    )
    key_new = rotate(projected[:, 1].reshape(tok_count, head_count, HEAD_DIM), positions).astype(
        jnp.bfloat16
    )
    value_new = projected[:, 2].reshape(tok_count, head_count, HEAD_DIM).astype(jnp.bfloat16)
    pool_count = lax.axis_size("pool")
    blocks_here = cache_pool.shape[0]
    entries = block_table.reshape(-1)
    holder_order = jnp.argsort(entries // blocks_here, stable=True)
    slot_ids = (entries % blocks_here)[holder_order].reshape(pool_count, -1)
    wanted = lax.all_to_all(slot_ids, "pool", split_axis=0, concat_axis=0, tiled=True)
    packed = cache_pool[wanted.reshape(-1)].reshape((pool_count, -1) + cache_pool.shape[1:])
    arrived = lax.all_to_all(packed, "pool", split_axis=0, concat_axis=0, tiled=True)
    table_blocks = arrived.reshape((-1,) + cache_pool.shape[1:])[jnp.argsort(holder_order)]
    span = block_table.shape[1] * cache_pool.shape[2]
    slot_total = request_count * span
    cached_keys = table_blocks[:, 0].reshape(slot_total, head_count, HEAD_DIM)
    cached_values = table_blocks[:, 1].reshape(slot_total, head_count, HEAD_DIM)
    slot_index = jnp.arange(slot_total, dtype=jnp.int32)
    slot_req = slot_index // span
    slot_len = jnp.repeat(cache_len, span, total_repeat_length=slot_total)
    cache_ok = (slot_req[None, :] == local_req[:, None]) & (slot_index % span < slot_len)[None, :]
    new_ok = (token_request[None, :] == token_request[:, None]) & (
        token_index[None, :] <= token_index[:, None]
    )
    allowed = jnp.concatenate([cache_ok, new_ok], axis=1)
    key_all = jnp.concatenate([cached_keys, key_new], axis=0).transpose(1, 0, 2)
    value_all = jnp.concatenate([cached_values, value_new], axis=0).transpose(1, 0, 2)
    score_scale = HEAD_DIM ** (-0.5)

    def one_head(operands):
        q_head, k_head, v_head = operands
        scores = (
            jnp.einsum("qd,kd->qk", q_head, k_head, preferred_element_type=jnp.float32)
            * score_scale
        )
        scores = jnp.where(allowed, scores, -1e30)
        row_max = jnp.max(scores, axis=1, keepdims=True)
        weights = jnp.exp(scores - row_max)
        probs = (weights / jnp.sum(weights, axis=1, keepdims=True)).astype(jnp.bfloat16)
        return jnp.dot(probs, v_head, preferred_element_type=jnp.float32).astype(jnp.bfloat16)

    mixed = lax.map(one_head, (query.transpose(1, 0, 2), key_all, value_all))
    attended = mixed.transpose(1, 0, 2).reshape(tok_count, col_width)
    partial_out = jnp.dot(
        attended,
        lax.all_gather(w_dense, "pool", axis=1, tiled=True),
        preferred_element_type=jnp.float32,
    )
    mp_index = lax.axis_index("mp")
    dense_total = lax.psum(partial_out.astype(jnp.bfloat16), "mp").astype(jnp.float32)
    whole_hidden = (
        full_rows.astype(jnp.float32) + dense_total + dense_bias + mlp_branch.astype(jnp.float32)
    ).astype(jnp.bfloat16)
    hidden_out = lax.dynamic_slice_in_dim(whole_hidden, mp_index * col_width, col_width, 1)
    normed_next = layer_norm(whole_hidden, next_gain, next_bias).astype(jnp.bfloat16)
    next_raw = row_folder(
        normed_next, empty_sum, lax.all_gather(w_next, "pool", axis=0, tiled=True)
    )
    next_qkv = (
        (next_raw + next_qkv_bias.reshape(1, 3 * col_width))
        .astype(jnp.bfloat16)
        .reshape(tok_count, 3, col_width)
    )
    return (hidden_out, next_qkv)


def solution(mesh):
    in_specs = (
        P("pool", "mp"),
        P("pool", None),
        P(),
        P(),
        P("pool", None, "mp"),
        P(None, "mp"),
        P("pool", None, None, "mp"),
        P("mp", "pool"),
        P(),
        P(),
        P(),
        P("pool", None, "mp"),
        P(None, "mp"),
        P("pool"),
        P("pool"),
        P("pool", None),
    )
    out_specs = (P("pool", "mp"), P("pool", None, "mp"))
    return jax.shard_map(local, mesh=mesh, in_specs=in_specs, out_specs=out_specs, check_vma=False)
```

profile of v0, /device:TPU:1, one launch (start us, length us, event | category | flops | bytes accessed | tf_op | source)
XLA Modules:
  0.0 417.1 jit_solution(15002149205869213757)
XLA Ops:
  10.3 2.5 sort.34
  14.2 23.9 %all_to_all.14 = s32[64,1,2]{2,1,0:T(1,128)S(1)} all-to-all(s32[64,1,2]{2,1,0:T(1,128)S(1)} %bitcast.83), channel_id=1, replica_groups=mesh['pool'=64,'mp'=8] {'pool'}, dimensions={0} | all-to-all | bytes 1024 | tf_op jit(solution)/shard_map/all_to_all | solution.py:94
  39.6 2.8 gather_fusion.1
  42.4 5.8 %all-to-all-start.1 = ((bf16[64,2,2,32,256]{4,3,2,1,0:T(8,128)(2,1)}), bf16[64,2,2,32,256]{4,3,2,1,0:T(8,128)(2,1)}, u32[]{:S(2)}, u32[]{:S(2)}) async-start(bf16[64,2,2,32,256]{4,3,2,1,0:T(8,128)(2,1)} %bitcast.71), calls=%async_computation.1 | async-start | bytes 8388608 | tf_op jit(solution)/shard_map/all_to_all | solution.py:96
  50.4 2.5 sort.35
  53.9 2.5 fusion.51
  60.7 98.1 %all-gather.7.cloned.1.call-done = bf16[2048,3,256]{2,0,1:T(8,128)(2,1)} async-done(((bf16[32,3,256]{2,0,1:T(8,128)(2,1)}), bf16[2048,3,256]{2,0,1:T(8,128)(2,1)}) %all-gather.7.cloned.1.call-update) | async-done | bytes 3145744 | tf_op jit(solution)/shard_map/all_gather | solution.py:73
  158.8 4.7 %copy.69 = bf16[2048,3,256]{0,2,1:T(8,128)(2,1)} copy(bf16[2048,3,256]{2,0,1:T(8,128)(2,1)} %all-gather.7.cloned.1.call-done) | data formatting | bytes 6291456 | tf_op jit(solution)/shard_map/all_gather | solution.py:73
  163.5 4.0 convolution_add_fusion.1
  169.5 5.0 %gather_fusion.2 = bf16[128,2,32,256]{3,2,1,0:T(8,128)(2,1)} fusion(bf16[128,2,32,256]{3,2,1,0:T(8,128)(2,1)} %bitcast.13, s32[1024]{0:T(1024)S(1)} %pad_clamp_fusion), kind=kCustom, calls=%fused_computation.2 | custom fusion | bytes 8389120 | tf_op jit(solution)/shard_map/gather | solution.py:97
  174.4 4.7 %fusion.58 = (bf16[128,1,32,256]{3,2,1,0:T(8,128)(2,1)}, bf16[128,1,32,256]{3,2,1,0:T(8,128)(2,1)}) fusion(bf16[128,2,32,256]{3,2,1,0:T(8,128)(2,1)} %gather_fusion.2), kind=kLoop, calls=%fused_computation.109 | loop fusion | bytes 8388608 | tf_op jit(solution)/shard_map/slice | solution.py:101
  179.1 7.1 %reshape_squeeze.14 = bf16[4096,4,64]{2,1,0:T(4,128)(2,1)} reshape(bf16[128,1,32,256]{3,2,1,0:T(8,128)(2,1)} %get-tuple-element.110) | data formatting | bytes 4194304 | tf_op jit(solution)/shard_map/reshape;squeeze | solution.py:100
  186.2 17.6 %maximum_bitcast_fusion = bf16[4,4352,64]{2,0,1:T(4,128)(2,1)S(1)} fusion(bf16[256,4,64]{2,1,0:T(4,128)(2,1)S(1)} %copy.72, bf16[4096,4,64]{2,1,0:T(4,128)(2,1)} %reshape_squeeze.14), kind=kLoop, calls=%fused_computation.20 | loop fusion | flops 1114112 | bytes 4456448 | tf_op jit(solution)/shard_map/transpose | solution.py:110
  203.8 2.7 copy.75
  206.5 7.1 %reshape_squeeze.16 = bf16[4096,4,64]{2,1,0:T(4,128)(2,1)} reshape(bf16[128,1,32,256]{3,2,1,0:T(8,128)(2,1)} %get-tuple-element.109) | data formatting | bytes 4194304 | tf_op jit(solution)/shard_map/reshape;squeeze | solution.py:101
  213.6 17.7 %maximum_bitcast_fusion.1 = bf16[4,4352,64]{2,0,1:T(4,128)(2,1)S(1)} fusion(bf16[256,4,64]{2,1,0:T(4,128)(2,1)S(1)} %copy.73, bf16[4096,4,64]{2,1,0:T(4,128)(2,1)} %reshape_squeeze.16), kind=kLoop, calls=%fused_computation.21 | loop fusion | flops 1114112 | bytes 4456448 | tf_op jit(solution)/shard_map/transpose | solution.py:111
  231.3 2.7 copy.76
  234.0 21.9 %while.11 = (s32[]{:T(128)}, bf16[4,256,64]{1,2,0:T(8,128)(2,1)S(1)}, bf16[4,256,64]{1,2,0:T(8,128)(2,1)S(1)}, bf16[4,4352,64]{2,1,0:T(8,128)(2,1)}, pred[256,43...) while((s32[]{:T(128)}, bf16[4,256,64]{1,2,0:T(8,128)(2,1)S(1)}, ...), condition=%wide.region_10.11_spmd, body=%wide.region_7.10_spmd.sunk | while | flops 294141440 | bytes 16784460 | solution.py:126
  237.1 2.4 fusion.72
  248.0 2.4 fusion.72
  255.9 2.7 convolution_convert_fusion
  258.7 69.5 %all-gather.11.cloned.1.call-done = bf16[2048,3,256]{2,0,1:T(8,128)(2,1)} async-done(((bf16[32,3,256]{2,0,1:T(8,128)(2,1)}), bf16[2048,3,256]{2,0,1:T(8,128)(2,1)}) %all-gather.11.cloned.1.call-update) | async-done | bytes 3145744 | tf_op jit(solution)/shard_map/all_gather | solution.py:141
  328.2 4.7 %copy.77 = bf16[2048,3,256]{0,2,1:T(8,128)(2,1)} copy(bf16[2048,3,256]{2,0,1:T(8,128)(2,1)} %all-gather.11.cloned.1.call-done) | data formatting | bytes 6291456 | tf_op jit(solution)/shard_map/all_gather | solution.py:141
  332.9 70.9 %all-reduce.2.cloned.1.call-done = bf16[256,2048]{1,0:T(8,128)(2,1)} async-done(((bf16[256,2048]{1,0:T(8,128)(2,1)}), bf16[256,2048]{1,0:T(8,128)(2,1)}) %all-reduce.2.cloned.1.call-update) | async-done | bytes 1048592 | tf_op jit(solution)/shard_map/psum | solution.py:134
  (120 shorter events, 39.0 us)
Async XLA Ops:
  7.2 32.4 %copy-start = (bf16[48,2,32,256]{3,2,1,0:T(8,128)(2,1)S(1)}, bf16[48,2,32,256]{3,2,1,0:T(8,128)(2,1)}, u32[]{:S(2)}) copy-start(bf16[48,2,32,256]{3,2,1,0:T(8,128)(2,1)} %param.26) | copy-start | bytes 4718596
  7.2 50.4 %all-gather.5.cloned.1.call-start = ((), (), s32[]{:S(2)}) async-start(), calls=%async_computation.2 | async-start | bytes 1179648 | tf_op jit(solution)/shard_map/all_gather | solution.py:67
  7.9 150.9 %all-gather.7.cloned.1.call-start = ((), (), s32[]{:S(2)}) async-start(), calls=%async_computation.3 | async-start | bytes 3194880 | tf_op jit(solution)/shard_map/all_gather | solution.py:73
  42.4 7.4 %copy-start.10 = (f32[3,256]{1,0:T(4,128)S(1)}, f32[3,256]{1,0:T(4,128)}, u32[]{:S(2)}) copy-start(f32[3,256]{1,0:T(4,128)} %param.25) | copy-start | bytes 9220
  42.4 7.5 %copy-start.7 = (s32[256]{0:T(256)S(1)}, s32[256]{0:T(256)}, u32[]{:S(2)}) copy-start(s32[256]{0:T(256)} %param.33) | copy-start | bytes 3076
  42.4 10.7 %copy-start.8 = (s32[4]{0:T(128)S(1)}, s32[4]{0:T(128)}, u32[]{:S(2)}) copy-start(s32[4]{0:T(128)} %param.34) | copy-start | bytes 52
  42.4 11.5 %copy-start.12 = (pred[4096]{0:T(1024)(128)(4,1)S(1)}, pred[4096]{0:T(1024)(128)(4,1)}, u32[]{:S(2)}) copy-start(pred[4096]{0:T(1024)(128)(4,1)} %constant.223) | copy-start | bytes 12292
  42.4 11.5 %copy-start.13 = (pred[4096]{0:T(1024)(128)(4,1)S(1)}, pred[4096]{0:T(1024)(128)(4,1)}, u32[]{:S(2)}) copy-start(pred[4096]{0:T(1024)(128)(4,1)} %constant.224) | copy-start | bytes 12292
  42.4 11.5 %copy-start.14 = (pred[4096]{0:T(1024)(128)(4,1)S(1)}, pred[4096]{0:T(1024)(128)(4,1)}, u32[]{:S(2)}) copy-start(pred[4096]{0:T(1024)(128)(4,1)} %constant.225) | copy-start | bytes 12292
  42.4 127.0 %all-to-all-start.1 = ((bf16[64,2,2,32,256]{4,3,2,1,0:T(8,128)(2,1)}), bf16[64,2,2,32,256]{4,3,2,1,0:T(8,128)(2,1)}, u32[]{:S(2)}, u32[]{:S(2)}) async-start(bf16[64,2,2,32,256]{4,3,2,1,0:T(8,128)(2,1)} %bitcast.71), calls=%async_computation.1 | async-start | bytes 8388608 | tf_op jit(solution)/shard_map/all_to_all | solution.py:96
  48.3 207.7 %all-gather.9.cloned.1.call-start = ((), (), s32[]{:S(2)}) async-start(), calls=%async_computation.4 | async-start | bytes 1064960 | tf_op jit(solution)/shard_map/all_gather | solution.py:130
  49.0 279.2 %all-gather.11.cloned.1.call-start = ((), (), s32[]{:S(2)}) async-start(), calls=%async_computation.6 | async-start | bytes 3194880 | tf_op jit(solution)/shard_map/all_gather | solution.py:141
  49.6 354.2 %all-reduce.2.cloned.1.call-start = ((), (), s32[]{:S(2)}) async-start(), calls=%async_computation.5 | async-start | bytes 2097152 | tf_op jit(solution)/shard_map/psum | solution.py:134
  60.7 102.9 %copy-start.2 = (bf16[256,2048]{1,0:T(8,128)(2,1)S(1)}, bf16[256,2048]{1,0:T(8,128)(2,1)}, u32[]{:S(2)}) copy-start(bf16[256,2048]{1,0:T(8,128)(2,1)} %all-gather.5.cloned.1.call-done) | copy-start | bytes 3145732
  60.7 102.8 %copy-start.15 = (f32[2048]{0:T(1024)S(1)}, f32[2048]{0:T(1024)}, u32[]{:S(2)}) copy-start(f32[2048]{0:T(1024)} %param.23) | copy-start | bytes 24580
  60.7 102.8 %copy-start.16 = (f32[2048]{0:T(1024)S(1)}, f32[2048]{0:T(1024)}, u32[]{:S(2)}) copy-start(f32[2048]{0:T(1024)} %param.22) | copy-start | bytes 24580
  231.3 2.7 copy-start.6
  255.9 2.8 copy-start.11
  258.7 145.0 %copy-start.5 = (bf16[256,2048]{1,0:T(8,128)(2,1)S(1)}, bf16[256,2048]{1,0:T(8,128)(2,1)}, u32[]{:S(2)}) copy-start(bf16[256,2048]{1,0:T(8,128)(2,1)} %param.21) | copy-start | bytes 3145732
  258.7 145.0 %copy-start.9 = (f32[2048]{0:T(1024)S(1)}, f32[2048]{0:T(1024)}, u32[]{:S(2)}) copy-start(f32[2048]{0:T(1024)} %param.28) | copy-start | bytes 24580
  332.9 73.9 %copy-start.17 = (f32[2048]{0:T(1024)S(1)}, f32[2048]{0:T(1024)}, u32[]{:S(2)}) copy-start(f32[2048]{0:T(1024)} %param.30) | copy-start | bytes 24580
  332.9 73.9 %copy-start.18 = (f32[2048]{0:T(1024)S(1)}, f32[2048]{0:T(1024)}, u32[]{:S(2)}) copy-start(f32[2048]{0:T(1024)} %param.29) | copy-start | bytes 24580
  403.7 3.0 copy-start.4
  406.2 4.4 %copy-start.1 = (bf16[48,2,32,256]{3,2,1,0:T(8,128)(2,1)S(1)}, bf16[48,2,32,256]{3,2,1,0:T(8,128)(2,1)}, u32[]{:S(2)}) copy-start(bf16[48,2,32,256]{3,2,1,0:T(8,128)(2,1)} %param.26) | copy-start | bytes 4718596
  (1 other events, 1.0 us)
Sparse Core Ops, SparseCore 0:
  10.0 43.6 all-gather.4
  57.2 101.6 all-gather.6
  162.2 80.8 all-gather.8
  246.3 81.8 all-gather.10
  330.4 73.3 all-reduce.1
where the time goes:
time: 422 us; the launch traced here: 417 us
  waiting for transfers between devices  241 us (57%)
  other arithmetic  55.4 us (13%)
  local copies, waits for them, and re-layouts  49.6 us (12%)
  matrix products  26.7 us (6%)
  blocking collectives  23.9 us (6%)
  between operations  14.2 us (3%)
  starting transfers between devices  6.2 us (1%)
    all_gather x1, waiting for transfers between devices, local(): lax.all_gather(w_qkv, 'pool', axis=0, tiled=True)  98.1 us
    psum x1, waiting for transfers between devices, local(): lax.psum(partial_out.astype(jnp.bfloat16), 'mp').astype(jnp.float32)  70.9 us
    all_gather x1, waiting for transfers between devices, local(): lax.all_gather(w_next, 'pool', axis=0, tiled=True)  69.5 us
    all_to_all x1, blocking collectives, local(): lax.all_to_all(slot_ids, 'pool', split_axis=0, concat_axis=0, tiled=True)  23.9 us
    transpose x1, other arithmetic, local(): jnp.concatenate([cached_values, value_new], axis=0).transpose(1, 0, 2)  17.7 us
    transpose x1, other arithmetic, local(): key_all = jnp.concatenate([cached_keys, key_new], axis=0).transpose(1, 0, 2)  17.6 us
    dot_general x4, matrix products, one_head(): jnp.dot(probs, v_head, preferred_element_type=jnp.float32)  9.41 us
    dot_general x4, matrix products, one_head(): jnp.einsum('qd,kd->qk', q_head, k_head, preferred_element_type=jnp.float32)  9.38 us
  transfers between devices with their start and end apart: 6, of which 3 were waited for; matrix products, arithmetic and copies ran while one was open for 30% of the time, Pallas kernels for 0%

commit v1 on v0

--- a/solution.py
+++ b/solution.py
@@ -70,7 +70,23 @@
     head_count = col_width // HEAD_DIM
     normed = layer_norm(full_rows, norm_gain, norm_bias).astype(jnp.bfloat16)
     empty_sum = jnp.zeros((tok_count, 3 * col_width), jnp.float32)
-    projected = row_folder(normed, empty_sum, lax.all_gather(w_qkv, "pool", axis=0, tiled=True))
+    w_rows = w_qkv.shape[0]
+    dense_shard = w_dense.reshape(w_rows, -1)
+    joined = jnp.concatenate(
+        [w_qkv.reshape(w_rows, -1), w_next.reshape(w_rows, -1), dense_shard], axis=1
+    )
+    gathered = lax.all_gather(joined, "pool", axis=0, tiled=True)
+    qkv_cols = 3 * col_width
+    w_qkv_full = gathered[:, :qkv_cols]
+    w_next_full = gathered[:, qkv_cols : 2 * qkv_cols]
+    pool_total = lax.axis_size("pool")
+    w_dense_full = (
+        gathered[:, 2 * qkv_cols :]
+        .reshape((pool_total,) + w_dense.shape)
+        .transpose(1, 0, 2)
+        .reshape(w_dense.shape[0], -1)
+    )
+    projected = row_folder(normed, empty_sum, w_qkv_full)
     projected = (projected + qkv_bias.reshape(1, 3 * col_width)).reshape(tok_count, 3, col_width)
     token_index, starts = run_starts(token_request)
     request_count = cache_len.shape[0]
@@ -127,7 +143,7 @@
     attended = mixed.transpose(1, 0, 2).reshape(tok_count, col_width)
     partial_out = jnp.dot(
         attended,
-        lax.all_gather(w_dense, "pool", axis=1, tiled=True),
+        w_dense_full,
         preferred_element_type=jnp.float32,
     )
     mp_index = lax.axis_index("mp")
@@ -138,7 +154,7 @@
     hidden_out = lax.dynamic_slice_in_dim(whole_hidden, mp_index * col_width, col_width, 1)
     normed_next = layer_norm(whole_hidden, next_gain, next_bias).astype(jnp.bfloat16)
     next_raw = row_folder(
-        normed_next, empty_sum, lax.all_gather(w_next, "pool", axis=0, tiled=True)
+        normed_next, empty_sum, w_next_full
     )
     next_qkv = (
         (next_raw + next_qkv_bias.reshape(1, 3 * col_width))

time: 422 us -> 358 us (0.85)
  waiting for transfers between devices: 241 us -> 175 us
    all_gather x3 -> x1, waiting for transfers between devices: 168 us -> 0.01 us  [local(): gathered = lax.all_gather(joined, 'pool', axis=0, tiled=True)]
    all_to_all x1, waiting for transfers between devices: 0.01 us -> 99.8 us  [local(): lax.all_to_all(packed, 'pool', split_axis=0, concat_axis=0, tiled=True)]
    all_gather x2 -> x0, local copies, waits for them, and re-layouts: 9.4 us -> none  [the longest x1 4.71 us: local(): lax.all_gather(w_qkv, 'pool', axis=0, tiled=True)]
    reshape x0 -> x4, local copies, waits for them, and re-layouts: none -> 5.1 us  [the longest x1 3.39 us: local(): w_dense_full = gathered[:, 2 * qkv_cols:].reshape((pool_total,) + w_dense...]
  transfers between devices with their start and end apart: 6 -> 4, of which waited for: 3 -> 2; matrix products, arithmetic and copies ran while one was open for 30% -> 13% of each run, Pallas kernels for 0% -> 0%
where the time goes in v1:
time: 358 us; the launch traced here: 354 us
  waiting for transfers between devices  175 us (49%)
  other arithmetic  56.6 us (16%)
  local copies, waits for them, and re-layouts  51 us (14%)
  matrix products  27.3 us (8%)
  blocking collectives  23.9 us (7%)
  between operations  14.1 us (4%)
  starting transfers between devices  5.96 us (2%)
    all_to_all x1, waiting for transfers between devices, local(): lax.all_to_all(packed, 'pool', split_axis=0, concat_axis=0, tiled=True)  99.8 us
    psum x1, waiting for transfers between devices, local(): lax.psum(partial_out.astype(jnp.bfloat16), 'mp').astype(jnp.float32)  74 us
    all_to_all x1, blocking collectives, local(): lax.all_to_all(slot_ids, 'pool', split_axis=0, concat_axis=0, tiled=True)  23.9 us
    transpose x1, other arithmetic, local(): jnp.concatenate([cached_values, value_new], axis=0).transpose(1, 0, 2)  17.9 us
    transpose x1, other arithmetic, local(): key_all = jnp.concatenate([cached_keys, key_new], axis=0).transpose(1, 0, 2)  17.7 us
    dot_general x4, matrix products, one_head(): jnp.dot(probs, v_head, preferred_element_type=jnp.float32)  9.41 us
    dot_general x4, matrix products, one_head(): jnp.einsum('qd,kd->qk', q_head, k_head, preferred_element_type=jnp.float32)  9.37 us
  transfers between devices with their start and end apart: 4, of which 2 were waited for; matrix products, arithmetic and copies ran while one was open for 13% of the time, Pallas kernels for 0%

profile of v1, /device:TPU:1, one launch (start us, length us, event | category | flops | bytes accessed | tf_op | source)
XLA Modules:
  0.0 353.5 jit_solution(5560518545241421026)
XLA Ops:
  12.8 2.5 sort.34
  16.8 23.9 %all_to_all.14 = s32[64,1,2]{2,1,0:T(1,128)S(1)} all-to-all(s32[64,1,2]{2,1,0:T(1,128)S(1)} %bitcast.87), channel_id=1, replica_groups=mesh['pool'=64,'mp'=8] {'pool'}, dimensions={0} | all-to-all | bytes 1024 | tf_op jit(solution)/shard_map/all_to_all | solution.py:110
  42.1 2.8 gather_fusion.1
  44.9 5.8 %all-to-all-start.1 = ((bf16[64,2,2,32,256]{4,3,2,1,0:T(8,128)(2,1)}), bf16[64,2,2,32,256]{4,3,2,1,0:T(8,128)(2,1)}, u32[]{:S(2)}, u32[]{:S(2)}) async-start(bf16[64,2,2,32,256]{4,3,2,1,0:T(8,128)(2,1)} %bitcast.74), calls=%async_computation.1 | async-start | bytes 8388608 | tf_op jit(solution)/shard_map/all_to_all | solution.py:112
  51.4 2.6 sort.35
  55.1 2.6 fusion.63
  61.9 99.8 %all-to-all-done.1 = bf16[64,2,2,32,256]{4,3,2,1,0:T(8,128)(2,1)} async-done(((bf16[64,2,2,32,256]{4,3,2,1,0:T(8,128)(2,1)}), bf16[64,2,2,32,256]{4,3,2,1,0:T(8,128)(2,1)}, u32[]{:S(2)}, u32[]{:S(2)}) %all-to-all-start.1) | async-done | bytes 4194336 | tf_op jit(solution)/shard_map/all_to_all | solution.py:112
  161.6 5.0 %gather_fusion.2 = bf16[128,2,32,256]{3,2,1,0:T(8,128)(2,1)} fusion(bf16[128,2,32,256]{3,2,1,0:T(8,128)(2,1)} %bitcast.12, s32[1024]{0:T(1024)S(1)} %pad_clamp_fusion), kind=kCustom, calls=%fused_computation.2 | custom fusion | bytes 8389120 | tf_op jit(solution)/shard_map/gather | solution.py:113
  166.6 4.7 %fusion.70 = (bf16[128,1,32,256]{3,2,1,0:T(8,128)(2,1)}, bf16[128,1,32,256]{3,2,1,0:T(8,128)(2,1)}) fusion(bf16[128,2,32,256]{3,2,1,0:T(8,128)(2,1)} %gather_fusion.2), kind=kLoop, calls=%fused_computation.114 | loop fusion | bytes 8388608 | tf_op jit(solution)/shard_map/slice | solution.py:117
  171.3 7.1 %reshape_squeeze.14 = bf16[4096,4,64]{2,1,0:T(4,128)(2,1)} reshape(bf16[128,1,32,256]{3,2,1,0:T(8,128)(2,1)} %get-tuple-element.110) | data formatting | bytes 4194304 | tf_op jit(solution)/shard_map/reshape;squeeze | solution.py:116
  178.4 7.2 %reshape_squeeze.16 = bf16[4096,4,64]{2,1,0:T(4,128)(2,1)} reshape(bf16[128,1,32,256]{3,2,1,0:T(8,128)(2,1)} %get-tuple-element.109) | data formatting | bytes 4194304 | tf_op jit(solution)/shard_map/reshape;squeeze | solution.py:117
  185.6 3.9 %fusion.37 = f32[256,768]{1,0:T(8,128)} fusion(bf16[2048,1792]{1,0:T(8,128)(2,1)} %all-gather.5.cloned.1.call-done, bf16[256,2048]{1,0:T(8,128)(2,1)S(1)} %copy-done.2, f32[2048]{0:T(1024)S(1)} %copy-done.13, f32[2048]{0:T(1024)S(1)} %copy-done.14, f32[256]{0:T(256)S(1)} %add_rsqrt_fusion.1, f32[256]{0:T(256)S(1)} %broadcast_multiply_fusion.1, ...), kind=kOutput, calls=%fused_computation.49 | convolution fusion | flops 808648704 | bytes 5002240 | tf_op jit(solution)/shard_map/dot_general | solution.py:44
  191.3 17.7 %maximum_bitcast_fusion = bf16[4,4352,64]{2,0,1:T(4,128)(2,1)S(1)} fusion(bf16[256,4,64]{2,1,0:T(4,128)(2,1)S(1)} %copy.82, bf16[4096,4,64]{2,1,0:T(4,128)(2,1)} %reshape_squeeze.14), kind=kLoop, calls=%fused_computation.20 | loop fusion | flops 1114112 | bytes 4456448 | tf_op jit(solution)/shard_map/transpose | solution.py:126
  208.9 2.7 copy.85
  211.8 17.9 %maximum_bitcast_fusion.1 = bf16[4,4352,64]{2,0,1:T(4,128)(2,1)S(1)} fusion(bf16[256,4,64]{2,1,0:T(4,128)(2,1)S(1)} %copy.83, bf16[4096,4,64]{2,1,0:T(4,128)(2,1)} %reshape_squeeze.16), kind=kLoop, calls=%fused_computation.21 | loop fusion | flops 1114112 | bytes 4456448 | tf_op jit(solution)/shard_map/transpose | solution.py:127
  229.7 2.6 copy.86
  232.4 21.9 %while.11 = (s32[]{:T(128)}, bf16[4,256,64]{1,2,0:T(8,128)(2,1)S(1)}, bf16[4,256,64]{1,2,0:T(8,128)(2,1)S(1)}, bf16[4,4352,64]{2,1,0:T(8,128)(2,1)}, pred[256,43...) while((s32[]{:T(128)}, bf16[4,256,64]{1,2,0:T(8,128)(2,1)S(1)}, ...), condition=%wide.region_10.11_spmd, body=%wide.region_7.10_spmd.sunk | while | flops 294141440 | bytes 16784460 | solution.py:142
  235.5 2.4 fusion.82
  240.9 2.4 fusion.82
  246.4 2.4 fusion.82
  255.5 3.4 reshape.322
  258.9 3.5 copy.87
  264.1 74.0 %all-reduce.2.cloned.1.call-done = bf16[256,2048]{1,0:T(8,128)(2,1)} async-done(((bf16[256,2048]{1,0:T(8,128)(2,1)}), bf16[256,2048]{1,0:T(8,128)(2,1)}) %all-reduce.2.cloned.1.call-update) | async-done | bytes 1048592 | tf_op jit(solution)/shard_map/psum | solution.py:150
  341.3 3.0 fusion.43
  (116 shorter events, 39.5 us)
Async XLA Ops:
  7.2 34.9 %copy-start = (bf16[48,2,32,256]{3,2,1,0:T(8,128)(2,1)S(1)}, bf16[48,2,32,256]{3,2,1,0:T(8,128)(2,1)}, u32[]{:S(2)}) copy-start(bf16[48,2,32,256]{3,2,1,0:T(8,128)(2,1)} %param.26) | copy-start | bytes 4718596
  7.2 51.6 %all-gather.3.cloned.1.call-start = ((), (), s32[]{:S(2)}) async-start(), calls=%async_computation.2 | async-start | bytes 1179648 | tf_op jit(solution)/shard_map/all_gather | solution.py:67
  7.9 177.7 %all-gather.5.cloned.1.call-start = ((), (), s32[]{:S(2)}) async-start(), calls=%async_computation.3 | async-start | bytes 7454720 | tf_op jit(solution)/shard_map/all_gather | solution.py:78
  44.9 6.0 %copy-start.8 = (f32[3,256]{1,0:T(4,128)S(1)}, f32[3,256]{1,0:T(4,128)}, u32[]{:S(2)}) copy-start(f32[3,256]{1,0:T(4,128)} %param.25) | copy-start | bytes 9220
  44.9 6.0 %copy-start.5 = (s32[256]{0:T(256)S(1)}, s32[256]{0:T(256)}, u32[]{:S(2)}) copy-start(s32[256]{0:T(256)} %param.33) | copy-start | bytes 3076
  44.9 9.3 %copy-start.6 = (s32[4]{0:T(128)S(1)}, s32[4]{0:T(128)}, u32[]{:S(2)}) copy-start(s32[4]{0:T(128)} %param.34) | copy-start | bytes 52
  44.9 10.2 %copy-start.10 = (pred[4096]{0:T(1024)(128)(4,1)S(1)}, pred[4096]{0:T(1024)(128)(4,1)}, u32[]{:S(2)}) copy-start(pred[4096]{0:T(1024)(128)(4,1)} %constant.223) | copy-start | bytes 12292
  44.9 10.2 %copy-start.11 = (pred[4096]{0:T(1024)(128)(4,1)S(1)}, pred[4096]{0:T(1024)(128)(4,1)}, u32[]{:S(2)}) copy-start(pred[4096]{0:T(1024)(128)(4,1)} %constant.224) | copy-start | bytes 12292
  44.9 10.2 %copy-start.12 = (pred[4096]{0:T(1024)(128)(4,1)S(1)}, pred[4096]{0:T(1024)(128)(4,1)}, u32[]{:S(2)}) copy-start(pred[4096]{0:T(1024)(128)(4,1)} %constant.225) | copy-start | bytes 12292
  44.9 116.7 %all-to-all-start.1 = ((bf16[64,2,2,32,256]{4,3,2,1,0:T(8,128)(2,1)}), bf16[64,2,2,32,256]{4,3,2,1,0:T(8,128)(2,1)}, u32[]{:S(2)}, u32[]{:S(2)}) async-start(bf16[64,2,2,32,256]{4,3,2,1,0:T(8,128)(2,1)} %bitcast.74), calls=%async_computation.1 | async-start | bytes 8388608 | tf_op jit(solution)/shard_map/all_to_all | solution.py:112
  50.8 287.3 %all-reduce.2.cloned.1.call-start = ((), (), s32[]{:S(2)}) async-start(), calls=%async_computation.4 | async-start | bytes 2097152 | tf_op jit(solution)/shard_map/psum | solution.py:150
  178.4 7.2 %copy-start.2 = (bf16[256,2048]{1,0:T(8,128)(2,1)S(1)}, bf16[256,2048]{1,0:T(8,128)(2,1)}, u32[]{:S(2)}) copy-start(bf16[256,2048]{1,0:T(8,128)(2,1)} %all-gather.3.cloned.1.call-done) | copy-start | bytes 3145732
  178.4 7.2 %copy-start.13 = (f32[2048]{0:T(1024)S(1)}, f32[2048]{0:T(1024)}, u32[]{:S(2)}) copy-start(f32[2048]{0:T(1024)} %param.23) | copy-start | bytes 24580
  178.4 7.2 %copy-start.14 = (f32[2048]{0:T(1024)S(1)}, f32[2048]{0:T(1024)}, u32[]{:S(2)}) copy-start(f32[2048]{0:T(1024)} %param.22) | copy-start | bytes 24580
  229.7 2.7 copy-start.4
  258.9 5.1 %copy-start.9 = (f32[3,256]{1,0:T(4,128)S(1)}, f32[3,256]{1,0:T(4,128)}, u32[]{:S(2)}) copy-start(f32[3,256]{1,0:T(4,128)} %param.32) | copy-start | bytes 9220
  258.9 79.2 %copy-start.7 = (f32[2048]{0:T(1024)S(1)}, f32[2048]{0:T(1024)}, u32[]{:S(2)}) copy-start(f32[2048]{0:T(1024)} %param.28) | copy-start | bytes 24580
  264.0 77.3 %copy-start.15 = (f32[2048]{0:T(1024)S(1)}, f32[2048]{0:T(1024)}, u32[]{:S(2)}) copy-start(f32[2048]{0:T(1024)} %param.30) | copy-start | bytes 24580
  264.0 77.3 %copy-start.16 = (f32[2048]{0:T(1024)S(1)}, f32[2048]{0:T(1024)}, u32[]{:S(2)}) copy-start(f32[2048]{0:T(1024)} %param.29) | copy-start | bytes 24580
  340.3 1.0 copy-start.3
  340.7 6.3 %copy-start.1 = (bf16[48,2,32,256]{3,2,1,0:T(8,128)(2,1)S(1)}, bf16[48,2,32,256]{3,2,1,0:T(8,128)(2,1)}, u32[]{:S(2)}) copy-start(bf16[48,2,32,256]{3,2,1,0:T(8,128)(2,1)} %param.26) | copy-start | bytes 4718596
Sparse Core Ops, SparseCore 0:
  10.0 43.6 all-gather.2
  57.6 113.7 all-gather.4
  264.2 73.8 all-reduce.1

commit v2 on v1

--- a/solution.py
+++ b/solution.py
@@ -2,6 +2,8 @@
 import jax.numpy as jnp
 from jax import lax
 from jax.sharding import PartitionSpec as P
+from jax.experimental import pallas as pl
+from jax.experimental.pallas import tpu as pltpu
 
 HEAD_DIM = 64
 ROT = 32
@@ -44,6 +46,77 @@
     return running + jnp.dot(
         columns_part, w_piece.reshape(w_piece.shape[0], -1), preferred_element_type=jnp.float32
     )
+
+
+Q_CHUNK = 128
+PAIR = 128
+
+
+def attention_body(q_ref, kc_ref, vc_ref, kn_ref, vn_ref, keyc_ref, keyn_ref, qreq_ref, out_ref):
+    chunk = pl.program_id(0)
+    n_slots = kc_ref.shape[0] * kc_ref.shape[1] * kc_ref.shape[2]
+    n_new = kn_ref.shape[0]
+    score_scale = HEAD_DIM ** (-0.5)
+    q_req = qreq_ref[...]
+    mask_c = q_req == keyc_ref[...]
+    row_ids = chunk * Q_CHUNK + lax.broadcasted_iota(jnp.int32, (Q_CHUNK, n_new), 0)
+    col_ids = lax.broadcasted_iota(jnp.int32, (Q_CHUNK, n_new), 1)
+    mask_n = (q_req == keyn_ref[...]) & (col_ids <= row_ids)
+    lane = lax.broadcasted_iota(jnp.int32, (1, PAIR), 1)
+    nt = (((1,), (1,)), ((), ()))
+    for pair in range(out_ref.shape[1] // PAIR):
+        cols = slice(pair * PAIR, (pair + 1) * PAIR)
+        q_pair = q_ref[:, cols]
+        k_pair = kc_ref[:, :, :, cols].reshape(n_slots, PAIR)
+        v_pair = vc_ref[:, :, :, cols].reshape(n_slots, PAIR)
+        kn_pair = kn_ref[:, cols]
+        vn_pair = vn_ref[:, cols]
+        halves = []
+        for half in range(PAIR // HEAD_DIM):
+            in_head = (lane >= half * HEAD_DIM) & (lane < (half + 1) * HEAD_DIM)
+            q_head = jnp.where(in_head, q_pair, jnp.zeros_like(q_pair))
+            s_c = lax.dot_general(q_head, k_pair, nt, preferred_element_type=jnp.float32)
+            s_n = lax.dot_general(q_head, kn_pair, nt, preferred_element_type=jnp.float32)
+            s_c = jnp.where(mask_c, s_c * score_scale, -1e30)
+            s_n = jnp.where(mask_n, s_n * score_scale, -1e30)
+            row_max = jnp.maximum(
+                jnp.max(s_c, axis=1, keepdims=True), jnp.max(s_n, axis=1, keepdims=True)
+            )
+            w_c = jnp.exp(s_c - row_max)
+            w_n = jnp.exp(s_n - row_max)
+            total = jnp.sum(w_c, axis=1, keepdims=True) + jnp.sum(w_n, axis=1, keepdims=True)
+            p_c = (w_c / total).astype(jnp.bfloat16)
+            p_n = (w_n / total).astype(jnp.bfloat16)
+            o = jnp.dot(p_c, v_pair, preferred_element_type=jnp.float32) + jnp.dot(
+                p_n, vn_pair, preferred_element_type=jnp.float32
+            )
+            halves.append((in_head, o))
+        merged = jnp.where(halves[0][0], halves[0][1], halves[1][1])
+        out_ref[:, cols] = merged.astype(out_ref.dtype)
+
+
+def attention_call(query, arrived, key_new, value_new, key_req_c, key_req_n, q_req):
+    tok, width = query.shape
+    holders, per, _, blk, _ = arrived.shape
+    n_slots = holders * per * blk
+    grid = (tok // Q_CHUNK,)
+    full = lambda c: (0, 0)
+    return pl.pallas_call(
+        attention_body,
+        grid=grid,
+        in_specs=[
+            pl.BlockSpec((Q_CHUNK, width), lambda c: (c, 0)),
+            pl.BlockSpec((holders, per, None, blk, width), lambda c: (0, 0, 0, 0, 0)),
+            pl.BlockSpec((holders, per, None, blk, width), lambda c: (0, 0, 1, 0, 0)),
+            pl.BlockSpec((tok, width), full),
+            pl.BlockSpec((tok, width), full),
+            pl.BlockSpec((1, n_slots), full),
+            pl.BlockSpec((1, tok), full),
+            pl.BlockSpec((Q_CHUNK, 1), lambda c: (c, 0)),
+        ],
+        out_specs=pl.BlockSpec((Q_CHUNK, width), lambda c: (c, 0)),
+        out_shape=jax.ShapeDtypeStruct((tok, width), jnp.bfloat16),
+    )(query, arrived, arrived, key_new, value_new, key_req_c, key_req_n, q_req)
 
 
 def local(
@@ -110,37 +183,24 @@
     wanted = lax.all_to_all(slot_ids, "pool", split_axis=0, concat_axis=0, tiled=True)
     packed = cache_pool[wanted.reshape(-1)].reshape((pool_count, -1) + cache_pool.shape[1:])
     arrived = lax.all_to_all(packed, "pool", split_axis=0, concat_axis=0, tiled=True)
-    table_blocks = arrived.reshape((-1,) + cache_pool.shape[1:])[jnp.argsort(holder_order)]
     span = block_table.shape[1] * cache_pool.shape[2]
-    slot_total = request_count * span
-    cached_keys = table_blocks[:, 0].reshape(slot_total, head_count, HEAD_DIM)
-    cached_values = table_blocks[:, 1].reshape(slot_total, head_count, HEAD_DIM)
-    slot_index = jnp.arange(slot_total, dtype=jnp.int32)
-    slot_req = slot_index // span
-    slot_len = jnp.repeat(cache_len, span, total_repeat_length=slot_total)
-    cache_ok = (slot_req[None, :] == local_req[:, None]) & (slot_index % span < slot_len)[None, :]
-    new_ok = (token_request[None, :] == token_request[:, None]) & (
-        token_index[None, :] <= token_index[:, None]
-    )
-    allowed = jnp.concatenate([cache_ok, new_ok], axis=1)
-    key_all = jnp.concatenate([cached_keys, key_new], axis=0).transpose(1, 0, 2)
-    value_all = jnp.concatenate([cached_values, value_new], axis=0).transpose(1, 0, 2)
-    score_scale = HEAD_DIM ** (-0.5)
-
-    def one_head(operands):
-        q_head, k_head, v_head = operands
-        scores = (
-            jnp.einsum("qd,kd->qk", q_head, k_head, preferred_element_type=jnp.float32)
-            * score_scale
-        )
-        scores = jnp.where(allowed, scores, -1e30)
-        row_max = jnp.max(scores, axis=1, keepdims=True)
-        weights = jnp.exp(scores - row_max)
-        probs = (weights / jnp.sum(weights, axis=1, keepdims=True)).astype(jnp.bfloat16)
-        return jnp.dot(probs, v_head, preferred_element_type=jnp.float32).astype(jnp.bfloat16)
-
-    mixed = lax.map(one_head, (query.transpose(1, 0, 2), key_all, value_all))
-    attended = mixed.transpose(1, 0, 2).reshape(tok_count, col_width)
+    blk_len = cache_pool.shape[2]
+    entry_of = holder_order.astype(jnp.int32)
+    entry_req = entry_of // block_table.shape[1]
+    entry_lim = cache_len[entry_req] - (entry_of % block_table.shape[1]) * blk_len
+    pos_in_blk = jnp.arange(blk_len, dtype=jnp.int32)
+    key_req_c = jnp.where(
+        pos_in_blk[None, :] < entry_lim[:, None], entry_req[:, None], -1
+    ).reshape(1, -1)
+    attended = attention_call(
+        query.reshape(tok_count, col_width),
+        arrived,
+        key_new.reshape(tok_count, col_width),
+        value_new.reshape(tok_count, col_width),
+        key_req_c,
+        local_req.reshape(1, tok_count),
+        local_req.reshape(tok_count, 1),
+    )
     partial_out = jnp.dot(
         attended,
         w_dense_full,

time: 358 us -> 305 us (0.85)
  other arithmetic: 56.6 us -> 16 us
  local copies, waits for them, and re-layouts: 51 us -> 29 us
  matrix products: 27.3 us -> 9.72 us
  Pallas kernels: 0 us -> 13.7 us
  waiting for transfers between devices: 175 us -> 188 us
    all_gather x1, waiting for transfers between devices: 0.01 us -> 112 us  [local(): gathered = lax.all_gather(joined, 'pool', axis=0, tiled=True)]
    all_to_all x1, waiting for transfers between devices: 99.8 us -> 0.01 us  [local(): lax.all_to_all(packed, 'pool', split_axis=0, concat_axis=0, tiled=True)]
    transpose x3 -> x0, other arithmetic: 35.6 us -> none  [the longest x1 17.9 us: local(): jnp.concatenate([cached_values, value_new], axis=0).transpose(1, 0, 2)]
    dot_general x8 -> x0, matrix products: 18.8 us -> none  [the longest x4 9.41 us: one_head(): jnp.dot(probs, v_head, preferred_element_type=jnp.float32)]
    another operation x4 -> x1, local copies, waits for them, and re-layouts: 14.4 us -> 0.11 us  [the longest x1 7.16 us: local(): cached_values = table_blocks[:, 1].reshape(slot_total, head_count, HEAD_DIM)]
    pallas_call x0 -> x1, Pallas kernels: none -> 13.7 us  [attention_call(): pl.pallas_call(attention_body, grid=grid, in_specs=[pl.BlockSpec((Q_CHUNK...]
    while x2 -> x0, local copies, waits for them, and re-layouts: 5.38 us -> none  [local(): mixed = lax.map(one_head, (query.transpose(1, 0, 2), key_all, value_all))]
    slice x1, local copies, waits for them, and re-layouts: 4.7 us -> 0.07 us  [local(): cached_values = table_blocks[:, 1].reshape(slot_total, head_count, HEAD_DIM)]
  transfers between devices with their start and end apart: 4 -> 4, of which waited for: 2 -> 2; matrix products, arithmetic and copies ran while one was open for 13% -> 15% of each run, Pallas kernels for 0% -> 0%
where the time goes in v2:
time: 305 us; the launch traced here: 301 us
  waiting for transfers between devices  188 us (62%)
  local copies, waits for them, and re-layouts  29 us (10%)
  blocking collectives  23.9 us (8%)
  other arithmetic  16 us (5%)
  between operations  14 us (5%)
  Pallas kernels  13.7 us (4%)
  matrix products  9.72 us (3%)
  starting transfers between devices  6.11 us (2%)
    all_gather x1, waiting for transfers between devices, local(): gathered = lax.all_gather(joined, 'pool', axis=0, tiled=True)  112 us
    psum x1, waiting for transfers between devices, local(): lax.psum(partial_out.astype(jnp.bfloat16), 'mp').astype(jnp.float32)  75.7 us
    all_to_all x1, blocking collectives, local(): lax.all_to_all(slot_ids, 'pool', split_axis=0, concat_axis=0, tiled=True)  23.9 us
    pallas_call x1, Pallas kernels, attention_call(): pl.pallas_call(attention_body, grid=grid, in_specs=[pl.BlockSpec((Q_CHUNK...  13.7 us
    dot_general x2, matrix products, row_folder(): jnp.dot(columns_part, w_piece.reshape(w_piece.shape[0], -1), preferred_el...  6.95 us
  transfers between devices with their start and end apart: 4, of which 2 were waited for; matrix products, arithmetic and copies ran while one was open for 15% of the time, Pallas kernels for 0%

profile of v2, /device:TPU:1, one launch (start us, length us, event | category | flops | bytes accessed | tf_op | source)
XLA Modules:
  0.0 300.9 jit_solution(11248862775763650492)
XLA Ops:
  8.0 0.8 copy.44
  8.9 0.8 copy.56
  9.7 0.8 copy.55
  12.8 2.5 sort.17
  15.4 1.5 fusion.46
  16.8 2.5 fusion.41
  19.4 1.2 gather_fusion
  20.8 23.9 %all_to_all.14 = s32[64,1,2]{2,1,0:T(1,128)S(1)} all-to-all(s32[64,1,2]{2,1,0:T(1,128)S(1)} %bitcast.50), channel_id=1, replica_groups=mesh['pool'=64,'mp'=8] {'pool'}, dimensions={0} | all-to-all | bytes 1024 | tf_op jit(solution)/shard_map/all_to_all | solution.py:183
  46.1 2.9 gather_fusion.1
  49.0 5.8 %all-to-all-start.1 = ((bf16[64,2,2,32,256]{4,3,2,1,0:T(8,128)(2,1)}), bf16[64,2,2,32,256]{4,3,2,1,0:T(8,128)(2,1)}, u32[]{:S(2)}, u32[]{:S(2)}) async-start(bf16[64,2,2,32,256]{4,3,2,1,0:T(8,128)(2,1)} %bitcast.36), calls=%async_computation.1 | async-start | bytes 8388608 | tf_op jit(solution)/shard_map/all_to_all | solution.py:185
  58.3 1.5 convert_reduce_fusion
  59.8 1.6 fusion.8
  61.5 112.0 %all-gather.5.cloned.1.call-done = bf16[2048,1792]{1,0:T(8,128)(2,1)} async-done(((bf16[32,1792]{1,0:T(8,128)(2,1)}), bf16[2048,1792]{1,0:T(8,128)(2,1)}) %all-gather.5.cloned.1.call-update) | async-done | bytes 7340048 | tf_op jit(solution)/shard_map/all_gather | solution.py:151
  173.5 3.9 %fusion.19 = f32[256,768]{1,0:T(8,128)} fusion(bf16[2048,1792]{1,0:T(8,128)(2,1)} %all-gather.5.cloned.1.call-done, bf16[256,2048]{1,0:T(8,128)(2,1)S(1)} %copy-done.1, f32[2048]{0:T(1024)S(1)} %copy-done.8, f32[2048]{0:T(1024)S(1)} %copy-done.9, f32[256]{0:T(256)S(1)} %add_rsqrt_fusion.1, f32[256]{0:T(256)S(1)} %broadcast_multiply_fusion.1, f32[768]{0:T(1024)S(1)} %add.123), kind=kOutput, calls=%fused_computation.27 | convolution fusion | flops 808648704 | bytes 5002240 | tf_op jit(solution)/shard_map/dot_general | solution.py:46
  177.4 1.4 copy.45
  182.0 2.3 slice.87
  184.3 5.8 %reshape.251 = bf16[64,256,32]{2,1,0:T(8,128)(2,1)} reshape(bf16[2048,256]{1,0:T(8,128)(2,1)} %slice.87) | data formatting | bytes 2097152 | tf_op jit(solution)/shard_map/reshape | solution.py:158
  190.0 4.6 %copy.51 = bf16[256,64,32]{0,2,1:T(8,128)(2,1)} copy(bf16[256,64,32]{2,0,1:T(8,128)(2,1)} %bitcast.35) | data formatting | bytes 2097152 | tf_op jit(solution)/shard_map/transpose | solution.py:159
  194.6 13.7 %shard_map.167 = bf16[256,256]{1,0:T(8,128)(2,1)} custom-call(bf16[256,256]{1,0:T(8,128)(2,1)} %copy.48.q_ref, bf16[64,2,2,32,256]{4,3,2,1,0:T(8,128)(2,1)} %all-to-all-done.1.kc_ref.vc_ref, bf16[64,2,2,32,256]{4,3,2,1,0:T(8,128)(2,1)} %all-to-all-done.1.kc_ref.vc_ref, bf16[256,256]{1,0:T(8,128)(2,1)} %copy.49.kn_ref, bf16[256,256]{1,0:T(8,128)(2,1)} %bitcast.45, ...), custom_call_target="tpu_custom_call" | custom-call | tf_op jit(solution)/shard_map/pallas_call | solution.py:104
  208.4 2.8 convolution_convert_fusion
  211.2 75.7 %all-reduce.2.cloned.1.call-done = bf16[256,2048]{1,0:T(8,128)(2,1)} async-done(((bf16[256,2048]{1,0:T(8,128)(2,1)}), bf16[256,2048]{1,0:T(8,128)(2,1)}) %all-reduce.2.cloned.1.call-update) | async-done | bytes 1048592 | tf_op jit(solution)/shard_map/psum | solution.py:210
  286.9 2.2 convert_reduce_fusion.1
  290.2 3.0 %fusion.25 = bf16[256,768]{1,0:T(8,128)(2,1)S(1)} fusion(bf16[2048,1792]{1,0:T(8,128)(2,1)} %all-gather.5.cloned.1.call-done, bf16[256,2048]{1,0:T(8,128)(2,1)S(1)} %get-tuple-element.13, f32[2048]{0:T(1024)S(1)} %copy-done.10, f32[2048]{0:T(1024)S(1)} %copy-done.11, f32[256]{0:T(256)S(1)} %add_rsqrt_fusion, f32[256]{0:T(256)S(1)} %broadcast_multiply_fusion, ...), kind=kOutput, calls=%fused_computation.29 | convolution fusion | flops 808845312 | bytes 4609024 | tf_op jit(solution)/shard_map/dot_general | solution.py:46
  293.5 0.9 copy.53
  (80 shorter events, 12.6 us)
Async XLA Ops:
  7.2 38.9 %copy-start = (bf16[48,2,32,256]{3,2,1,0:T(8,128)(2,1)S(1)}, bf16[48,2,32,256]{3,2,1,0:T(8,128)(2,1)}, u32[]{:S(2)}) copy-start(bf16[48,2,32,256]{3,2,1,0:T(8,128)(2,1)} %param.22) | copy-start | bytes 4718596
  7.2 51.1 %all-gather.3.cloned.1.call-start = ((), (), s32[]{:S(2)}) async-start(), calls=%async_computation.2 | async-start | bytes 1179648 | tf_op jit(solution)/shard_map/all_gather | solution.py:140
  7.9 165.6 %all-gather.5.cloned.1.call-start = ((), (), s32[]{:S(2)}) async-start(), calls=%async_computation.3 | async-start | bytes 7454720 | tf_op jit(solution)/shard_map/all_gather | solution.py:151
  49.0 6.1 %copy-start.6 = (f32[3,256]{1,0:T(4,128)S(1)}, f32[3,256]{1,0:T(4,128)}, u32[]{:S(2)}) copy-start(f32[3,256]{1,0:T(4,128)} %param.21) | copy-start | bytes 9220
  49.0 6.1 %copy-start.4 = (s32[256]{0:T(256)S(1)}, s32[256]{0:T(256)}, u32[]{:S(2)}) copy-start(s32[256]{0:T(256)} %param.29) | copy-start | bytes 3076
  49.0 8.4 %copy-start.3 = (s32[4]{0:T(128)S(1)}, s32[4]{0:T(128)}, u32[]{:S(2)}) copy-start(s32[4]{0:T(128)} %param.30) | copy-start | bytes 52
  49.0 145.6 %all-to-all-start.1 = ((bf16[64,2,2,32,256]{4,3,2,1,0:T(8,128)(2,1)}), bf16[64,2,2,32,256]{4,3,2,1,0:T(8,128)(2,1)}, u32[]{:S(2)}, u32[]{:S(2)}) async-start(bf16[64,2,2,32,256]{4,3,2,1,0:T(8,128)(2,1)} %bitcast.36), calls=%async_computation.1 | async-start | bytes 8388608 | tf_op jit(solution)/shard_map/all_to_all | solution.py:185
  54.8 118.7 %copy-start.8 = (f32[2048]{0:T(1024)S(1)}, f32[2048]{0:T(1024)}, u32[]{:S(2)}) copy-start(f32[2048]{0:T(1024)} %param.19) | copy-start | bytes 24580
  54.8 118.7 %copy-start.9 = (f32[2048]{0:T(1024)S(1)}, f32[2048]{0:T(1024)}, u32[]{:S(2)}) copy-start(f32[2048]{0:T(1024)} %param.18) | copy-start | bytes 24580
  54.8 232.1 %all-reduce.2.cloned.1.call-start = ((), (), s32[]{:S(2)}) async-start(), calls=%async_computation.4 | async-start | bytes 2097152 | tf_op jit(solution)/shard_map/psum | solution.py:210
  56.5 1.8 copy-start.2
  58.3 115.2 %copy-start.1 = (bf16[256,2048]{1,0:T(8,128)(2,1)S(1)}, bf16[256,2048]{1,0:T(8,128)(2,1)}, u32[]{:S(2)}) copy-start(bf16[256,2048]{1,0:T(8,128)(2,1)} %all-gather.3.cloned.1.call-done) | copy-start | bytes 3145732
  208.4 2.8 copy-start.7
  208.4 78.6 %copy-start.5 = (f32[2048]{0:T(1024)S(1)}, f32[2048]{0:T(1024)}, u32[]{:S(2)}) copy-start(f32[2048]{0:T(1024)} %param.24) | copy-start | bytes 24580
  211.2 79.1 %copy-start.10 = (f32[2048]{0:T(1024)S(1)}, f32[2048]{0:T(1024)}, u32[]{:S(2)}) copy-start(f32[2048]{0:T(1024)} %param.26) | copy-start | bytes 24580
  211.2 79.1 %copy-start.11 = (f32[2048]{0:T(1024)S(1)}, f32[2048]{0:T(1024)}, u32[]{:S(2)}) copy-start(f32[2048]{0:T(1024)} %param.25) | copy-start | bytes 24580
Sparse Core Ops, SparseCore 0:
  10.0 43.7 all-gather.2
  57.7 115.7 all-gather.4
  211.3 75.5 all-reduce.1

commit v3 on v2

--- a/solution.py
+++ b/solution.py
@@ -46,6 +46,12 @@
     return running + jnp.dot(
         columns_part, w_piece.reshape(w_piece.shape[0], -1), preferred_element_type=jnp.float32
     )
+
+
+def mp_gather(block, mp_count):
+    spread = jnp.broadcast_to(block[None], (mp_count,) + block.shape)
+    joined = lax.all_to_all(spread, "mp", split_axis=0, concat_axis=2, tiled=True)
+    return joined.reshape(block.shape[0], mp_count * block.shape[1])
 
 
 Q_CHUNK = 128
@@ -137,14 +143,15 @@
     cache_len,
     block_table,
 ):
-    full_rows = lax.all_gather(residual_in, "mp", axis=1, tiled=True)
+    mp_count = lax.axis_size("mp")
+    full_rows = mp_gather(residual_in, mp_count)
     tok_count = full_rows.shape[0]
     col_width = w_qkv.shape[2]
     head_count = col_width // HEAD_DIM
     normed = layer_norm(full_rows, norm_gain, norm_bias).astype(jnp.bfloat16)
     empty_sum = jnp.zeros((tok_count, 3 * col_width), jnp.float32)
     w_rows = w_qkv.shape[0]
-    dense_shard = w_dense.reshape(w_rows, -1)
+    dense_shard = w_dense.T
     joined = jnp.concatenate(
         [w_qkv.reshape(w_rows, -1), w_next.reshape(w_rows, -1), dense_shard], axis=1
     )
@@ -153,12 +160,7 @@
     w_qkv_full = gathered[:, :qkv_cols]
     w_next_full = gathered[:, qkv_cols : 2 * qkv_cols]
     pool_total = lax.axis_size("pool")
-    w_dense_full = (
-        gathered[:, 2 * qkv_cols :]
-        .reshape((pool_total,) + w_dense.shape)
-        .transpose(1, 0, 2)
-        .reshape(w_dense.shape[0], -1)
-    )
+    w_dense_t = gathered[:, 2 * qkv_cols :]
     projected = row_folder(normed, empty_sum, w_qkv_full)
     projected = (projected + qkv_bias.reshape(1, 3 * col_width)).reshape(tok_count, 3, col_width)
     token_index, starts = run_starts(token_request)
@@ -201,17 +203,22 @@
         local_req.reshape(1, tok_count),
         local_req.reshape(tok_count, 1),
     )
-    partial_out = jnp.dot(
-        attended,
-        w_dense_full,
-        preferred_element_type=jnp.float32,
+    partial_out = lax.dot_general(
+        attended, w_dense_t, (((1,), (1,)), ((), ())), preferred_element_type=jnp.float32
     )
     mp_index = lax.axis_index("mp")
-    dense_total = lax.psum(partial_out.astype(jnp.bfloat16), "mp").astype(jnp.float32)
-    whole_hidden = (
-        full_rows.astype(jnp.float32) + dense_total + dense_bias + mlp_branch.astype(jnp.float32)
+    pieces = partial_out.astype(jnp.bfloat16).reshape(tok_count, mp_count, col_width)
+    arrived_sums = lax.all_to_all(pieces, "mp", split_axis=1, concat_axis=1, tiled=True)
+    dense_total = jnp.sum(arrived_sums.astype(jnp.float32), axis=1)
+    own_cols = lambda vec: lax.dynamic_slice_in_dim(vec, mp_index * col_width, col_width, 0)
+    own_mlp = lax.dynamic_slice_in_dim(mlp_branch, mp_index * col_width, col_width, 1)
+    hidden_out = (
+        residual_in.astype(jnp.float32)
+        + dense_total
+        + own_cols(dense_bias)
+        + own_mlp.astype(jnp.float32)
     ).astype(jnp.bfloat16)
-    hidden_out = lax.dynamic_slice_in_dim(whole_hidden, mp_index * col_width, col_width, 1)
+    whole_hidden = mp_gather(hidden_out, mp_count)
     normed_next = layer_norm(whole_hidden, next_gain, next_bias).astype(jnp.bfloat16)
     next_raw = row_folder(
         normed_next, empty_sum, w_next_full

time: 305 us -> 291 us (0.954); the launches traced: 301 us -> 290 us
  starting transfers between devices: 6.11 us -> 36.9 us
  blocking collectives: 23.9 us -> 0 us
  local copies, waits for them, and re-layouts: 29 us -> 19.3 us
  waiting for transfers between devices: 188 us -> 184 us
    all_to_all x0 -> x4, waiting for transfers between devices: none -> 90.9 us  [the longest x2 54.1 us: mp_gather(): lax.all_to_all(spread, 'mp', split_axis=0, concat_axis=2, tiled=True)]
    all_gather x1, waiting for transfers between devices: 112 us -> 34 us  [local(): gathered = lax.all_gather(joined, 'pool', axis=0, tiled=True)]
    psum x1 -> x0, waiting for transfers between devices: 75.7 us -> none  [local(): lax.psum(partial_out.astype(jnp.bfloat16), 'mp').astype(jnp.float32)]
    all_to_all x1, waiting for transfers between devices: 0.01 us -> 58.9 us  [local(): lax.all_to_all(packed, 'pool', split_axis=0, concat_axis=0, tiled=True)]
    all_to_all x0 -> x4, starting transfers between devices: none -> 31.2 us  [the longest x1 14.8 us: local(): lax.all_to_all(slot_ids, 'pool', split_axis=0, concat_axis=0, tiled=True)]
    all_to_all x1 -> x0, blocking collectives: 23.9 us -> none  [local(): lax.all_to_all(slot_ids, 'pool', split_axis=0, concat_axis=0, tiled=True)]
    reshape x2 -> x1, local copies, waits for them, and re-layouts: 5.88 us -> 1.04 us  [local(): partial_out.astype(jnp.bfloat16).reshape(tok_count, mp_count, col_width)]
    transpose x1 -> x0, local copies, waits for them, and re-layouts: 4.58 us -> none  [local(): w_dense_full = gathered[:, 2 * qkv_cols:].reshape((pool_total,) + w_dense...]
  transfers between devices with their start and end apart: 4 -> 6, of which waited for: 2 -> 6; matrix products, arithmetic and copies ran while one was open for 15% -> 9% of each run, Pallas kernels for 0% -> 0%
where the time goes in v3:
time: 291 us; the launch traced here: 290 us
  waiting for transfers between devices  184 us (63%)
  starting transfers between devices  36.9 us (13%)
  local copies, waits for them, and re-layouts  19.3 us (7%)
  between operations  14.3 us (5%)
  other arithmetic  14.1 us (5%)
  Pallas kernels  13.7 us (5%)
  matrix products  7.89 us (3%)
    all_to_all x1, waiting for transfers between devices, local(): lax.all_to_all(packed, 'pool', split_axis=0, concat_axis=0, tiled=True)  58.9 us
    all_to_all x2, waiting for transfers between devices, mp_gather(): lax.all_to_all(spread, 'mp', split_axis=0, concat_axis=2, tiled=True)  54.1 us
    all_gather x1, waiting for transfers between devices, local(): gathered = lax.all_gather(joined, 'pool', axis=0, tiled=True)  34 us
    all_to_all x1, waiting for transfers between devices, local(): lax.all_to_all(pieces, 'mp', split_axis=1, concat_axis=1, tiled=True)  28.6 us
    all_to_all x1, starting transfers between devices, local(): lax.all_to_all(slot_ids, 'pool', split_axis=0, concat_axis=0, tiled=True)  14.8 us
    pallas_call x1, Pallas kernels, attention_call(): pl.pallas_call(attention_body, grid=grid, in_specs=[pl.BlockSpec((Q_CHUNK...  13.7 us
    all_to_all x2, starting transfers between devices, mp_gather(): lax.all_to_all(spread, 'mp', split_axis=0, concat_axis=2, tiled=True)  10.4 us
    all_to_all x1, waiting for transfers between devices, local(): lax.all_to_all(slot_ids, 'pool', split_axis=0, concat_axis=0, tiled=True)  8.26 us
  transfers between devices with their start and end apart: 6, of which 6 were waited for; matrix products, arithmetic and copies ran while one was open for 9% of the time, Pallas kernels for 0%

profile of v3, /device:TPU:1, one launch (start us, length us, event | category | flops | bytes accessed | tf_op | source)
XLA Modules:
  0.0 290.1 jit_solution(7314189937018658190)
XLA Ops:
  8.9 1.4 pad_maximum_fusion.2
  12.0 2.5 sort.17
  14.5 1.5 fusion.33
  16.0 2.5 fusion.29
  18.5 1.2 gather_fusion
  20.5 14.8 %all-to-all-start.1 = ((s32[64,1,2]{2,1,0:T(1,128)}), s32[64,1,2]{2,1,0:T(1,128)S(1)}, u32[]{:S(2)}, u32[]{:S(2)}) async-start(s32[64,1,2]{2,1,0:T(1,128)} %bitcast.9), calls=%async_computation.1 | async-start | bytes 65536 | tf_op jit(solution)/shard_map/all_to_all | solution.py:185
  36.4 8.3 %all-to-all-done.1 = s32[64,1,2]{2,1,0:T(1,128)S(1)} async-done(((s32[64,1,2]{2,1,0:T(1,128)}), s32[64,1,2]{2,1,0:T(1,128)S(1)}, u32[]{:S(2)}, u32[]{:S(2)}) %all-to-all-start.1) | async-done | bytes 544 | tf_op jit(solution)/shard_map/all_to_all | solution.py:185
  45.7 6.7 %all-to-all-start = ((bf16[8,256,256]{1,2,0:T(8,128)(2,1)}), bf16[8,256,256]{1,2,0:T(8,128)(2,1)S(1)}, u32[]{:S(2)}, u32[]{:S(2)}) async-start(bf16[8,256,256]{1,2,0:T(8,128)(2,1)} %broadcast_in_dim.34), calls=%async_computation | async-start | bytes 2097152 | tf_op jit(solution)/shard_map/all_to_all | solution.py:53
  53.8 2.9 gather_fusion.1
  56.7 24.9 %all-to-all-done = bf16[8,256,256]{1,2,0:T(8,128)(2,1)S(1)} async-done(((bf16[8,256,256]{1,2,0:T(8,128)(2,1)}), bf16[8,256,256]{1,2,0:T(8,128)(2,1)S(1)}, u32[]{:S(2)}, u32[]{:S(2)}) %all-to-all-start) | async-done | bytes 1048608 | tf_op jit(solution)/shard_map/all_to_all | solution.py:53
  81.6 5.7 %all-to-all-start.2 = ((bf16[64,2,2,32,256]{4,3,2,1,0:T(8,128)(2,1)}), bf16[64,2,2,32,256]{4,3,2,1,0:T(8,128)(2,1)}, u32[]{:S(2)}, u32[]{:S(2)}) async-start(bf16[64,2,2,32,256]{4,3,2,1,0:T(8,128)(2,1)} %bitcast.77), calls=%async_computation.2 | async-start | bytes 8388608 | tf_op jit(solution)/shard_map/all_to_all | solution.py:187
  90.6 1.5 fusion.11
  92.1 34.0 %all-gather.2.cloned.1.call-done = bf16[2048,1792]{1,0:T(8,128)(2,1)} async-done(((bf16[32,1792]{1,0:T(8,128)(2,1)}), bf16[2048,1792]{1,0:T(8,128)(2,1)}) %all-gather.2.cloned.1.call-update) | async-done | bytes 7340048 | tf_op jit(solution)/shard_map/all_gather | solution.py:158
  126.1 3.2 %fusion.16 = f32[256,768]{1,0:T(8,128)S(1)} fusion(bf16[256,2048]{0,1:T(8,128)(2,1)} %fusion.11, bf16[2048,1792]{1,0:T(8,128)(2,1)} %all-gather.2.cloned.1.call-done, f32[768]{0:T(1024)S(1)} %add.122), kind=kOutput, calls=%fused_computation.24 | convolution fusion | flops 805502976 | bytes 4983808 | tf_op jit(solution)/shard_map/dot_general | solution.py:46
  132.0 58.9 %all-to-all-done.2.kc_ref.vc_ref = bf16[64,2,2,32,256]{4,3,2,1,0:T(8,128)(2,1)} async-done(((bf16[64,2,2,32,256]{4,3,2,1,0:T(8,128)(2,1)}), bf16[64,2,2,32,256]{4,3,2,1,0:T(8,128)(2,1)}, u32[]{:S(2)}, u32[]{:S(2)}) %all-to-all-start.2) | async-done | bytes 4194336 | tf_op jit(solution)/shard_map/all_to_all | solution.py:187
  190.9 13.7 %shard_map.167 = bf16[256,256]{1,0:T(8,128)(2,1)} custom-call(bf16[256,256]{1,0:T(8,128)(2,1)} %copy.49.q_ref, bf16[64,2,2,32,256]{4,3,2,1,0:T(8,128)(2,1)} %all-to-all-done.2.kc_ref.vc_ref, bf16[64,2,2,32,256]{4,3,2,1,0:T(8,128)(2,1)} %all-to-all-done.2.kc_ref.vc_ref, bf16[256,256]{1,0:T(8,128)(2,1)} %copy.50.kn_ref, bf16[256,256]{1,0:T(8,128)(2,1)} %bitcast.87, ...), custom_call_target="tpu_custom_call" | custom-call | tf_op jit(solution)/shard_map/pallas_call | solution.py:110
  204.7 1.8 convolution_convert_fusion
  206.4 1.0 copy.61
  207.5 5.9 %all-to-all-start.3 = ((bf16[256,8,256]{2,0,1:T(8,128)(2,1)}), bf16[256,8,256]{2,0,1:T(8,128)(2,1)S(1)}, u32[]{:S(2)}, u32[]{:S(2)}) async-start(bf16[256,8,256]{2,0,1:T(8,128)(2,1)} %bitcast.78), calls=%async_computation.3 | async-start | bytes 2097152 | tf_op jit(solution)/shard_map/all_to_all | solution.py:211
  214.2 28.6 %all-to-all-done.3 = bf16[256,8,256]{2,0,1:T(8,128)(2,1)S(1)} async-done(((bf16[256,8,256]{2,0,1:T(8,128)(2,1)}), bf16[256,8,256]{2,0,1:T(8,128)(2,1)S(1)}, u32[]{:S(2)}, u32[]{:S(2)}) %all-to-all-start.3) | async-done | bytes 1048608 | tf_op jit(solution)/shard_map/all_to_all | solution.py:211
  244.0 1.0 broadcast_in_dim.47
  245.1 3.7 %all-to-all-start.4 = ((bf16[8,256,256]{1,2,0:T(8,128)(2,1)}), bf16[8,256,256]{1,2,0:T(8,128)(2,1)S(1)}, u32[]{:S(2)}, u32[]{:S(2)}) async-start(bf16[8,256,256]{1,2,0:T(8,128)(2,1)} %broadcast_in_dim.47), calls=%async_computation.4 | async-start | bytes 2097152 | tf_op jit(solution)/shard_map/all_to_all | solution.py:53
  248.8 29.1 %all-to-all-done.4 = bf16[8,256,256]{1,2,0:T(8,128)(2,1)S(1)} async-done(((bf16[8,256,256]{1,2,0:T(8,128)(2,1)}), bf16[8,256,256]{1,2,0:T(8,128)(2,1)S(1)}, u32[]{:S(2)}, u32[]{:S(2)}) %all-to-all-start.4) | async-done | bytes 1048608 | tf_op jit(solution)/shard_map/all_to_all | solution.py:53
  279.3 2.9 %fusion.22 = bf16[256,768]{1,0:T(8,128)(2,1)S(1)} fusion(bf16[256,2048]{0,1:T(8,128)(2,1)S(1)} %fusion.7, bf16[2048,1792]{1,0:T(8,128)(2,1)} %all-gather.2.cloned.1.call-done, f32[768]{0:T(1024)S(1)} %add.143), kind=kOutput, calls=%fused_computation.26 | convolution fusion | flops 805699584 | bytes 4590592 | tf_op jit(solution)/shard_map/dot_general | solution.py:46
  (85 shorter events, 18.0 us)
Async XLA Ops:
  7.2 46.7 %copy-start = (bf16[48,2,32,256]{3,2,1,0:T(8,128)(2,1)S(1)}, bf16[48,2,32,256]{3,2,1,0:T(8,128)(2,1)}, u32[]{:S(2)}) copy-start(bf16[48,2,32,256]{3,2,1,0:T(8,128)(2,1)} %param.22) | copy-start | bytes 4718596
  7.2 118.9 %all-gather.2.cloned.1.call-start = ((), (), s32[]{:S(2)}) async-start(), calls=%async_computation.5 | async-start | bytes 7454720 | tf_op jit(solution)/shard_map/all_gather | solution.py:158
  20.5 24.1 %all-to-all-start.1 = ((s32[64,1,2]{2,1,0:T(1,128)}), s32[64,1,2]{2,1,0:T(1,128)S(1)}, u32[]{:S(2)}, u32[]{:S(2)}) async-start(s32[64,1,2]{2,1,0:T(1,128)} %bitcast.9), calls=%async_computation.1 | async-start | bytes 65536 | tf_op jit(solution)/shard_map/all_to_all | solution.py:185
  45.7 35.9 %all-to-all-start = ((bf16[8,256,256]{1,2,0:T(8,128)(2,1)}), bf16[8,256,256]{1,2,0:T(8,128)(2,1)S(1)}, u32[]{:S(2)}, u32[]{:S(2)}) async-start(bf16[8,256,256]{1,2,0:T(8,128)(2,1)} %broadcast_in_dim.34), calls=%async_computation | async-start | bytes 2097152 | tf_op jit(solution)/shard_map/all_to_all | solution.py:53
  81.6 5.7 %copy-start.5 = (s32[256]{0:T(256)S(1)}, s32[256]{0:T(256)}, u32[]{:S(2)}) copy-start(s32[256]{0:T(256)} %param.29) | copy-start | bytes 3076
  81.6 6.3 %copy-start.10 = (f32[3,256]{1,0:T(4,128)S(1)}, f32[3,256]{1,0:T(4,128)}, u32[]{:S(2)}) copy-start(f32[3,256]{1,0:T(4,128)} %param.21) | copy-start | bytes 9220
  81.6 8.0 %copy-start.4 = (s32[4]{0:T(128)S(1)}, s32[4]{0:T(128)}, u32[]{:S(2)}) copy-start(s32[4]{0:T(128)} %param.30) | copy-start | bytes 52
  81.6 109.3 %all-to-all-start.2 = ((bf16[64,2,2,32,256]{4,3,2,1,0:T(8,128)(2,1)}), bf16[64,2,2,32,256]{4,3,2,1,0:T(8,128)(2,1)}, u32[]{:S(2)}, u32[]{:S(2)}) async-start(bf16[64,2,2,32,256]{4,3,2,1,0:T(8,128)(2,1)} %bitcast.77), calls=%async_computation.2 | async-start | bytes 8388608 | tf_op jit(solution)/shard_map/all_to_all | solution.py:187
  87.3 3.3 %copy-start.6 = (f32[2048]{0:T(1024)S(1)}, f32[2048]{0:T(1024)}, u32[]{:S(2)}) copy-start(f32[2048]{0:T(1024)} %param.19) | copy-start | bytes 24580
  87.3 3.3 %copy-start.7 = (f32[2048]{0:T(1024)S(1)}, f32[2048]{0:T(1024)}, u32[]{:S(2)}) copy-start(f32[2048]{0:T(1024)} %param.18) | copy-start | bytes 24580
  88.7 3.4 %copy-start.3 = (s32[256]{0:T(256)}, s32[256]{0:T(256)S(1)}, u32[]{:S(2)}) copy-start(s32[256]{0:T(256)S(1)} %broadcast_subtract_fusion) | copy-start | bytes 3076
  207.5 35.4 %copy-start.1 = (bf16[256,256]{1,0:T(8,128)(2,1)S(1)}, bf16[256,256]{1,0:T(8,128)(2,1)}, u32[]{:S(2)}) copy-start(bf16[256,256]{1,0:T(8,128)(2,1)} %param.16) | copy-start | bytes 393220
  207.5 35.3 %all-to-all-start.3 = ((bf16[256,8,256]{2,0,1:T(8,128)(2,1)}), bf16[256,8,256]{2,0,1:T(8,128)(2,1)S(1)}, u32[]{:S(2)}, u32[]{:S(2)}) async-start(bf16[256,8,256]{2,0,1:T(8,128)(2,1)} %bitcast.78), calls=%async_computation.3 | async-start | bytes 2097152 | tf_op jit(solution)/shard_map/all_to_all | solution.py:211
  242.9 5.8 %copy-start.11 = (f32[3,256]{1,0:T(4,128)S(1)}, f32[3,256]{1,0:T(4,128)}, u32[]{:S(2)}) copy-start(f32[3,256]{1,0:T(4,128)} %param.28) | copy-start | bytes 9220
  243.9 34.3 %copy-start.2 = (bf16[256,256]{1,0:T(8,128)(2,1)}, bf16[256,256]{1,0:T(8,128)(2,1)S(1)}, u32[]{:S(2)}) copy-start(bf16[256,256]{1,0:T(8,128)(2,1)S(1)} %add_convert_fusion) | copy-start | bytes 393220
  245.0 33.5 %copy-start.8 = (f32[2048]{0:T(1024)S(1)}, f32[2048]{0:T(1024)}, u32[]{:S(2)}) copy-start(f32[2048]{0:T(1024)} %param.26) | copy-start | bytes 24580
  245.1 33.5 %copy-start.9 = (f32[2048]{0:T(1024)S(1)}, f32[2048]{0:T(1024)}, u32[]{:S(2)}) copy-start(f32[2048]{0:T(1024)} %param.25) | copy-start | bytes 24580
  245.1 32.9 %all-to-all-start.4 = ((bf16[8,256,256]{1,2,0:T(8,128)(2,1)}), bf16[8,256,256]{1,2,0:T(8,128)(2,1)S(1)}, u32[]{:S(2)}, u32[]{:S(2)}) async-start(bf16[8,256,256]{1,2,0:T(8,128)(2,1)} %broadcast_in_dim.47), calls=%async_computation.4 | async-start | bytes 2097152 | tf_op jit(solution)/shard_map/all_to_all | solution.py:53
Sparse Core Ops, SparseCore 0:
  11.9 114.1 all-gather.1

commit v4 on v3

--- a/solution.py
+++ b/solution.py
@@ -52,6 +52,17 @@
     spread = jnp.broadcast_to(block[None], (mp_count,) + block.shape)
     joined = lax.all_to_all(spread, "mp", split_axis=0, concat_axis=2, tiled=True)
     return joined.reshape(block.shape[0], mp_count * block.shape[1])
+
+
+def mp_permute_gather(block, mp_count):
+    mp_index = lax.axis_index("mp")
+    moved = [block] + [
+        lax.ppermute(block, "mp", [(src, (src + shift) % mp_count) for src in range(mp_count)])
+        for shift in range(1, mp_count)
+    ]
+    stacked = jnp.stack(moved)
+    by_source = stacked[(mp_index - jnp.arange(mp_count)) % mp_count]
+    return by_source.transpose(1, 0, 2).reshape(block.shape[0], mp_count * block.shape[1])
 
 
 Q_CHUNK = 128
@@ -144,7 +155,7 @@
     block_table,
 ):
     mp_count = lax.axis_size("mp")
-    full_rows = mp_gather(residual_in, mp_count)
+    full_rows = mp_permute_gather(residual_in, mp_count)
     tok_count = full_rows.shape[0]
     col_width = w_qkv.shape[2]
     head_count = col_width // HEAD_DIM

time: 291 us -> 268 us (0.921)
  waiting for transfers between devices: 184 us -> 119 us
  blocking collectives: 0 us -> 23.9 us
  local copies, waits for them, and re-layouts: 19.3 us -> 28.6 us
  starting transfers between devices: 36.9 us -> 44.7 us
    all_to_all x1, waiting for transfers between devices: 58.9 us -> 21 us  [local(): lax.all_to_all(packed, 'pool', split_axis=0, concat_axis=0, tiled=True)]
    ppermute x0 -> x7, starting transfers between devices: none -> 28.6 us  [mp_permute_gather(): lax.ppermute(block, 'mp', [(src, (src + shift) % mp_count) for src in ran...]
    all_to_all x2 -> x1, waiting for transfers between devices: 54.1 us -> 29.1 us  [mp_gather(): lax.all_to_all(spread, 'mp', split_axis=0, concat_axis=2, tiled=True)]
    all_to_all x0 -> x1, blocking collectives: none -> 23.9 us  [local(): lax.all_to_all(slot_ids, 'pool', split_axis=0, concat_axis=0, tiled=True)]
    all_to_all x1 -> x0, starting transfers between devices: 14.8 us -> none  [local(): lax.all_to_all(slot_ids, 'pool', split_axis=0, concat_axis=0, tiled=True)]
    all_to_all x1 -> x0, waiting for transfers between devices: 8.26 us -> none  [local(): lax.all_to_all(slot_ids, 'pool', split_axis=0, concat_axis=0, tiled=True)]
    all_to_all x2 -> x1, starting transfers between devices: 10.4 us -> 3.69 us  [mp_gather(): lax.all_to_all(spread, 'mp', split_axis=0, concat_axis=2, tiled=True)]
    unnamed x27 -> x37, local copies, waits for them, and re-layouts: 2.74 us -> 7.58 us
  transfers between devices with their start and end apart: 6 -> 11, of which waited for: 6 -> 6; matrix products, arithmetic and copies ran while one was open for 9% -> 14% of each run, Pallas kernels for 0% -> 0%
where the time goes in v4:
time: 268 us; the launch traced here: 267 us
  waiting for transfers between devices  119 us (44%)
  starting transfers between devices  44.7 us (17%)
  local copies, waits for them, and re-layouts  28.6 us (11%)
  blocking collectives  23.9 us (9%)
  other arithmetic  15.6 us (6%)
  between operations  14.5 us (5%)
  Pallas kernels  13.7 us (5%)
  matrix products  7.57 us (3%)
    all_gather x1, waiting for transfers between devices, local(): gathered = lax.all_gather(joined, 'pool', axis=0, tiled=True)  36.2 us
    all_to_all x1, waiting for transfers between devices, mp_gather(): lax.all_to_all(spread, 'mp', split_axis=0, concat_axis=2, tiled=True)  29.1 us
    ppermute x7, starting transfers between devices, mp_permute_gather(): lax.ppermute(block, 'mp', [(src, (src + shift) % mp_count) for src in ran...  28.6 us
    all_to_all x1, waiting for transfers between devices, local(): lax.all_to_all(pieces, 'mp', split_axis=1, concat_axis=1, tiled=True)  28.5 us
    all_to_all x1, blocking collectives, local(): lax.all_to_all(slot_ids, 'pool', split_axis=0, concat_axis=0, tiled=True)  23.9 us
    all_to_all x1, waiting for transfers between devices, local(): lax.all_to_all(packed, 'pool', split_axis=0, concat_axis=0, tiled=True)  21 us
    pallas_call x1, Pallas kernels, attention_call(): pl.pallas_call(attention_body, grid=grid, in_specs=[pl.BlockSpec((Q_CHUNK...  13.7 us
    unnamed x37, local copies, waits for them, and re-layouts  7.58 us
  transfers between devices with their start and end apart: 11, of which 6 were waited for; matrix products, arithmetic and copies ran while one was open for 14% of the time, Pallas kernels for 0%

profile of v4, /device:TPU:1, one launch (start us, length us, event | category | flops | bytes accessed | tf_op | source)
XLA Modules:
  0.0 267.2 jit_solution(16962969205466651255)
XLA Ops:
  12.0 2.5 sort.17
  16.0 2.5 fusion.29
  19.9 23.9 %all_to_all.28 = s32[64,1,2]{2,1,0:T(1,128)S(1)} all-to-all(s32[64,1,2]{2,1,0:T(1,128)S(1)} %bitcast.103), channel_id=1, replica_groups=mesh['pool'=64,'mp'=8] {'pool'}, dimensions={0} | all-to-all | bytes 1024 | tf_op jit(solution)/shard_map/all_to_all | solution.py:196
  45.2 2.9 %gather_fusion.2 = bf16[128,2,32,256]{3,2,1,0:T(8,128)(2,1)} fusion(bf16[48,2,32,256]{3,2,1,0:T(8,128)(2,1)S(1)} %copy-done, s32[1024]{0:T(1024)S(1)} %pad_clamp_fusion), kind=kCustom, calls=%fused_computation.2 | custom fusion | bytes 8389120 | tf_op jit(solution)/shard_map/gather | solution.py:197
  48.1 5.8 %all-to-all-start.1 = ((bf16[64,2,2,32,256]{4,3,2,1,0:T(8,128)(2,1)}), bf16[64,2,2,32,256]{4,3,2,1,0:T(8,128)(2,1)}, u32[]{:S(2)}, u32[]{:S(2)}) async-start(bf16[64,2,2,32,256]{4,3,2,1,0:T(8,128)(2,1)} %bitcast.88), calls=%async_computation.1 | async-start | bytes 8388608 | tf_op jit(solution)/shard_map/all_to_all | solution.py:198
  54.0 3.2 %collective-permute-start = (bf16[256,256]{1,0:T(8,128)(2,1)S(1)}, bf16[256,256]{1,0:T(8,128)(2,1)S(1)}, u32[]{:S(2)}, u32[]{:S(2)}) collective-permute-start(bf16[256,256]{1,0:T(8,128)(2,1)S(1)} %copy-done.2), channel_id=1, source_target_pairs={{0,1},{1,2},{2,3},{3,4},{4,5},{5,6},{6,7},{7,0},{8,9},{9,10},{10,1... | collective-permute-start | bytes 393224 | tf_op jit(solution)/shard_map/ppermute | solution.py:60
  57.2 4.2 %collective-permute-start.1 = (bf16[256,256]{1,0:T(8,128)(2,1)S(1)}, bf16[256,256]{1,0:T(8,128)(2,1)S(1)}, u32[]{:S(2)}, u32[]{:S(2)}) collective-permute-start(bf16[256,256]{1,0:T(8,128)(2,1)S(1)} %copy-done.2), channel_id=1, source_target_pairs={{0,2},{1,3},{2,4},{3,5},{4,6},{5,7},{6,0},{7,1},{8,10},{9,11},{10,... | collective-permute-start | bytes 393224 | tf_op jit(solution)/shard_map/ppermute | solution.py:60
  61.4 4.6 %collective-permute-start.2 = (bf16[256,256]{1,0:T(8,128)(2,1)S(1)}, bf16[256,256]{1,0:T(8,128)(2,1)S(1)}, u32[]{:S(2)}, u32[]{:S(2)}) collective-permute-start(bf16[256,256]{1,0:T(8,128)(2,1)S(1)} %copy-done.2), channel_id=1, source_target_pairs={{0,3},{1,4},{2,5},{3,6},{4,7},{5,0},{6,1},{7,2},{8,11},{9,12},{10,... | collective-permute-start | bytes 393224 | tf_op jit(solution)/shard_map/ppermute | solution.py:60
  66.0 3.5 %collective-permute-start.3 = (bf16[256,256]{1,0:T(8,128)(2,1)S(1)}, bf16[256,256]{1,0:T(8,128)(2,1)S(1)}, u32[]{:S(2)}, u32[]{:S(2)}) collective-permute-start(bf16[256,256]{1,0:T(8,128)(2,1)S(1)} %copy-done.2), channel_id=1, source_target_pairs={{0,4},{1,5},{2,6},{3,7},{4,0},{5,1},{6,2},{7,3},{8,12},{9,13},{10,... | collective-permute-start | bytes 393224 | tf_op jit(solution)/shard_map/ppermute | solution.py:60
  69.6 4.9 %collective-permute-start.4 = (bf16[256,256]{1,0:T(8,128)(2,1)S(1)}, bf16[256,256]{1,0:T(8,128)(2,1)S(1)}, u32[]{:S(2)}, u32[]{:S(2)}) collective-permute-start(bf16[256,256]{1,0:T(8,128)(2,1)S(1)} %copy-done.2), channel_id=1, source_target_pairs={{0,5},{1,6},{2,7},{3,0},{4,1},{5,2},{6,3},{7,4},{8,13},{9,14},{10,... | collective-permute-start | bytes 393224 | tf_op jit(solution)/shard_map/ppermute | solution.py:60
  79.0 5.0 %collective-permute-start.5 = (bf16[256,256]{1,0:T(8,128)(2,1)S(1)}, bf16[256,256]{1,0:T(8,128)(2,1)S(1)}, u32[]{:S(2)}, u32[]{:S(2)}) collective-permute-start(bf16[256,256]{1,0:T(8,128)(2,1)S(1)} %copy-done.2), channel_id=1, source_target_pairs={{0,6},{1,7},{2,0},{3,1},{4,2},{5,3},{6,4},{7,5},{8,14},{9,15},{10,... | collective-permute-start | bytes 393224 | tf_op jit(solution)/shard_map/ppermute | solution.py:60
  84.7 3.1 %collective-permute-start.6 = (bf16[256,256]{1,0:T(8,128)(2,1)S(1)}, bf16[256,256]{1,0:T(8,128)(2,1)S(1)}, u32[]{:S(2)}, u32[]{:S(2)}) collective-permute-start(bf16[256,256]{1,0:T(8,128)(2,1)S(1)} %copy-done.2), channel_id=1, source_target_pairs={{0,7},{1,0},{2,1},{3,2},{4,3},{5,4},{6,5},{7,6},{8,15},{9,8},{10,9... | collective-permute-start | bytes 393224 | tf_op jit(solution)/shard_map/ppermute | solution.py:60
  90.5 2.9 %collective-permute-done.5 = bf16[256,256]{1,0:T(8,128)(2,1)S(1)} collective-permute-done((bf16[256,256]{1,0:T(8,128)(2,1)S(1)}, bf16[256,256]{1,0:T(8,128)(2,1)S(1)}, u32[]{:S(2)}, u32[]{:S(2)}) %collective-permute-start.5) | collective-permute-done | bytes 131104 | tf_op jit(solution)/shard_map/ppermute | solution.py:60
  95.5 1.9 gather_fusion
  98.9 3.0 %copy.53 = f32[256,8,256]{0,2,1:T(8,128)} copy(f32[256,8,256]{2,0,1:T(8,128)} %convert_bitcast_fusion) | data formatting | bytes 4194304 | tf_op jit(solution)/shard_map/convert_element_type | solution.py:16
  104.3 36.2 %all-gather.2.cloned.1.call-done = bf16[2048,1792]{1,0:T(8,128)(2,1)} async-done(((bf16[32,1792]{1,0:T(8,128)(2,1)}), bf16[2048,1792]{1,0:T(8,128)(2,1)}) %all-gather.2.cloned.1.call-update) | async-done | bytes 7340048 | tf_op jit(solution)/shard_map/all_gather | solution.py:169
  140.5 2.9 %fusion.16 = f32[256,768]{1,0:T(8,128)S(1)} fusion(bf16[256,2048]{0,1:T(8,128)(2,1)S(1)} %fusion.15, bf16[2048,1792]{1,0:T(8,128)(2,1)} %all-gather.2.cloned.1.call-done, f32[768]{0:T(1024)} %add.147), kind=kOutput, calls=%fused_computation.27 | convolution fusion | flops 805502976 | bytes 4984832 | tf_op jit(solution)/shard_map/dot_general | solution.py:46
  146.5 21.0 %all-to-all-done.1.kc_ref.vc_ref = bf16[64,2,2,32,256]{4,3,2,1,0:T(8,128)(2,1)} async-done(((bf16[64,2,2,32,256]{4,3,2,1,0:T(8,128)(2,1)}), bf16[64,2,2,32,256]{4,3,2,1,0:T(8,128)(2,1)}, u32[]{:S(2)}, u32[]{:S(2)}) %all-to-all-start.1) | async-done | bytes 4194336 | tf_op jit(solution)/shard_map/all_to_all | solution.py:198
  167.4 13.7 %shard_map.167 = bf16[256,256]{1,0:T(8,128)(2,1)} custom-call(bf16[256,256]{1,0:T(8,128)(2,1)} %copy.59.q_ref, bf16[64,2,2,32,256]{4,3,2,1,0:T(8,128)(2,1)} %all-to-all-done.1.kc_ref.vc_ref, bf16[64,2,2,32,256]{4,3,2,1,0:T(8,128)(2,1)} %all-to-all-done.1.kc_ref.vc_ref, bf16[256,256]{1,0:T(8,128)(2,1)} %copy.60.kn_ref, bf16[256,256]{1,0:T(8,128)(2,1)} %bitcast.98, ...), custom_call_target="tpu_custom_call" | custom-call | tf_op jit(solution)/shard_map/pallas_call | solution.py:121
  184.0 6.6 %all-to-all-start.2 = ((bf16[256,8,256]{2,0,1:T(8,128)(2,1)}), bf16[256,8,256]{2,0,1:T(8,128)(2,1)S(1)}, u32[]{:S(2)}, u32[]{:S(2)}) async-start(bf16[256,8,256]{2,0,1:T(8,128)(2,1)} %bitcast.89), calls=%async_computation.2 | async-start | bytes 2097152 | tf_op jit(solution)/shard_map/all_to_all | solution.py:222
  191.3 28.5 %all-to-all-done.2 = bf16[256,8,256]{2,0,1:T(8,128)(2,1)S(1)} async-done(((bf16[256,8,256]{2,0,1:T(8,128)(2,1)}), bf16[256,8,256]{2,0,1:T(8,128)(2,1)S(1)}, u32[]{:S(2)}, u32[]{:S(2)}) %all-to-all-start.2) | async-done | bytes 1048608 | tf_op jit(solution)/shard_map/all_to_all | solution.py:222
  222.1 3.7 %all-to-all-start.3 = ((bf16[8,256,256]{1,2,0:T(8,128)(2,1)}), bf16[8,256,256]{1,2,0:T(8,128)(2,1)S(1)}, u32[]{:S(2)}, u32[]{:S(2)}) async-start(bf16[8,256,256]{1,2,0:T(8,128)(2,1)} %broadcast_in_dim.44), calls=%async_computation.3 | async-start | bytes 2097152 | tf_op jit(solution)/shard_map/all_to_all | solution.py:53
  225.8 29.1 %all-to-all-done.3 = bf16[8,256,256]{1,2,0:T(8,128)(2,1)S(1)} async-done(((bf16[8,256,256]{1,2,0:T(8,128)(2,1)}), bf16[8,256,256]{1,2,0:T(8,128)(2,1)S(1)}, u32[]{:S(2)}, u32[]{:S(2)}) %all-to-all-start.3) | async-done | bytes 1048608 | tf_op jit(solution)/shard_map/all_to_all | solution.py:53
  256.4 2.9 %fusion.22 = bf16[256,768]{1,0:T(8,128)(2,1)S(1)} fusion(bf16[256,2048]{0,1:T(8,128)(2,1)S(1)} %fusion.9, bf16[2048,1792]{1,0:T(8,128)(2,1)} %all-gather.2.cloned.1.call-done, f32[768]{0:T(1024)S(1)} %add.168), kind=kOutput, calls=%fused_computation.29 | convolution fusion | flops 805699584 | bytes 4590592 | tf_op jit(solution)/shard_map/dot_general | solution.py:46
  (111 shorter events, 34.2 us)
Async XLA Ops:
  7.2 38.1 %copy-start = (bf16[48,2,32,256]{3,2,1,0:T(8,128)(2,1)S(1)}, bf16[48,2,32,256]{3,2,1,0:T(8,128)(2,1)}, u32[]{:S(2)}) copy-start(bf16[48,2,32,256]{3,2,1,0:T(8,128)(2,1)} %param.22) | copy-start | bytes 4718596
  7.2 133.3 %all-gather.2.cloned.1.call-start = ((), (), s32[]{:S(2)}) async-start(), calls=%async_computation.4 | async-start | bytes 7454720 | tf_op jit(solution)/shard_map/all_gather | solution.py:169
  48.1 5.9 %copy-start.2 = (bf16[256,256]{1,0:T(8,128)(2,1)S(1)}, bf16[256,256]{1,0:T(8,128)(2,1)}, u32[]{:S(2)}) copy-start(bf16[256,256]{1,0:T(8,128)(2,1)} %param.16) | copy-start | bytes 393220
  48.1 26.4 %copy-start.7 = (s32[256]{0:T(256)S(1)}, s32[256]{0:T(256)}, u32[]{:S(2)}) copy-start(s32[256]{0:T(256)} %param.29) | copy-start | bytes 3076
  48.1 27.1 %copy-start.6 = (s32[4]{0:T(128)S(1)}, s32[4]{0:T(128)}, u32[]{:S(2)}) copy-start(s32[4]{0:T(128)} %param.30) | copy-start | bytes 52
  48.1 28.8 %copy-start.12 = (f32[3,256]{1,0:T(4,128)S(1)}, f32[3,256]{1,0:T(4,128)}, u32[]{:S(2)}) copy-start(f32[3,256]{1,0:T(4,128)} %param.21) | copy-start | bytes 9220
  48.1 119.3 %all-to-all-start.1 = ((bf16[64,2,2,32,256]{4,3,2,1,0:T(8,128)(2,1)}), bf16[64,2,2,32,256]{4,3,2,1,0:T(8,128)(2,1)}, u32[]{:S(2)}, u32[]{:S(2)}) async-start(bf16[64,2,2,32,256]{4,3,2,1,0:T(8,128)(2,1)} %bitcast.88), calls=%async_computation.1 | async-start | bytes 8388608 | tf_op jit(solution)/shard_map/all_to_all | solution.py:198
  54.0 25.1 %collective-permute-start = (bf16[256,256]{1,0:T(8,128)(2,1)S(1)}, bf16[256,256]{1,0:T(8,128)(2,1)S(1)}, u32[]{:S(2)}, u32[]{:S(2)}) collective-permute-start(bf16[256,256]{1,0:T(8,128)(2,1)S(1)} %copy-done.2), channel_id=1, source_target_pairs={{0,1},{1,2},{2,3},{3,4},{4,5},{5,6},{6,7},{7,0},{8,9},{9,10},{10,1... | collective-permute-start | bytes 393224 | tf_op jit(solution)/shard_map/ppermute | solution.py:60
  57.2 27.5 %collective-permute-start.1 = (bf16[256,256]{1,0:T(8,128)(2,1)S(1)}, bf16[256,256]{1,0:T(8,128)(2,1)S(1)}, u32[]{:S(2)}, u32[]{:S(2)}) collective-permute-start(bf16[256,256]{1,0:T(8,128)(2,1)S(1)} %copy-done.2), channel_id=1, source_target_pairs={{0,2},{1,3},{2,4},{3,5},{4,6},{5,7},{6,0},{7,1},{8,10},{9,11},{10,... | collective-permute-start | bytes 393224 | tf_op jit(solution)/shard_map/ppermute | solution.py:60
  61.4 27.1 %collective-permute-start.2 = (bf16[256,256]{1,0:T(8,128)(2,1)S(1)}, bf16[256,256]{1,0:T(8,128)(2,1)S(1)}, u32[]{:S(2)}, u32[]{:S(2)}) collective-permute-start(bf16[256,256]{1,0:T(8,128)(2,1)S(1)} %copy-done.2), channel_id=1, source_target_pairs={{0,3},{1,4},{2,5},{3,6},{4,7},{5,0},{6,1},{7,2},{8,11},{9,12},{10,... | collective-permute-start | bytes 393224 | tf_op jit(solution)/shard_map/ppermute | solution.py:60
  66.0 23.1 %collective-permute-start.3 = (bf16[256,256]{1,0:T(8,128)(2,1)S(1)}, bf16[256,256]{1,0:T(8,128)(2,1)S(1)}, u32[]{:S(2)}, u32[]{:S(2)}) collective-permute-start(bf16[256,256]{1,0:T(8,128)(2,1)S(1)} %copy-done.2), channel_id=1, source_target_pairs={{0,4},{1,5},{2,6},{3,7},{4,0},{5,1},{6,2},{7,3},{8,12},{9,13},{10,... | collective-permute-start | bytes 393224 | tf_op jit(solution)/shard_map/ppermute | solution.py:60
  69.6 20.2 %collective-permute-start.4 = (bf16[256,256]{1,0:T(8,128)(2,1)S(1)}, bf16[256,256]{1,0:T(8,128)(2,1)S(1)}, u32[]{:S(2)}, u32[]{:S(2)}) collective-permute-start(bf16[256,256]{1,0:T(8,128)(2,1)S(1)} %copy-done.2), channel_id=1, source_target_pairs={{0,5},{1,6},{2,7},{3,0},{4,1},{5,2},{6,3},{7,4},{8,13},{9,14},{10,... | collective-permute-start | bytes 393224 | tf_op jit(solution)/shard_map/ppermute | solution.py:60
  75.2 3.8 %copy-start.5 = (s32[256]{0:T(256)}, s32[256]{0:T(256)S(1)}, u32[]{:S(2)}) copy-start(s32[256]{0:T(256)S(1)} %broadcast_subtract_fusion) | copy-start | bytes 3076
  79.0 14.3 %collective-permute-start.5 = (bf16[256,256]{1,0:T(8,128)(2,1)S(1)}, bf16[256,256]{1,0:T(8,128)(2,1)S(1)}, u32[]{:S(2)}, u32[]{:S(2)}) collective-permute-start(bf16[256,256]{1,0:T(8,128)(2,1)S(1)} %copy-done.2), channel_id=1, source_target_pairs={{0,6},{1,7},{2,0},{3,1},{4,2},{5,3},{6,4},{7,5},{8,14},{9,15},{10,... | collective-permute-start | bytes 393224 | tf_op jit(solution)/shard_map/ppermute | solution.py:60
  84.7 10.2 %collective-permute-start.6 = (bf16[256,256]{1,0:T(8,128)(2,1)S(1)}, bf16[256,256]{1,0:T(8,128)(2,1)S(1)}, u32[]{:S(2)}, u32[]{:S(2)}) collective-permute-start(bf16[256,256]{1,0:T(8,128)(2,1)S(1)} %copy-done.2), channel_id=1, source_target_pairs={{0,7},{1,0},{2,1},{3,2},{4,3},{5,4},{6,5},{7,6},{8,15},{9,8},{10,9... | collective-permute-start | bytes 393224 | tf_op jit(solution)/shard_map/ppermute | solution.py:60
  98.9 3.6 %copy-start.8 = (f32[2048]{0:T(1024)S(1)}, f32[2048]{0:T(1024)}, u32[]{:S(2)}) copy-start(f32[2048]{0:T(1024)} %param.19) | copy-start | bytes 24580
  98.9 3.6 %copy-start.9 = (f32[2048]{0:T(1024)S(1)}, f32[2048]{0:T(1024)}, u32[]{:S(2)}) copy-start(f32[2048]{0:T(1024)} %param.18) | copy-start | bytes 24580
  101.8 1.6 copy-start.1
  184.0 35.8 %all-to-all-start.2 = ((bf16[256,8,256]{2,0,1:T(8,128)(2,1)}), bf16[256,8,256]{2,0,1:T(8,128)(2,1)S(1)}, u32[]{:S(2)}, u32[]{:S(2)}) async-start(bf16[256,8,256]{2,0,1:T(8,128)(2,1)} %bitcast.89), calls=%async_computation.2 | async-start | bytes 2097152 | tf_op jit(solution)/shard_map/all_to_all | solution.py:222
  220.0 5.9 %copy-start.13 = (f32[3,256]{1,0:T(4,128)S(1)}, f32[3,256]{1,0:T(4,128)}, u32[]{:S(2)}) copy-start(f32[3,256]{1,0:T(4,128)} %param.28) | copy-start | bytes 9220
  220.9 34.3 %copy-start.3 = (bf16[256,256]{1,0:T(8,128)(2,1)}, bf16[256,256]{1,0:T(8,128)(2,1)S(1)}, u32[]{:S(2)}) copy-start(bf16[256,256]{1,0:T(8,128)(2,1)S(1)} %add_convert_fusion) | copy-start | bytes 393220
  222.1 33.5 %copy-start.10 = (f32[2048]{0:T(1024)S(1)}, f32[2048]{0:T(1024)}, u32[]{:S(2)}) copy-start(f32[2048]{0:T(1024)} %param.26) | copy-start | bytes 24580
  222.1 33.5 %copy-start.11 = (f32[2048]{0:T(1024)S(1)}, f32[2048]{0:T(1024)}, u32[]{:S(2)}) copy-start(f32[2048]{0:T(1024)} %param.25) | copy-start | bytes 24580
  222.1 32.9 %all-to-all-start.3 = ((bf16[8,256,256]{1,2,0:T(8,128)(2,1)}), bf16[8,256,256]{1,2,0:T(8,128)(2,1)S(1)}, u32[]{:S(2)}, u32[]{:S(2)}) async-start(bf16[8,256,256]{1,2,0:T(8,128)(2,1)} %broadcast_in_dim.44), calls=%async_computation.3 | async-start | bytes 2097152 | tf_op jit(solution)/shard_map/all_to_all | solution.py:53
  (1 other events, 0.7 us)
Sparse Core Ops, SparseCore 0:
  11.9 128.5 all-gather.1

commit v5 on v4

--- a/solution.py
+++ b/solution.py
@@ -162,7 +162,7 @@
     normed = layer_norm(full_rows, norm_gain, norm_bias).astype(jnp.bfloat16)
     empty_sum = jnp.zeros((tok_count, 3 * col_width), jnp.float32)
     w_rows = w_qkv.shape[0]
-    dense_shard = w_dense.T
+    dense_shard = mp_permute_gather(w_dense.T, mp_count)
     joined = jnp.concatenate(
         [w_qkv.reshape(w_rows, -1), w_next.reshape(w_rows, -1), dense_shard], axis=1
     )
@@ -214,22 +214,17 @@
         local_req.reshape(1, tok_count),
         local_req.reshape(tok_count, 1),
     )
-    partial_out = lax.dot_general(
-        attended, w_dense_t, (((1,), (1,)), ((), ())), preferred_element_type=jnp.float32
-    )
     mp_index = lax.axis_index("mp")
-    pieces = partial_out.astype(jnp.bfloat16).reshape(tok_count, mp_count, col_width)
-    arrived_sums = lax.all_to_all(pieces, "mp", split_axis=1, concat_axis=1, tiled=True)
-    dense_total = jnp.sum(arrived_sums.astype(jnp.float32), axis=1)
-    own_cols = lambda vec: lax.dynamic_slice_in_dim(vec, mp_index * col_width, col_width, 0)
-    own_mlp = lax.dynamic_slice_in_dim(mlp_branch, mp_index * col_width, col_width, 1)
-    hidden_out = (
-        residual_in.astype(jnp.float32)
-        + dense_total
-        + own_cols(dense_bias)
-        + own_mlp.astype(jnp.float32)
+    whole_dense = lax.dot_general(
+        mp_gather(attended, mp_count),
+        w_dense_t,
+        (((1,), (1,)), ((), ())),
+        preferred_element_type=jnp.float32,
+    )
+    whole_hidden = (
+        full_rows.astype(jnp.float32) + whole_dense + dense_bias + mlp_branch.astype(jnp.float32)
     ).astype(jnp.bfloat16)
-    whole_hidden = mp_gather(hidden_out, mp_count)
+    hidden_out = lax.dynamic_slice_in_dim(whole_hidden, mp_index * col_width, col_width, 1)
     normed_next = layer_norm(whole_hidden, next_gain, next_bias).astype(jnp.bfloat16)
     next_raw = row_folder(
         normed_next, empty_sum, w_next_full

time: 268 us -> 293 us (1.093)
  starting transfers between devices: 44.7 us -> 62.9 us
  matrix products: 7.57 us -> 14 us
  other arithmetic: 15.6 us -> 10.2 us
  waiting for transfers between devices: 119 us -> 123 us
    all_gather x1, waiting for transfers between devices: 36.2 us -> 85.8 us  [local(): gathered = lax.all_gather(joined, 'pool', axis=0, tiled=True)]
    all_to_all x1 -> x0, waiting for transfers between devices: 28.5 us -> none  [local(): lax.all_to_all(pieces, 'mp', split_axis=1, concat_axis=1, tiled=True)]
    ppermute x7 -> x14, starting transfers between devices: 28.6 us -> 53.1 us  [mp_permute_gather(): lax.ppermute(block, 'mp', [(src, (src + shift) % mp_count) for src in ran...]
    all_to_all x1, waiting for transfers between devices: 21 us -> 0.01 us  [local(): lax.all_to_all(packed, 'pool', split_axis=0, concat_axis=0, tiled=True)]
    all_to_all x1 -> x0, starting transfers between devices: 6.58 us -> none  [local(): lax.all_to_all(pieces, 'mp', split_axis=1, concat_axis=1, tiled=True)]
    dot_general x1, matrix products: 1.77 us -> 7.38 us  [local(): lax.dot_general(mp_gather(attended, mp_count), w_dense_t, (((1,), (1,)),...]
    ppermute x7 -> x14, waiting for transfers between devices: 3.73 us -> 8.31 us  [mp_permute_gather(): lax.ppermute(block, 'mp', [(src, (src + shift) % mp_count) for src in ran...]
    convert_element_type x4 -> x0, other arithmetic: 4.04 us -> none  [the longest x1 1.5 us: layer_norm(): values = row_data.astype(jnp.float32)]
  transfers between devices with their start and end apart: 11 -> 17, of which waited for: 6 -> 5; matrix products, arithmetic and copies ran while one was open for 14% -> 12% of each run, Pallas kernels for 0% -> 0%
where the time goes in v5:
time: 293 us; the launch traced here: 292 us
  waiting for transfers between devices  123 us (42%)
  starting transfers between devices  62.9 us (21%)
  local copies, waits for them, and re-layouts  27.5 us (9%)
  blocking collectives  25.8 us (9%)
  between operations  14.6 us (5%)
  matrix products  14 us (5%)
  Pallas kernels  13.7 us (5%)
  other arithmetic  10.2 us (3%)
    all_gather x1, waiting for transfers between devices, local(): gathered = lax.all_gather(joined, 'pool', axis=0, tiled=True)  85.8 us
    ppermute x14, starting transfers between devices, mp_permute_gather(): lax.ppermute(block, 'mp', [(src, (src + shift) % mp_count) for src in ran...  53.1 us
    all_to_all x1, waiting for transfers between devices, mp_gather(): lax.all_to_all(spread, 'mp', split_axis=0, concat_axis=2, tiled=True)  29.2 us
    all_to_all x1, blocking collectives, local(): lax.all_to_all(slot_ids, 'pool', split_axis=0, concat_axis=0, tiled=True)  25.8 us
    pallas_call x1, Pallas kernels, attention_call(): pl.pallas_call(attention_body, grid=grid, in_specs=[pl.BlockSpec((Q_CHUNK...  13.7 us
    ppermute x14, waiting for transfers between devices, mp_permute_gather(): lax.ppermute(block, 'mp', [(src, (src + shift) % mp_count) for src in ran...  8.31 us
    unnamed x42, local copies, waits for them, and re-layouts  8.13 us
    dot_general x1, matrix products, local(): lax.dot_general(mp_gather(attended, mp_count), w_dense_t, (((1,), (1,)),...  7.38 us
  transfers between devices with their start and end apart: 17, of which 5 were waited for; matrix products, arithmetic and copies ran while one was open for 12% of the time, Pallas kernels for 0%

profile of v5, /device:TPU:1, one launch (start us, length us, event | category | flops | bytes accessed | tf_op | source)
XLA Modules:
  0.0 292.1 jit_solution(829357130223925539)
XLA Ops:
  7.2 4.2 %collective-permute-start.7 = (bf16[32,256]{1,0:T(8,128)(2,1)}, bf16[32,256]{1,0:T(8,128)(2,1)S(1)}, u32[]{:S(2)}, u32[]{:S(2)}) collective-permute-start(bf16[32,256]{1,0:T(8,128)(2,1)} %bitcast.103), channel_id=1, source_target_pairs={{0,1},{1,2},{2,3},{3,4},{4,5},{5,6},{6,7},{7,0},{8,9},{9,10},{10,1... | collective-permute-start | bytes 49160 | tf_op jit(solution)/shard_map/ppermute | solution.py:60
  11.4 4.2 %collective-permute-start.8 = (bf16[32,256]{1,0:T(8,128)(2,1)}, bf16[32,256]{1,0:T(8,128)(2,1)S(1)}, u32[]{:S(2)}, u32[]{:S(2)}) collective-permute-start(bf16[32,256]{1,0:T(8,128)(2,1)} %bitcast.104), channel_id=1, source_target_pairs={{0,2},{1,3},{2,4},{3,5},{4,6},{5,7},{6,0},{7,1},{8,10},{9,11},{10,... | collective-permute-start | bytes 49160 | tf_op jit(solution)/shard_map/ppermute | solution.py:60
  15.6 4.6 %collective-permute-start.9 = (bf16[32,256]{1,0:T(8,128)(2,1)}, bf16[32,256]{1,0:T(8,128)(2,1)S(1)}, u32[]{:S(2)}, u32[]{:S(2)}) collective-permute-start(bf16[32,256]{1,0:T(8,128)(2,1)} %bitcast.105), channel_id=1, source_target_pairs={{0,3},{1,4},{2,5},{3,6},{4,7},{5,0},{6,1},{7,2},{8,11},{9,12},{10,... | collective-permute-start | bytes 49160 | tf_op jit(solution)/shard_map/ppermute | solution.py:60
  20.3 3.5 %collective-permute-start.10 = (bf16[32,256]{1,0:T(8,128)(2,1)}, bf16[32,256]{1,0:T(8,128)(2,1)S(1)}, u32[]{:S(2)}, u32[]{:S(2)}) collective-permute-start(bf16[32,256]{1,0:T(8,128)(2,1)} %bitcast.106), channel_id=1, source_target_pairs={{0,4},{1,5},{2,6},{3,7},{4,0},{5,1},{6,2},{7,3},{8,12},{9,13},{10,... | collective-permute-start | bytes 49160 | tf_op jit(solution)/shard_map/ppermute | solution.py:60
  23.8 4.9 %collective-permute-start.11 = (bf16[32,256]{1,0:T(8,128)(2,1)}, bf16[32,256]{1,0:T(8,128)(2,1)S(1)}, u32[]{:S(2)}, u32[]{:S(2)}) collective-permute-start(bf16[32,256]{1,0:T(8,128)(2,1)} %bitcast.107), channel_id=1, source_target_pairs={{0,5},{1,6},{2,7},{3,0},{4,1},{5,2},{6,3},{7,4},{8,13},{9,14},{10,... | collective-permute-start | bytes 49160 | tf_op jit(solution)/shard_map/ppermute | solution.py:60
  31.1 5.0 %collective-permute-start.12 = (bf16[32,256]{1,0:T(8,128)(2,1)}, bf16[32,256]{1,0:T(8,128)(2,1)S(1)}, u32[]{:S(2)}, u32[]{:S(2)}) collective-permute-start(bf16[32,256]{1,0:T(8,128)(2,1)} %bitcast.108), channel_id=1, source_target_pairs={{0,6},{1,7},{2,0},{3,1},{4,2},{5,3},{6,4},{7,5},{8,14},{9,15},{10,... | collective-permute-start | bytes 49160 | tf_op jit(solution)/shard_map/ppermute | solution.py:60
  36.1 3.0 %collective-permute-start.13 = (bf16[32,256]{1,0:T(8,128)(2,1)}, bf16[32,256]{1,0:T(8,128)(2,1)S(1)}, u32[]{:S(2)}, u32[]{:S(2)}) collective-permute-start(bf16[32,256]{1,0:T(8,128)(2,1)} %bitcast.109), channel_id=1, source_target_pairs={{0,7},{1,0},{2,1},{3,2},{4,3},{5,4},{6,5},{7,6},{8,15},{9,8},{10,9... | collective-permute-start | bytes 49160 | tf_op jit(solution)/shard_map/ppermute | solution.py:60
  44.0 2.5 sort.17
  48.0 2.6 fusion.47
  52.0 25.8 %all_to_all.29 = s32[64,1,2]{2,1,0:T(1,128)S(1)} all-to-all(s32[64,1,2]{2,1,0:T(1,128)S(1)} %bitcast.98), channel_id=1, replica_groups=mesh['pool'=64,'mp'=8] {'pool'}, dimensions={0} | all-to-all | bytes 1024 | tf_op jit(solution)/shard_map/all_to_all | solution.py:196
  79.2 2.9 gather_fusion.3
  82.1 5.8 %all-to-all-start.1 = ((bf16[64,2,2,32,256]{4,3,2,1,0:T(8,128)(2,1)}), bf16[64,2,2,32,256]{4,3,2,1,0:T(8,128)(2,1)}, u32[]{:S(2)}, u32[]{:S(2)}) async-start(bf16[64,2,2,32,256]{4,3,2,1,0:T(8,128)(2,1)} %bitcast.80), calls=%async_computation.1 | async-start | bytes 8388608 | tf_op jit(solution)/shard_map/all_to_all | solution.py:198
  91.9 4.5 %collective-permute-start.2 = (bf16[256,256]{1,0:T(8,128)(2,1)S(1)}, bf16[256,256]{1,0:T(8,128)(2,1)S(1)}, u32[]{:S(2)}, u32[]{:S(2)}) collective-permute-start(bf16[256,256]{1,0:T(8,128)(2,1)S(1)} %copy-done.2), channel_id=1, source_target_pairs={{0,3},{1,4},{2,5},{3,6},{4,7},{5,0},{6,1},{7,2},{8,11},{9,12},{10,... | collective-permute-start | bytes 393224 | tf_op jit(solution)/shard_map/ppermute | solution.py:60
  96.4 4.8 %collective-permute-start.3 = (bf16[256,256]{1,0:T(8,128)(2,1)S(1)}, bf16[256,256]{1,0:T(8,128)(2,1)S(1)}, u32[]{:S(2)}, u32[]{:S(2)}) collective-permute-start(bf16[256,256]{1,0:T(8,128)(2,1)S(1)} %copy-done.2), channel_id=1, source_target_pairs={{0,4},{1,5},{2,6},{3,7},{4,0},{5,1},{6,2},{7,3},{8,12},{9,13},{10,... | collective-permute-start | bytes 393224 | tf_op jit(solution)/shard_map/ppermute | solution.py:60
  101.2 6.2 %collective-permute-start.4 = (bf16[256,256]{1,0:T(8,128)(2,1)S(1)}, bf16[256,256]{1,0:T(8,128)(2,1)S(1)}, u32[]{:S(2)}, u32[]{:S(2)}) collective-permute-start(bf16[256,256]{1,0:T(8,128)(2,1)S(1)} %copy-done.2), channel_id=1, source_target_pairs={{0,5},{1,6},{2,7},{3,0},{4,1},{5,2},{6,3},{7,4},{8,13},{9,14},{10,... | collective-permute-start | bytes 393224 | tf_op jit(solution)/shard_map/ppermute | solution.py:60
  113.3 2.4 collective-permute-start.6
  118.4 6.0 %collective-permute-done.5 = bf16[256,256]{1,0:T(8,128)(2,1)S(1)} collective-permute-done((bf16[256,256]{1,0:T(8,128)(2,1)S(1)}, bf16[256,256]{1,0:T(8,128)(2,1)S(1)}, u32[]{:S(2)}, u32[]{:S(2)}) %collective-permute-start.5) | collective-permute-done | bytes 131104 | tf_op jit(solution)/shard_map/ppermute | solution.py:60
  130.4 85.8 %all-gather.2.cloned.1.call-done = bf16[2048,3584]{1,0:T(8,128)(2,1)} async-done(((bf16[32,3584]{1,0:T(8,128)(2,1)}), bf16[2048,3584]{1,0:T(8,128)(2,1)}) %all-gather.2.cloned.1.call-update) | async-done | bytes 14680080 | tf_op jit(solution)/shard_map/all_gather | solution.py:169
  216.2 3.6 %fusion.26 = f32[256,768]{1,0:T(8,128)S(1)} fusion(bf16[2048,3584]{1,0:T(8,128)(2,1)} %all-gather.2.cloned.1.call-done, f32[256,2048]{1,0:T(8,128)} %bitcast.83, f32[2048]{0:T(1024)S(1)} %copy-done.8, f32[2048]{0:T(1024)S(1)} %copy-done.9, f32[256]{0:T(256)S(1)} %add_rsqrt_fusion.1, f32[256]{0:T(256)S(1)} %broadcast_multiply_fusion.1, f32[768]{0:T(1024)S(1)} %add.149), kind=kOutput, calls=%fused_computation.28 | convolution fusion | flops 808124416 | bytes 6050816 | tf_op jit(solution)/shard_map/dot_general | solution.py:46
  222.6 13.7 %shard_map.167 = bf16[256,256]{1,0:T(8,128)(2,1)} custom-call(bf16[256,256]{1,0:T(8,128)(2,1)} %copy.52.q_ref, bf16[64,2,2,32,256]{4,3,2,1,0:T(8,128)(2,1)} %all-to-all-done.1.kc_ref.vc_ref, bf16[64,2,2,32,256]{4,3,2,1,0:T(8,128)(2,1)} %all-to-all-done.1.kc_ref.vc_ref, bf16[256,256]{1,0:T(8,128)(2,1)} %copy.53.kn_ref, bf16[256,256]{1,0:T(8,128)(2,1)} %bitcast.91, ...), custom_call_target="tpu_custom_call" | custom-call | tf_op jit(solution)/shard_map/pallas_call | solution.py:121
  238.4 3.9 %all-to-all-start.2 = ((bf16[8,256,256]{1,2,0:T(8,128)(2,1)}), bf16[8,256,256]{1,2,0:T(8,128)(2,1)S(1)}, u32[]{:S(2)}, u32[]{:S(2)}) async-start(bf16[8,256,256]{1,2,0:T(8,128)(2,1)} %broadcast_in_dim.44), calls=%async_computation.2 | async-start | bytes 2097152 | tf_op jit(solution)/shard_map/all_to_all | solution.py:53
  242.4 29.2 %all-to-all-done.2 = bf16[8,256,256]{1,2,0:T(8,128)(2,1)S(1)} async-done(((bf16[8,256,256]{1,2,0:T(8,128)(2,1)}), bf16[8,256,256]{1,2,0:T(8,128)(2,1)S(1)}, u32[]{:S(2)}, u32[]{:S(2)}) %all-to-all-start.2) | async-done | bytes 1048608 | tf_op jit(solution)/shard_map/all_to_all | solution.py:53
  272.6 7.4 %convert_reduce_fusion.1 = (f32[256]{0:T(256)S(1)}, bf16[256,2048]{1,0:T(8,128)(2,1)S(1)}) fusion(bf16[256,2048]{1,0:T(8,128)(2,1)} %param.17, f32[2048]{0:T(1024)S(1)} %copy-done.10, f32[256,2048]{1,0:T(8,128)} %bitcast.84, bf16[256,2048]{0,1:T(8,128)(2,1)} %bitcast.86, bf16[2048,3584]{1,0:T(8,128)(2,1)} %all-gather.2.cloned.1.call-done), kind=kOutput, calls=%fused_computation.15 | convolution fusion | flops 2151153408 | bytes 13640704 | tf_op jit(solution)/shard_map/dot_general | solution.py:218
  280.4 3.0 %fusion.32 = bf16[256,768]{1,0:T(8,128)(2,1)S(1)} fusion(bf16[2048,3584]{1,0:T(8,128)(2,1)} %all-gather.2.cloned.1.call-done, bf16[256,2048]{1,0:T(8,128)(2,1)S(1)} %get-tuple-element.34, f32[2048]{0:T(1024)S(1)} %copy-done.11, f32[2048]{0:T(1024)S(1)} %copy-done.12, f32[256]{0:T(256)S(1)} %add_rsqrt_fusion, f32[256]{0:T(256)S(1)} %broadcast_multiply_fusion, ...), kind=kOutput, calls=%fused_computation.30 | convolution fusion | flops 808845312 | bytes 4609024 | tf_op jit(solution)/shard_map/dot_general | solution.py:46
  (125 shorter events, 37.9 us)
Async XLA Ops:
  7.2 72.1 %copy-start = (bf16[48,2,32,256]{3,2,1,0:T(8,128)(2,1)S(1)}, bf16[48,2,32,256]{3,2,1,0:T(8,128)(2,1)}, u32[]{:S(2)}) copy-start(bf16[48,2,32,256]{3,2,1,0:T(8,128)(2,1)} %param.22) | copy-start | bytes 4718596
  7.2 209.1 %all-gather.2.cloned.1.call-start = ((), (), s32[]{:S(2)}) async-start(), calls=%async_computation.3 | async-start | bytes 14909440 | tf_op jit(solution)/shard_map/all_gather | solution.py:169
  7.2 23.8 %collective-permute-start.7 = (bf16[32,256]{1,0:T(8,128)(2,1)}, bf16[32,256]{1,0:T(8,128)(2,1)S(1)}, u32[]{:S(2)}, u32[]{:S(2)}) collective-permute-start(bf16[32,256]{1,0:T(8,128)(2,1)} %bitcast.103), channel_id=1, source_target_pairs={{0,1},{1,2},{2,3},{3,4},{4,5},{5,6},{6,7},{7,0},{8,9},{9,10},{10,1... | collective-permute-start | bytes 49160 | tf_op jit(solution)/shard_map/ppermute | solution.py:60
  11.4 24.7 %collective-permute-start.8 = (bf16[32,256]{1,0:T(8,128)(2,1)}, bf16[32,256]{1,0:T(8,128)(2,1)S(1)}, u32[]{:S(2)}, u32[]{:S(2)}) collective-permute-start(bf16[32,256]{1,0:T(8,128)(2,1)} %bitcast.104), channel_id=1, source_target_pairs={{0,2},{1,3},{2,4},{3,5},{4,6},{5,7},{6,0},{7,1},{8,10},{9,11},{10,... | collective-permute-start | bytes 49160 | tf_op jit(solution)/shard_map/ppermute | solution.py:60
  15.6 23.4 %collective-permute-start.9 = (bf16[32,256]{1,0:T(8,128)(2,1)}, bf16[32,256]{1,0:T(8,128)(2,1)S(1)}, u32[]{:S(2)}, u32[]{:S(2)}) collective-permute-start(bf16[32,256]{1,0:T(8,128)(2,1)} %bitcast.105), channel_id=1, source_target_pairs={{0,3},{1,4},{2,5},{3,6},{4,7},{5,0},{6,1},{7,2},{8,11},{9,12},{10,... | collective-permute-start | bytes 49160 | tf_op jit(solution)/shard_map/ppermute | solution.py:60
  20.3 18.8 %collective-permute-start.10 = (bf16[32,256]{1,0:T(8,128)(2,1)}, bf16[32,256]{1,0:T(8,128)(2,1)S(1)}, u32[]{:S(2)}, u32[]{:S(2)}) collective-permute-start(bf16[32,256]{1,0:T(8,128)(2,1)} %bitcast.106), channel_id=1, source_target_pairs={{0,4},{1,5},{2,6},{3,7},{4,0},{5,1},{6,2},{7,3},{8,12},{9,13},{10,... | collective-permute-start | bytes 49160 | tf_op jit(solution)/shard_map/ppermute | solution.py:60
  23.8 15.3 %collective-permute-start.11 = (bf16[32,256]{1,0:T(8,128)(2,1)}, bf16[32,256]{1,0:T(8,128)(2,1)S(1)}, u32[]{:S(2)}, u32[]{:S(2)}) collective-permute-start(bf16[32,256]{1,0:T(8,128)(2,1)} %bitcast.107), channel_id=1, source_target_pairs={{0,5},{1,6},{2,7},{3,0},{4,1},{5,2},{6,3},{7,4},{8,13},{9,14},{10,... | collective-permute-start | bytes 49160 | tf_op jit(solution)/shard_map/ppermute | solution.py:60
  31.1 8.1 %collective-permute-start.12 = (bf16[32,256]{1,0:T(8,128)(2,1)}, bf16[32,256]{1,0:T(8,128)(2,1)S(1)}, u32[]{:S(2)}, u32[]{:S(2)}) collective-permute-start(bf16[32,256]{1,0:T(8,128)(2,1)} %bitcast.108), channel_id=1, source_target_pairs={{0,6},{1,7},{2,0},{3,1},{4,2},{5,3},{6,4},{7,5},{8,14},{9,15},{10,... | collective-permute-start | bytes 49160 | tf_op jit(solution)/shard_map/ppermute | solution.py:60
  36.1 5.0 %collective-permute-start.13 = (bf16[32,256]{1,0:T(8,128)(2,1)}, bf16[32,256]{1,0:T(8,128)(2,1)S(1)}, u32[]{:S(2)}, u32[]{:S(2)}) collective-permute-start(bf16[32,256]{1,0:T(8,128)(2,1)} %bitcast.109), channel_id=1, source_target_pairs={{0,7},{1,0},{2,1},{3,2},{4,3},{5,4},{6,5},{7,6},{8,15},{9,8},{10,9... | collective-permute-start | bytes 49160 | tf_op jit(solution)/shard_map/ppermute | solution.py:60
  82.1 25.3 %copy-start.6 = (f32[3,256]{1,0:T(4,128)S(1)}, f32[3,256]{1,0:T(4,128)}, u32[]{:S(2)}) copy-start(f32[3,256]{1,0:T(4,128)} %param.21) | copy-start | bytes 9220
  82.1 25.3 %copy-start.5 = (s32[256]{0:T(256)S(1)}, s32[256]{0:T(256)}, u32[]{:S(2)}) copy-start(s32[256]{0:T(256)} %param.29) | copy-start | bytes 3076
  82.1 27.7 %copy-start.4 = (s32[4]{0:T(128)S(1)}, s32[4]{0:T(128)}, u32[]{:S(2)}) copy-start(s32[4]{0:T(128)} %param.30) | copy-start | bytes 52
  82.1 140.5 %all-to-all-start.1 = ((bf16[64,2,2,32,256]{4,3,2,1,0:T(8,128)(2,1)}), bf16[64,2,2,32,256]{4,3,2,1,0:T(8,128)(2,1)}, u32[]{:S(2)}, u32[]{:S(2)}) async-start(bf16[64,2,2,32,256]{4,3,2,1,0:T(8,128)(2,1)} %bitcast.80), calls=%async_computation.1 | async-start | bytes 8388608 | tf_op jit(solution)/shard_map/all_to_all | solution.py:198
  87.9 22.9 %collective-permute-start = (bf16[256,256]{1,0:T(8,128)(2,1)S(1)}, bf16[256,256]{1,0:T(8,128)(2,1)S(1)}, u32[]{:S(2)}, u32[]{:S(2)}) collective-permute-start(bf16[256,256]{1,0:T(8,128)(2,1)S(1)} %copy-done.2), channel_id=1, source_target_pairs={{0,1},{1,2},{2,3},{3,4},{4,5},{5,6},{6,7},{7,0},{8,9},{9,10},{10,1... | collective-permute-start | bytes 393224 | tf_op jit(solution)/shard_map/ppermute | solution.py:60
  89.8 23.5 %collective-permute-start.1 = (bf16[256,256]{1,0:T(8,128)(2,1)S(1)}, bf16[256,256]{1,0:T(8,128)(2,1)S(1)}, u32[]{:S(2)}, u32[]{:S(2)}) collective-permute-start(bf16[256,256]{1,0:T(8,128)(2,1)S(1)} %copy-done.2), channel_id=1, source_target_pairs={{0,2},{1,3},{2,4},{3,5},{4,6},{5,7},{6,0},{7,1},{8,10},{9,11},{10,... | collective-permute-start | bytes 393224 | tf_op jit(solution)/shard_map/ppermute | solution.py:60
  91.9 24.5 %collective-permute-start.2 = (bf16[256,256]{1,0:T(8,128)(2,1)S(1)}, bf16[256,256]{1,0:T(8,128)(2,1)S(1)}, u32[]{:S(2)}, u32[]{:S(2)}) collective-permute-start(bf16[256,256]{1,0:T(8,128)(2,1)S(1)} %copy-done.2), channel_id=1, source_target_pairs={{0,3},{1,4},{2,5},{3,6},{4,7},{5,0},{6,1},{7,2},{8,11},{9,12},{10,... | collective-permute-start | bytes 393224 | tf_op jit(solution)/shard_map/ppermute | solution.py:60
  96.4 20.7 %collective-permute-start.3 = (bf16[256,256]{1,0:T(8,128)(2,1)S(1)}, bf16[256,256]{1,0:T(8,128)(2,1)S(1)}, u32[]{:S(2)}, u32[]{:S(2)}) collective-permute-start(bf16[256,256]{1,0:T(8,128)(2,1)S(1)} %copy-done.2), channel_id=1, source_target_pairs={{0,4},{1,5},{2,6},{3,7},{4,0},{5,1},{6,2},{7,3},{8,12},{9,13},{10,... | collective-permute-start | bytes 393224 | tf_op jit(solution)/shard_map/ppermute | solution.py:60
  101.2 16.5 %collective-permute-start.4 = (bf16[256,256]{1,0:T(8,128)(2,1)S(1)}, bf16[256,256]{1,0:T(8,128)(2,1)S(1)}, u32[]{:S(2)}, u32[]{:S(2)}) collective-permute-start(bf16[256,256]{1,0:T(8,128)(2,1)S(1)} %copy-done.2), channel_id=1, source_target_pairs={{0,5},{1,6},{2,7},{3,0},{4,1},{5,2},{6,3},{7,4},{8,13},{9,14},{10,... | collective-permute-start | bytes 393224 | tf_op jit(solution)/shard_map/ppermute | solution.py:60
  110.8 13.7 %collective-permute-start.5 = (bf16[256,256]{1,0:T(8,128)(2,1)S(1)}, bf16[256,256]{1,0:T(8,128)(2,1)S(1)}, u32[]{:S(2)}, u32[]{:S(2)}) collective-permute-start(bf16[256,256]{1,0:T(8,128)(2,1)S(1)} %copy-done.2), channel_id=1, source_target_pairs={{0,6},{1,7},{2,0},{3,1},{4,2},{5,3},{6,4},{7,5},{8,14},{9,15},{10,... | collective-permute-start | bytes 393224 | tf_op jit(solution)/shard_map/ppermute | solution.py:60
  113.3 12.1 %collective-permute-start.6 = (bf16[256,256]{1,0:T(8,128)(2,1)S(1)}, bf16[256,256]{1,0:T(8,128)(2,1)S(1)}, u32[]{:S(2)}, u32[]{:S(2)}) collective-permute-start(bf16[256,256]{1,0:T(8,128)(2,1)S(1)} %copy-done.2), channel_id=1, source_target_pairs={{0,7},{1,0},{2,1},{3,2},{4,3},{5,4},{6,5},{7,6},{8,15},{9,8},{10,9... | collective-permute-start | bytes 393224 | tf_op jit(solution)/shard_map/ppermute | solution.py:60
  129.7 86.5 %copy-start.8 = (f32[2048]{0:T(1024)S(1)}, f32[2048]{0:T(1024)}, u32[]{:S(2)}) copy-start(f32[2048]{0:T(1024)} %param.19) | copy-start | bytes 24580
  129.7 86.5 %copy-start.9 = (f32[2048]{0:T(1024)S(1)}, f32[2048]{0:T(1024)}, u32[]{:S(2)}) copy-start(f32[2048]{0:T(1024)} %param.18) | copy-start | bytes 24580
  236.3 36.3 %copy-start.10 = (f32[2048]{0:T(1024)S(1)}, f32[2048]{0:T(1024)}, u32[]{:S(2)}) copy-start(f32[2048]{0:T(1024)} %param.24) | copy-start | bytes 24580
  238.4 33.2 %all-to-all-start.2 = ((bf16[8,256,256]{1,2,0:T(8,128)(2,1)}), bf16[8,256,256]{1,2,0:T(8,128)(2,1)S(1)}, u32[]{:S(2)}, u32[]{:S(2)}) async-start(bf16[8,256,256]{1,2,0:T(8,128)(2,1)} %broadcast_in_dim.44), calls=%async_computation.2 | async-start | bytes 2097152 | tf_op jit(solution)/shard_map/all_to_all | solution.py:53
  (6 other events, 47.6 us)
Sparse Core Ops, SparseCore 0:
  42.5 173.6 all-gather.1

commit v6 on v5

--- a/solution.py
+++ b/solution.py
@@ -1,3 +1,5 @@
+import functools
+
 import jax
 import jax.numpy as jnp
 from jax import lax
@@ -69,8 +71,7 @@
 PAIR = 128
 
 
-def attention_body(q_ref, kc_ref, vc_ref, kn_ref, vn_ref, keyc_ref, keyn_ref, qreq_ref, out_ref):
-    chunk = pl.program_id(0)
+def attention_body(chunk, q_ref, kc_ref, vc_ref, kn_ref, vn_ref, keyc_ref, keyn_ref, qreq_ref, out_ref):
     n_slots = kc_ref.shape[0] * kc_ref.shape[1] * kc_ref.shape[2]
     n_new = kn_ref.shape[0]
     score_scale = HEAD_DIM ** (-0.5)
@@ -112,27 +113,27 @@
         out_ref[:, cols] = merged.astype(out_ref.dtype)
 
 
-def attention_call(query, arrived, key_new, value_new, key_req_c, key_req_n, q_req):
+def attention_call(chunk, query, arrived, key_new, value_new, key_req_c, key_req_n, q_req):
     tok, width = query.shape
     holders, per, _, blk, _ = arrived.shape
     n_slots = holders * per * blk
-    grid = (tok // Q_CHUNK,)
+    grid = (1,)
     full = lambda c: (0, 0)
     return pl.pallas_call(
-        attention_body,
+        functools.partial(attention_body, chunk),
         grid=grid,
         in_specs=[
-            pl.BlockSpec((Q_CHUNK, width), lambda c: (c, 0)),
+            pl.BlockSpec((Q_CHUNK, width), lambda c: (chunk, 0)),
             pl.BlockSpec((holders, per, None, blk, width), lambda c: (0, 0, 0, 0, 0)),
             pl.BlockSpec((holders, per, None, blk, width), lambda c: (0, 0, 1, 0, 0)),
             pl.BlockSpec((tok, width), full),
             pl.BlockSpec((tok, width), full),
             pl.BlockSpec((1, n_slots), full),
             pl.BlockSpec((1, tok), full),
-            pl.BlockSpec((Q_CHUNK, 1), lambda c: (c, 0)),
+            pl.BlockSpec((Q_CHUNK, 1), lambda c: (chunk, 0)),
         ],
-        out_specs=pl.BlockSpec((Q_CHUNK, width), lambda c: (c, 0)),
-        out_shape=jax.ShapeDtypeStruct((tok, width), jnp.bfloat16),
+        out_specs=pl.BlockSpec((Q_CHUNK, width), lambda c: (0, 0)),
+        out_shape=jax.ShapeDtypeStruct((Q_CHUNK, width), jnp.bfloat16),
     )(query, arrived, arrived, key_new, value_new, key_req_c, key_req_n, q_req)
 
 
@@ -162,7 +163,7 @@
     normed = layer_norm(full_rows, norm_gain, norm_bias).astype(jnp.bfloat16)
     empty_sum = jnp.zeros((tok_count, 3 * col_width), jnp.float32)
     w_rows = w_qkv.shape[0]
-    dense_shard = mp_permute_gather(w_dense.T, mp_count)
+    dense_shard = w_dense.T
     joined = jnp.concatenate(
         [w_qkv.reshape(w_rows, -1), w_next.reshape(w_rows, -1), dense_shard], axis=1
     )
@@ -191,8 +192,16 @@
     pool_count = lax.axis_size("pool")
     blocks_here = cache_pool.shape[0]
     entries = block_table.reshape(-1)
-    holder_order = jnp.argsort(entries // blocks_here, stable=True)
-    slot_ids = (entries % blocks_here)[holder_order].reshape(pool_count, -1)
+    holder = entries // blocks_here
+    entry_ids = jnp.arange(entries.shape[0], dtype=jnp.int32)
+    earlier_same = (holder[:, None] == holder[None, :]) & (entry_ids[None, :] < entry_ids[:, None])
+    per_holder = entries.shape[0] // pool_count
+    slot_of = holder * per_holder + jnp.sum(earlier_same.astype(jnp.int32), axis=1)
+    placed = slot_of[:, None] == entry_ids[None, :]
+    holder_order = jnp.sum(jnp.where(placed, entry_ids[:, None], 0), axis=0)
+    slot_ids = jnp.sum(jnp.where(placed, (entries % blocks_here)[:, None], 0), axis=0).reshape(
+        pool_count, -1
+    )
     wanted = lax.all_to_all(slot_ids, "pool", split_axis=0, concat_axis=0, tiled=True)
     packed = cache_pool[wanted.reshape(-1)].reshape((pool_count, -1) + cache_pool.shape[1:])
     arrived = lax.all_to_all(packed, "pool", split_axis=0, concat_axis=0, tiled=True)
@@ -205,35 +214,46 @@
     key_req_c = jnp.where(
         pos_in_blk[None, :] < entry_lim[:, None], entry_req[:, None], -1
     ).reshape(1, -1)
-    attended = attention_call(
-        query.reshape(tok_count, col_width),
-        arrived,
-        key_new.reshape(tok_count, col_width),
-        value_new.reshape(tok_count, col_width),
-        key_req_c,
-        local_req.reshape(1, tok_count),
-        local_req.reshape(tok_count, 1),
-    )
     mp_index = lax.axis_index("mp")
-    whole_dense = lax.dot_general(
-        mp_gather(attended, mp_count),
-        w_dense_t,
-        (((1,), (1,)), ((), ())),
-        preferred_element_type=jnp.float32,
-    )
-    whole_hidden = (
-        full_rows.astype(jnp.float32) + whole_dense + dense_bias + mlp_branch.astype(jnp.float32)
-    ).astype(jnp.bfloat16)
-    hidden_out = lax.dynamic_slice_in_dim(whole_hidden, mp_index * col_width, col_width, 1)
-    normed_next = layer_norm(whole_hidden, next_gain, next_bias).astype(jnp.bfloat16)
-    next_raw = row_folder(
-        normed_next, empty_sum, w_next_full
-    )
-    next_qkv = (
-        (next_raw + next_qkv_bias.reshape(1, 3 * col_width))
-        .astype(jnp.bfloat16)
-        .reshape(tok_count, 3, col_width)
-    )
+    own_bias = lax.dynamic_slice_in_dim(dense_bias, mp_index * col_width, col_width, 0)
+    own_mlp = lax.dynamic_slice_in_dim(mlp_branch, mp_index * col_width, col_width, 1)
+    hidden_parts = []
+    next_parts = []
+    for chunk in range(tok_count // Q_CHUNK):
+        rows = slice(chunk * Q_CHUNK, (chunk + 1) * Q_CHUNK)
+        attended = attention_call(
+            chunk,
+            query.reshape(tok_count, col_width),
+            arrived,
+            key_new.reshape(tok_count, col_width),
+            value_new.reshape(tok_count, col_width),
+            key_req_c,
+            local_req.reshape(1, tok_count),
+            local_req.reshape(tok_count, 1),
+        )
+        partial_out = lax.dot_general(
+            attended, w_dense_t, (((1,), (1,)), ((), ())), preferred_element_type=jnp.float32
+        )
+        pieces = partial_out.astype(jnp.bfloat16).reshape(Q_CHUNK, mp_count, col_width)
+        arrived_sums = lax.all_to_all(pieces, "mp", split_axis=1, concat_axis=1, tiled=True)
+        dense_total = jnp.sum(arrived_sums.astype(jnp.float32), axis=1)
+        hidden_part = (
+            residual_in[rows].astype(jnp.float32)
+            + dense_total
+            + own_bias
+            + own_mlp[rows].astype(jnp.float32)
+        ).astype(jnp.bfloat16)
+        whole_hidden = mp_gather(hidden_part, mp_count)
+        normed_next = layer_norm(whole_hidden, next_gain, next_bias).astype(jnp.bfloat16)
+        next_raw = jnp.dot(normed_next, w_next_full, preferred_element_type=jnp.float32)
+        next_parts.append(
+            (next_raw + next_qkv_bias.reshape(1, 3 * col_width))
+            .astype(jnp.bfloat16)
+            .reshape(Q_CHUNK, 3, col_width)
+        )
+        hidden_parts.append(hidden_part)
+    hidden_out = jnp.concatenate(hidden_parts, axis=0)
+    next_qkv = jnp.concatenate(next_parts, axis=0)
     return (hidden_out, next_qkv)
 
 

time: 293 us -> 280 us (0.956)
  starting transfers between devices: 62.9 us -> 51.9 us
  waiting for transfers between devices: 123 us -> 117 us
  other arithmetic: 10.2 us -> 14.6 us
    all_gather x1, waiting for transfers between devices: 85.8 us -> 45 us  [local(): gathered = lax.all_gather(joined, 'pool', axis=0, tiled=True)]
    ppermute x14 -> x7, starting transfers between devices: 53.1 us -> 28.6 us  [mp_permute_gather(): lax.ppermute(block, 'mp', [(src, (src + shift) % mp_count) for src in ran...]
    all_to_all x0 -> x2, waiting for transfers between devices: none -> 24.1 us  [local(): lax.all_to_all(pieces, 'mp', split_axis=1, concat_axis=1, tiled=True)]
    all_to_all x1, waiting for transfers between devices: 0.01 us -> 12.4 us  [local(): lax.all_to_all(packed, 'pool', split_axis=0, concat_axis=0, tiled=True)]
    all_to_all x0 -> x2, starting transfers between devices: none -> 10.5 us  [local(): lax.all_to_all(pieces, 'mp', split_axis=1, concat_axis=1, tiled=True)]
    ppermute x14 -> x7, waiting for transfers between devices: 8.31 us -> 1.41 us  [mp_permute_gather(): lax.ppermute(block, 'mp', [(src, (src + shift) % mp_count) for src in ran...]
    all_to_all x1 -> x2, waiting for transfers between devices: 29.2 us -> 34.3 us  [mp_gather(): lax.all_to_all(spread, 'mp', split_axis=0, concat_axis=2, tiled=True)]
    convert_element_type x0 -> x4, other arithmetic: none -> 4.02 us  [the longest x1 1.5 us: layer_norm(): values = row_data.astype(jnp.float32)]
  transfers between devices with their start and end apart: 17 -> 13, of which waited for: 5 -> 7; matrix products, arithmetic and copies ran while one was open for 12% -> 13% of each run, Pallas kernels for 0% -> 3%
where the time goes in v6:
time: 280 us; the launch traced here: 278 us
  waiting for transfers between devices  117 us (42%)
  starting transfers between devices  51.9 us (19%)
  local copies, waits for them, and re-layouts  28.1 us (10%)
  blocking collectives  23.9 us (9%)
  Pallas kernels  16.6 us (6%)
  other arithmetic  14.6 us (5%)
  between operations  14.5 us (5%)
  matrix products  11.4 us (4%)
    all_gather x1, waiting for transfers between devices, local(): gathered = lax.all_gather(joined, 'pool', axis=0, tiled=True)  45 us
    all_to_all x2, waiting for transfers between devices, mp_gather(): lax.all_to_all(spread, 'mp', split_axis=0, concat_axis=2, tiled=True)  34.3 us
    ppermute x7, starting transfers between devices, mp_permute_gather(): lax.ppermute(block, 'mp', [(src, (src + shift) % mp_count) for src in ran...  28.6 us
    all_to_all x2, waiting for transfers between devices, local(): lax.all_to_all(pieces, 'mp', split_axis=1, concat_axis=1, tiled=True)  24.1 us
    all_to_all x1, blocking collectives, local(): lax.all_to_all(slot_ids, 'pool', split_axis=0, concat_axis=0, tiled=True)  23.9 us
    pallas_call x2, Pallas kernels, attention_call(): pl.pallas_call(functools.partial(attention_body, chunk), grid=grid, in_sp...  16.6 us
    all_to_all x1, waiting for transfers between devices, local(): lax.all_to_all(packed, 'pool', split_axis=0, concat_axis=0, tiled=True)  12.4 us
    all_to_all x2, starting transfers between devices, local(): lax.all_to_all(pieces, 'mp', split_axis=1, concat_axis=1, tiled=True)  10.5 us
  transfers between devices with their start and end apart: 13, of which 7 were waited for; matrix products, arithmetic and copies ran while one was open for 13% of the time, Pallas kernels for 3%

profile of v6, /device:TPU:1, one launch (start us, length us, event | category | flops | bytes accessed | tf_op | source)
XLA Modules:
  0.0 278.3 jit_solution(1495988934866639815)
XLA Ops:
  12.4 23.9 %all_to_all.42 = s32[64,1,2]{2,1,0:T(1,128)S(1)} all-to-all(s32[64,1,2]{2,1,0:T(1,128)S(1)} %bitcast.145), channel_id=1, replica_groups=mesh['pool'=64,'mp'=8] {'pool'}, dimensions={0} | all-to-all | bytes 1024 | tf_op jit(solution)/shard_map/all_to_all | solution.py:205
  37.8 2.9 %gather_fusion.1 = bf16[128,2,32,256]{3,2,1,0:T(8,128)(2,1)} fusion(bf16[48,2,32,256]{3,2,1,0:T(8,128)(2,1)S(1)} %copy-done, s32[1024]{0:T(1024)S(1)} %pad_clamp_fusion), kind=kCustom, calls=%fused_computation.1 | custom fusion | bytes 8389120 | tf_op jit(solution)/shard_map/gather | solution.py:206
  40.6 5.8 %all-to-all-start.1 = ((bf16[64,2,2,32,256]{4,3,2,1,0:T(8,128)(2,1)}), bf16[64,2,2,32,256]{4,3,2,1,0:T(8,128)(2,1)}, u32[]{:S(2)}, u32[]{:S(2)}) async-start(bf16[64,2,2,32,256]{4,3,2,1,0:T(8,128)(2,1)} %bitcast.128), calls=%async_computation.1 | async-start | bytes 8388608 | tf_op jit(solution)/shard_map/all_to_all | solution.py:207
  46.5 3.2 %collective-permute-start = (bf16[256,256]{1,0:T(8,128)(2,1)S(1)}, bf16[256,256]{1,0:T(8,128)(2,1)S(1)}, u32[]{:S(2)}, u32[]{:S(2)}) collective-permute-start(bf16[256,256]{1,0:T(8,128)(2,1)S(1)} %copy-done.2), channel_id=1, source_target_pairs={{0,1},{1,2},{2,3},{3,4},{4,5},{5,6},{6,7},{7,0},{8,9},{9,10},{10,1... | collective-permute-start | bytes 393224 | tf_op jit(solution)/shard_map/ppermute | solution.py:62
  49.7 4.2 %collective-permute-start.1 = (bf16[256,256]{1,0:T(8,128)(2,1)S(1)}, bf16[256,256]{1,0:T(8,128)(2,1)S(1)}, u32[]{:S(2)}, u32[]{:S(2)}) collective-permute-start(bf16[256,256]{1,0:T(8,128)(2,1)S(1)} %copy-done.2), channel_id=1, source_target_pairs={{0,2},{1,3},{2,4},{3,5},{4,6},{5,7},{6,0},{7,1},{8,10},{9,11},{10,... | collective-permute-start | bytes 393224 | tf_op jit(solution)/shard_map/ppermute | solution.py:62
  53.9 4.6 %collective-permute-start.2 = (bf16[256,256]{1,0:T(8,128)(2,1)S(1)}, bf16[256,256]{1,0:T(8,128)(2,1)S(1)}, u32[]{:S(2)}, u32[]{:S(2)}) collective-permute-start(bf16[256,256]{1,0:T(8,128)(2,1)S(1)} %copy-done.2), channel_id=1, source_target_pairs={{0,3},{1,4},{2,5},{3,6},{4,7},{5,0},{6,1},{7,2},{8,11},{9,12},{10,... | collective-permute-start | bytes 393224 | tf_op jit(solution)/shard_map/ppermute | solution.py:62
  58.6 3.5 %collective-permute-start.3 = (bf16[256,256]{1,0:T(8,128)(2,1)S(1)}, bf16[256,256]{1,0:T(8,128)(2,1)S(1)}, u32[]{:S(2)}, u32[]{:S(2)}) collective-permute-start(bf16[256,256]{1,0:T(8,128)(2,1)S(1)} %copy-done.2), channel_id=1, source_target_pairs={{0,4},{1,5},{2,6},{3,7},{4,0},{5,1},{6,2},{7,3},{8,12},{9,13},{10,... | collective-permute-start | bytes 393224 | tf_op jit(solution)/shard_map/ppermute | solution.py:62
  62.1 4.9 %collective-permute-start.4 = (bf16[256,256]{1,0:T(8,128)(2,1)S(1)}, bf16[256,256]{1,0:T(8,128)(2,1)S(1)}, u32[]{:S(2)}, u32[]{:S(2)}) collective-permute-start(bf16[256,256]{1,0:T(8,128)(2,1)S(1)} %copy-done.2), channel_id=1, source_target_pairs={{0,5},{1,6},{2,7},{3,0},{4,1},{5,2},{6,3},{7,4},{8,13},{9,14},{10,... | collective-permute-start | bytes 393224 | tf_op jit(solution)/shard_map/ppermute | solution.py:62
  74.7 5.0 %collective-permute-start.5 = (bf16[256,256]{1,0:T(8,128)(2,1)S(1)}, bf16[256,256]{1,0:T(8,128)(2,1)S(1)}, u32[]{:S(2)}, u32[]{:S(2)}) collective-permute-start(bf16[256,256]{1,0:T(8,128)(2,1)S(1)} %copy-done.2), channel_id=1, source_target_pairs={{0,6},{1,7},{2,0},{3,1},{4,2},{5,3},{6,4},{7,5},{8,14},{9,15},{10,... | collective-permute-start | bytes 393224 | tf_op jit(solution)/shard_map/ppermute | solution.py:62
  80.3 3.1 %collective-permute-start.6 = (bf16[256,256]{1,0:T(8,128)(2,1)S(1)}, bf16[256,256]{1,0:T(8,128)(2,1)S(1)}, u32[]{:S(2)}, u32[]{:S(2)}) collective-permute-start(bf16[256,256]{1,0:T(8,128)(2,1)S(1)} %copy-done.2), channel_id=1, source_target_pairs={{0,7},{1,0},{2,1},{3,2},{4,3},{5,4},{6,5},{7,6},{8,15},{9,8},{10,9... | collective-permute-start | bytes 393224 | tf_op jit(solution)/shard_map/ppermute | solution.py:62
  92.2 2.9 %copy.70 = f32[256,8,256]{0,2,1:T(8,128)} copy(f32[256,8,256]{2,0,1:T(8,128)} %convert_bitcast_fusion) | data formatting | bytes 4194304 | tf_op jit(solution)/shard_map/convert_element_type | solution.py:18
  97.6 45.0 %all-gather.2.cloned.1.call-done = bf16[2048,1792]{1,0:T(8,128)(2,1)} async-done(((bf16[32,1792]{1,0:T(8,128)(2,1)}), bf16[2048,1792]{1,0:T(8,128)(2,1)}) %all-gather.2.cloned.1.call-update) | async-done | bytes 7340048 | tf_op jit(solution)/shard_map/all_gather | solution.py:170
  142.6 2.9 %fusion.12 = f32[256,768]{1,0:T(8,128)S(1)} fusion(bf16[256,2048]{0,1:T(8,128)(2,1)S(1)} %fusion.11, bf16[2048,1792]{1,0:T(8,128)(2,1)} %all-gather.2.cloned.1.call-done, f32[768]{0:T(1024)} %add.220), kind=kOutput, calls=%fused_computation.20 | convolution fusion | flops 805502976 | bytes 4984832 | tf_op jit(solution)/shard_map/dot_general | solution.py:48
  148.5 12.4 %all-to-all-done.1.kc_ref.vc_ref = bf16[64,2,2,32,256]{4,3,2,1,0:T(8,128)(2,1)} async-done(((bf16[64,2,2,32,256]{4,3,2,1,0:T(8,128)(2,1)}), bf16[64,2,2,32,256]{4,3,2,1,0:T(8,128)(2,1)}, u32[]{:S(2)}, u32[]{:S(2)}) %all-to-all-start.1) | async-done | bytes 4194336 | tf_op jit(solution)/shard_map/all_to_all | solution.py:207
  161.0 8.3 %shard_map.168 = bf16[128,256]{1,0:T(8,128)(2,1)} custom-call(bf16[256,256]{1,0:T(8,128)(2,1)} %copy.76.q_ref, bf16[64,2,2,32,256]{4,3,2,1,0:T(8,128)(2,1)} %all-to-all-done.1.kc_ref.vc_ref, bf16[64,2,2,32,256]{4,3,2,1,0:T(8,128)(2,1)} %all-to-all-done.1.kc_ref.vc_ref, bf16[256,256]{1,0:T(8,128)(2,1)} %copy.77.kn_ref, bf16[256,256]{1,0:T(8,128)(2,1)} %bitcast.133, ...), custom_call_target="tpu_custom_call" | custom-call | tf_op jit(solution)/shard_map/pallas_call | solution.py:122
  171.8 6.9 %all-to-all-start.3 = ((bf16[128,8,256]{2,0,1:T(8,128)(2,1)}), bf16[128,8,256]{2,0,1:T(8,128)(2,1)S(1)}, u32[]{:S(2)}, u32[]{:S(2)}) async-start(bf16[128,8,256]{2,0,1:T(8,128)(2,1)} %bitcast.126), calls=%async_computation.3 | async-start | bytes 1048576 | tf_op jit(solution)/shard_map/all_to_all | solution.py:238
  178.7 8.3 %shard_map.167 = bf16[128,256]{1,0:T(8,128)(2,1)} custom-call(bf16[256,256]{1,0:T(8,128)(2,1)} %copy.76.q_ref, bf16[64,2,2,32,256]{4,3,2,1,0:T(8,128)(2,1)} %all-to-all-done.1.kc_ref.vc_ref, bf16[64,2,2,32,256]{4,3,2,1,0:T(8,128)(2,1)} %all-to-all-done.1.kc_ref.vc_ref, bf16[256,256]{1,0:T(8,128)(2,1)} %copy.77.kn_ref, bf16[256,256]{1,0:T(8,128)(2,1)} %bitcast.134, ...), custom_call_target="tpu_custom_call" | custom-call | tf_op jit(solution)/shard_map/pallas_call | solution.py:122
  189.6 7.1 %all-to-all-done.3 = bf16[128,8,256]{2,0,1:T(8,128)(2,1)S(1)} async-done(((bf16[128,8,256]{2,0,1:T(8,128)(2,1)}), bf16[128,8,256]{2,0,1:T(8,128)(2,1)S(1)}, u32[]{:S(2)}, u32[]{:S(2)}) %all-to-all-start.3) | async-done | bytes 524320 | tf_op jit(solution)/shard_map/all_to_all | solution.py:238
  196.6 3.6 %all-to-all-start.2 = ((bf16[128,8,256]{2,0,1:T(8,128)(2,1)}), bf16[128,8,256]{2,0,1:T(8,128)(2,1)S(1)}, u32[]{:S(2)}, u32[]{:S(2)}) async-start(bf16[128,8,256]{2,0,1:T(8,128)(2,1)} %bitcast.127), calls=%async_computation.2 | async-start | bytes 1048576 | tf_op jit(solution)/shard_map/all_to_all | solution.py:238
  201.1 17.0 %all-to-all-done.2 = bf16[128,8,256]{2,0,1:T(8,128)(2,1)S(1)} async-done(((bf16[128,8,256]{2,0,1:T(8,128)(2,1)}), bf16[128,8,256]{2,0,1:T(8,128)(2,1)S(1)}, u32[]{:S(2)}, u32[]{:S(2)}) %all-to-all-start.2) | async-done | bytes 524320 | tf_op jit(solution)/shard_map/all_to_all | solution.py:238
  220.2 3.5 %all-to-all-start.5 = ((bf16[8,128,256]{1,2,0:T(8,128)(2,1)}), bf16[8,128,256]{1,2,0:T(8,128)(2,1)S(1)}, u32[]{:S(2)}, u32[]{:S(2)}) async-start(bf16[8,128,256]{1,2,0:T(8,128)(2,1)} %broadcast_in_dim.59), calls=%async_computation.5 | async-start | bytes 1048576 | tf_op jit(solution)/shard_map/all_to_all | solution.py:55
  223.8 17.8 %all-to-all-done.5 = bf16[8,128,256]{1,2,0:T(8,128)(2,1)S(1)} async-done(((bf16[8,128,256]{1,2,0:T(8,128)(2,1)}), bf16[8,128,256]{1,2,0:T(8,128)(2,1)S(1)}, u32[]{:S(2)}, u32[]{:S(2)}) %all-to-all-start.5) | async-done | bytes 524320 | tf_op jit(solution)/shard_map/all_to_all | solution.py:55
  242.4 3.5 %all-to-all-start.4 = ((bf16[8,128,256]{1,2,0:T(8,128)(2,1)}), bf16[8,128,256]{1,2,0:T(8,128)(2,1)S(1)}, u32[]{:S(2)}, u32[]{:S(2)}) async-start(bf16[8,128,256]{1,2,0:T(8,128)(2,1)} %broadcast_in_dim.58), calls=%async_computation.4 | async-start | bytes 1048576 | tf_op jit(solution)/shard_map/all_to_all | solution.py:55
  247.2 16.6 %all-to-all-done.4 = bf16[8,128,256]{1,2,0:T(8,128)(2,1)S(1)} async-done(((bf16[8,128,256]{1,2,0:T(8,128)(2,1)}), bf16[8,128,256]{1,2,0:T(8,128)(2,1)S(1)}, u32[]{:S(2)}, u32[]{:S(2)}) %all-to-all-start.4) | async-done | bytes 524320 | tf_op jit(solution)/shard_map/all_to_all | solution.py:55
  (126 shorter events, 46.8 us)
Async XLA Ops:
  7.2 30.6 %copy-start = (bf16[48,2,32,256]{3,2,1,0:T(8,128)(2,1)S(1)}, bf16[48,2,32,256]{3,2,1,0:T(8,128)(2,1)}, u32[]{:S(2)}) copy-start(bf16[48,2,32,256]{3,2,1,0:T(8,128)(2,1)} %param.22) | copy-start | bytes 4718596
  7.2 135.4 %all-gather.2.cloned.1.call-start = ((), (), s32[]{:S(2)}) async-start(), calls=%async_computation.6 | async-start | bytes 7454720 | tf_op jit(solution)/shard_map/all_gather | solution.py:170
  40.6 5.8 %copy-start.2 = (bf16[256,256]{1,0:T(8,128)(2,1)S(1)}, bf16[256,256]{1,0:T(8,128)(2,1)}, u32[]{:S(2)}) copy-start(bf16[256,256]{1,0:T(8,128)(2,1)} %param.16) | copy-start | bytes 393220
  40.6 26.4 %copy-start.6 = (s32[256]{0:T(256)S(1)}, s32[256]{0:T(256)}, u32[]{:S(2)}) copy-start(s32[256]{0:T(256)} %param.29) | copy-start | bytes 3076
  40.6 27.1 %copy-start.5 = (s32[4]{0:T(128)S(1)}, s32[4]{0:T(128)}, u32[]{:S(2)}) copy-start(s32[4]{0:T(128)} %param.30) | copy-start | bytes 52
  40.6 31.9 %copy-start.11 = (f32[3,256]{1,0:T(4,128)S(1)}, f32[3,256]{1,0:T(4,128)}, u32[]{:S(2)}) copy-start(f32[3,256]{1,0:T(4,128)} %param.21) | copy-start | bytes 9220
  40.6 120.3 %all-to-all-start.1 = ((bf16[64,2,2,32,256]{4,3,2,1,0:T(8,128)(2,1)}), bf16[64,2,2,32,256]{4,3,2,1,0:T(8,128)(2,1)}, u32[]{:S(2)}, u32[]{:S(2)}) async-start(bf16[64,2,2,32,256]{4,3,2,1,0:T(8,128)(2,1)} %bitcast.128), calls=%async_computation.1 | async-start | bytes 8388608 | tf_op jit(solution)/shard_map/all_to_all | solution.py:207
  46.5 28.2 %collective-permute-start = (bf16[256,256]{1,0:T(8,128)(2,1)S(1)}, bf16[256,256]{1,0:T(8,128)(2,1)S(1)}, u32[]{:S(2)}, u32[]{:S(2)}) collective-permute-start(bf16[256,256]{1,0:T(8,128)(2,1)S(1)} %copy-done.2), channel_id=1, source_target_pairs={{0,1},{1,2},{2,3},{3,4},{4,5},{5,6},{6,7},{7,0},{8,9},{9,10},{10,1... | collective-permute-start | bytes 393224 | tf_op jit(solution)/shard_map/ppermute | solution.py:62
  49.7 30.6 %collective-permute-start.1 = (bf16[256,256]{1,0:T(8,128)(2,1)S(1)}, bf16[256,256]{1,0:T(8,128)(2,1)S(1)}, u32[]{:S(2)}, u32[]{:S(2)}) collective-permute-start(bf16[256,256]{1,0:T(8,128)(2,1)S(1)} %copy-done.2), channel_id=1, source_target_pairs={{0,2},{1,3},{2,4},{3,5},{4,6},{5,7},{6,0},{7,1},{8,10},{9,11},{10,... | collective-permute-start | bytes 393224 | tf_op jit(solution)/shard_map/ppermute | solution.py:62
  53.9 30.2 %collective-permute-start.2 = (bf16[256,256]{1,0:T(8,128)(2,1)S(1)}, bf16[256,256]{1,0:T(8,128)(2,1)S(1)}, u32[]{:S(2)}, u32[]{:S(2)}) collective-permute-start(bf16[256,256]{1,0:T(8,128)(2,1)S(1)} %copy-done.2), channel_id=1, source_target_pairs={{0,3},{1,4},{2,5},{3,6},{4,7},{5,0},{6,1},{7,2},{8,11},{9,12},{10,... | collective-permute-start | bytes 393224 | tf_op jit(solution)/shard_map/ppermute | solution.py:62
  58.6 26.2 %collective-permute-start.3 = (bf16[256,256]{1,0:T(8,128)(2,1)S(1)}, bf16[256,256]{1,0:T(8,128)(2,1)S(1)}, u32[]{:S(2)}, u32[]{:S(2)}) collective-permute-start(bf16[256,256]{1,0:T(8,128)(2,1)S(1)} %copy-done.2), channel_id=1, source_target_pairs={{0,4},{1,5},{2,6},{3,7},{4,0},{5,1},{6,2},{7,3},{8,12},{9,13},{10,... | collective-permute-start | bytes 393224 | tf_op jit(solution)/shard_map/ppermute | solution.py:62
  62.1 23.3 %collective-permute-start.4 = (bf16[256,256]{1,0:T(8,128)(2,1)S(1)}, bf16[256,256]{1,0:T(8,128)(2,1)S(1)}, u32[]{:S(2)}, u32[]{:S(2)}) collective-permute-start(bf16[256,256]{1,0:T(8,128)(2,1)S(1)} %copy-done.2), channel_id=1, source_target_pairs={{0,5},{1,6},{2,7},{3,0},{4,1},{5,2},{6,3},{7,4},{8,13},{9,14},{10,... | collective-permute-start | bytes 393224 | tf_op jit(solution)/shard_map/ppermute | solution.py:62
  68.4 19.8 %copy-start.4 = (s32[256]{0:T(256)}, s32[256]{0:T(256)S(1)}, u32[]{:S(2)}) copy-start(s32[256]{0:T(256)S(1)} %broadcast_subtract_fusion) | copy-start | bytes 3076
  74.7 11.4 %collective-permute-start.5 = (bf16[256,256]{1,0:T(8,128)(2,1)S(1)}, bf16[256,256]{1,0:T(8,128)(2,1)S(1)}, u32[]{:S(2)}, u32[]{:S(2)}) collective-permute-start(bf16[256,256]{1,0:T(8,128)(2,1)S(1)} %copy-done.2), channel_id=1, source_target_pairs={{0,6},{1,7},{2,0},{3,1},{4,2},{5,3},{6,4},{7,5},{8,14},{9,15},{10,... | collective-permute-start | bytes 393224 | tf_op jit(solution)/shard_map/ppermute | solution.py:62
  80.3 7.8 %collective-permute-start.6 = (bf16[256,256]{1,0:T(8,128)(2,1)S(1)}, bf16[256,256]{1,0:T(8,128)(2,1)S(1)}, u32[]{:S(2)}, u32[]{:S(2)}) collective-permute-start(bf16[256,256]{1,0:T(8,128)(2,1)S(1)} %copy-done.2), channel_id=1, source_target_pairs={{0,7},{1,0},{2,1},{3,2},{4,3},{5,4},{6,5},{7,6},{8,15},{9,8},{10,9... | collective-permute-start | bytes 393224 | tf_op jit(solution)/shard_map/ppermute | solution.py:62
  92.2 3.6 %copy-start.7 = (f32[2048]{0:T(1024)S(1)}, f32[2048]{0:T(1024)}, u32[]{:S(2)}) copy-start(f32[2048]{0:T(1024)} %param.19) | copy-start | bytes 24580
  92.2 3.6 %copy-start.8 = (f32[2048]{0:T(1024)S(1)}, f32[2048]{0:T(1024)}, u32[]{:S(2)}) copy-start(f32[2048]{0:T(1024)} %param.18) | copy-start | bytes 24580
  171.8 24.8 %all-to-all-start.3 = ((bf16[128,8,256]{2,0,1:T(8,128)(2,1)}), bf16[128,8,256]{2,0,1:T(8,128)(2,1)S(1)}, u32[]{:S(2)}, u32[]{:S(2)}) async-start(bf16[128,8,256]{2,0,1:T(8,128)(2,1)} %bitcast.126), calls=%async_computation.3 | async-start | bytes 1048576 | tf_op jit(solution)/shard_map/all_to_all | solution.py:238
  196.6 49.2 %copy-start.12 = (f32[3,256]{1,0:T(4,128)S(1)}, f32[3,256]{1,0:T(4,128)}, u32[]{:S(2)}) copy-start(f32[3,256]{1,0:T(4,128)} %param.28) | copy-start | bytes 9220
  196.6 21.5 %all-to-all-start.2 = ((bf16[128,8,256]{2,0,1:T(8,128)(2,1)}), bf16[128,8,256]{2,0,1:T(8,128)(2,1)S(1)}, u32[]{:S(2)}, u32[]{:S(2)}) async-start(bf16[128,8,256]{2,0,1:T(8,128)(2,1)} %bitcast.127), calls=%async_computation.2 | async-start | bytes 1048576 | tf_op jit(solution)/shard_map/all_to_all | solution.py:238
  218.2 46.1 %copy-start.9 = (f32[2048]{0:T(1024)S(1)}, f32[2048]{0:T(1024)}, u32[]{:S(2)}) copy-start(f32[2048]{0:T(1024)} %param.26) | copy-start | bytes 24580
  218.2 46.1 %copy-start.10 = (f32[2048]{0:T(1024)S(1)}, f32[2048]{0:T(1024)}, u32[]{:S(2)}) copy-start(f32[2048]{0:T(1024)} %param.25) | copy-start | bytes 24580
  220.2 21.4 %all-to-all-start.5 = ((bf16[8,128,256]{1,2,0:T(8,128)(2,1)}), bf16[8,128,256]{1,2,0:T(8,128)(2,1)S(1)}, u32[]{:S(2)}, u32[]{:S(2)}) async-start(bf16[8,128,256]{1,2,0:T(8,128)(2,1)} %broadcast_in_dim.59), calls=%async_computation.5 | async-start | bytes 1048576 | tf_op jit(solution)/shard_map/all_to_all | solution.py:55
  242.4 21.4 %all-to-all-start.4 = ((bf16[8,128,256]{1,2,0:T(8,128)(2,1)}), bf16[8,128,256]{1,2,0:T(8,128)(2,1)S(1)}, u32[]{:S(2)}, u32[]{:S(2)}) async-start(bf16[8,128,256]{1,2,0:T(8,128)(2,1)} %broadcast_in_dim.58), calls=%async_computation.4 | async-start | bytes 1048576 | tf_op jit(solution)/shard_map/all_to_all | solution.py:55
  (2 other events, 2.3 us)
Sparse Core Ops, SparseCore 0:
  11.9 130.6 all-gather.1

commit v7 on v4

--- a/solution.py
+++ b/solution.py
@@ -191,8 +191,16 @@
     pool_count = lax.axis_size("pool")
     blocks_here = cache_pool.shape[0]
     entries = block_table.reshape(-1)
-    holder_order = jnp.argsort(entries // blocks_here, stable=True)
-    slot_ids = (entries % blocks_here)[holder_order].reshape(pool_count, -1)
+    holder = entries // blocks_here
+    entry_ids = jnp.arange(entries.shape[0], dtype=jnp.int32)
+    earlier_same = (holder[:, None] == holder[None, :]) & (entry_ids[None, :] < entry_ids[:, None])
+    per_holder = entries.shape[0] // pool_count
+    slot_of = holder * per_holder + jnp.sum(earlier_same.astype(jnp.int32), axis=1)
+    placed = slot_of[:, None] == entry_ids[None, :]
+    holder_order = jnp.sum(jnp.where(placed, entry_ids[:, None], 0), axis=0)
+    slot_ids = jnp.sum(jnp.where(placed, (entries % blocks_here)[:, None], 0), axis=0).reshape(
+        pool_count, -1
+    )
     wanted = lax.all_to_all(slot_ids, "pool", split_axis=0, concat_axis=0, tiled=True)
     packed = cache_pool[wanted.reshape(-1)].reshape((pool_count, -1) + cache_pool.shape[1:])
     arrived = lax.all_to_all(packed, "pool", split_axis=0, concat_axis=0, tiled=True)

time: 268 us -> 262 us (0.978)
  waiting for transfers between devices: 119 us -> 116 us
    all_gather x1, waiting for transfers between devices: 36.2 us -> 45.4 us  [local(): gathered = lax.all_gather(joined, 'pool', axis=0, tiled=True)]
    all_to_all x1, waiting for transfers between devices: 21 us -> 12 us  [local(): lax.all_to_all(packed, 'pool', split_axis=0, concat_axis=0, tiled=True)]
  transfers between devices with their start and end apart: 11 -> 11, of which waited for: 6 -> 5; matrix products, arithmetic and copies ran while one was open for 14% -> 12% of each run, Pallas kernels for 0% -> 0%
where the time goes in v7:
time: 262 us; the launch traced here: 261 us
  waiting for transfers between devices  116 us (44%)
  starting transfers between devices  45 us (17%)
  local copies, waits for them, and re-layouts  26.6 us (10%)
  blocking collectives  23.9 us (9%)
  between operations  14.4 us (5%)
  Pallas kernels  13.7 us (5%)
  other arithmetic  13.3 us (5%)
  matrix products  7.57 us (3%)
    all_gather x1, waiting for transfers between devices, local(): gathered = lax.all_gather(joined, 'pool', axis=0, tiled=True)  45.4 us
    all_to_all x1, waiting for transfers between devices, mp_gather(): lax.all_to_all(spread, 'mp', split_axis=0, concat_axis=2, tiled=True)  29.1 us
    ppermute x7, starting transfers between devices, mp_permute_gather(): lax.ppermute(block, 'mp', [(src, (src + shift) % mp_count) for src in ran...  28.6 us
    all_to_all x1, waiting for transfers between devices, local(): lax.all_to_all(pieces, 'mp', split_axis=1, concat_axis=1, tiled=True)  28.5 us
    all_to_all x1, blocking collectives, local(): lax.all_to_all(slot_ids, 'pool', split_axis=0, concat_axis=0, tiled=True)  23.9 us
    pallas_call x1, Pallas kernels, attention_call(): pl.pallas_call(attention_body, grid=grid, in_specs=[pl.BlockSpec((Q_CHUNK...  13.7 us
    all_to_all x1, waiting for transfers between devices, local(): lax.all_to_all(packed, 'pool', split_axis=0, concat_axis=0, tiled=True)  12 us
    unnamed x37, local copies, waits for them, and re-layouts  7.58 us
  transfers between devices with their start and end apart: 11, of which 5 were waited for; matrix products, arithmetic and copies ran while one was open for 12% of the time, Pallas kernels for 0%

profile of v7, /device:TPU:1, one launch (start us, length us, event | category | flops | bytes accessed | tf_op | source)
XLA Modules:
  0.0 261.0 jit_solution(1278882499420584838)
XLA Ops:
  12.4 23.9 %all_to_all.28 = s32[64,1,2]{2,1,0:T(1,128)S(1)} all-to-all(s32[64,1,2]{2,1,0:T(1,128)S(1)} %bitcast.117), channel_id=1, replica_groups=mesh['pool'=64,'mp'=8] {'pool'}, dimensions={0} | all-to-all | bytes 1024 | tf_op jit(solution)/shard_map/all_to_all | solution.py:204
  37.8 2.9 %gather_fusion.1 = bf16[128,2,32,256]{3,2,1,0:T(8,128)(2,1)} fusion(bf16[48,2,32,256]{3,2,1,0:T(8,128)(2,1)S(1)} %copy-done, s32[1024]{0:T(1024)S(1)} %pad_clamp_fusion), kind=kCustom, calls=%fused_computation.1 | custom fusion | bytes 8389120 | tf_op jit(solution)/shard_map/gather | solution.py:205
  40.7 5.8 %all-to-all-start.1 = ((bf16[64,2,2,32,256]{4,3,2,1,0:T(8,128)(2,1)}), bf16[64,2,2,32,256]{4,3,2,1,0:T(8,128)(2,1)}, u32[]{:S(2)}, u32[]{:S(2)}) async-start(bf16[64,2,2,32,256]{4,3,2,1,0:T(8,128)(2,1)} %bitcast.102), calls=%async_computation.1 | async-start | bytes 8388608 | tf_op jit(solution)/shard_map/all_to_all | solution.py:206
  46.5 3.2 %collective-permute-start = (bf16[256,256]{1,0:T(8,128)(2,1)S(1)}, bf16[256,256]{1,0:T(8,128)(2,1)S(1)}, u32[]{:S(2)}, u32[]{:S(2)}) collective-permute-start(bf16[256,256]{1,0:T(8,128)(2,1)S(1)} %copy-done.2), channel_id=1, source_target_pairs={{0,1},{1,2},{2,3},{3,4},{4,5},{5,6},{6,7},{7,0},{8,9},{9,10},{10,1... | collective-permute-start | bytes 393224 | tf_op jit(solution)/shard_map/ppermute | solution.py:60
  49.7 4.2 %collective-permute-start.1 = (bf16[256,256]{1,0:T(8,128)(2,1)S(1)}, bf16[256,256]{1,0:T(8,128)(2,1)S(1)}, u32[]{:S(2)}, u32[]{:S(2)}) collective-permute-start(bf16[256,256]{1,0:T(8,128)(2,1)S(1)} %copy-done.2), channel_id=1, source_target_pairs={{0,2},{1,3},{2,4},{3,5},{4,6},{5,7},{6,0},{7,1},{8,10},{9,11},{10,... | collective-permute-start | bytes 393224 | tf_op jit(solution)/shard_map/ppermute | solution.py:60
  53.9 4.6 %collective-permute-start.2 = (bf16[256,256]{1,0:T(8,128)(2,1)S(1)}, bf16[256,256]{1,0:T(8,128)(2,1)S(1)}, u32[]{:S(2)}, u32[]{:S(2)}) collective-permute-start(bf16[256,256]{1,0:T(8,128)(2,1)S(1)} %copy-done.2), channel_id=1, source_target_pairs={{0,3},{1,4},{2,5},{3,6},{4,7},{5,0},{6,1},{7,2},{8,11},{9,12},{10,... | collective-permute-start | bytes 393224 | tf_op jit(solution)/shard_map/ppermute | solution.py:60
  58.6 3.5 %collective-permute-start.3 = (bf16[256,256]{1,0:T(8,128)(2,1)S(1)}, bf16[256,256]{1,0:T(8,128)(2,1)S(1)}, u32[]{:S(2)}, u32[]{:S(2)}) collective-permute-start(bf16[256,256]{1,0:T(8,128)(2,1)S(1)} %copy-done.2), channel_id=1, source_target_pairs={{0,4},{1,5},{2,6},{3,7},{4,0},{5,1},{6,2},{7,3},{8,12},{9,13},{10,... | collective-permute-start | bytes 393224 | tf_op jit(solution)/shard_map/ppermute | solution.py:60
  62.1 4.9 %collective-permute-start.4 = (bf16[256,256]{1,0:T(8,128)(2,1)S(1)}, bf16[256,256]{1,0:T(8,128)(2,1)S(1)}, u32[]{:S(2)}, u32[]{:S(2)}) collective-permute-start(bf16[256,256]{1,0:T(8,128)(2,1)S(1)} %copy-done.2), channel_id=1, source_target_pairs={{0,5},{1,6},{2,7},{3,0},{4,1},{5,2},{6,3},{7,4},{8,13},{9,14},{10,... | collective-permute-start | bytes 393224 | tf_op jit(solution)/shard_map/ppermute | solution.py:60
  68.4 2.5 fusion.31
  74.6 5.0 %collective-permute-start.5 = (bf16[256,256]{1,0:T(8,128)(2,1)S(1)}, bf16[256,256]{1,0:T(8,128)(2,1)S(1)}, u32[]{:S(2)}, u32[]{:S(2)}) collective-permute-start(bf16[256,256]{1,0:T(8,128)(2,1)S(1)} %copy-done.2), channel_id=1, source_target_pairs={{0,6},{1,7},{2,0},{3,1},{4,2},{5,3},{6,4},{7,5},{8,14},{9,15},{10,... | collective-permute-start | bytes 393224 | tf_op jit(solution)/shard_map/ppermute | solution.py:60
  80.3 3.1 %collective-permute-start.6 = (bf16[256,256]{1,0:T(8,128)(2,1)S(1)}, bf16[256,256]{1,0:T(8,128)(2,1)S(1)}, u32[]{:S(2)}, u32[]{:S(2)}) collective-permute-start(bf16[256,256]{1,0:T(8,128)(2,1)S(1)} %copy-done.2), channel_id=1, source_target_pairs={{0,7},{1,0},{2,1},{3,2},{4,3},{5,4},{6,5},{7,6},{8,15},{9,8},{10,9... | collective-permute-start | bytes 393224 | tf_op jit(solution)/shard_map/ppermute | solution.py:60
  88.8 1.9 gather_fusion
  90.7 1.5 convert_bitcast_fusion
  92.2 3.0 %copy.53 = f32[256,8,256]{0,2,1:T(8,128)} copy(f32[256,8,256]{2,0,1:T(8,128)} %convert_bitcast_fusion) | data formatting | bytes 4194304 | tf_op jit(solution)/shard_map/convert_element_type | solution.py:16
  97.6 45.4 %all-gather.2.cloned.1.call-done = bf16[2048,1792]{1,0:T(8,128)(2,1)} async-done(((bf16[32,1792]{1,0:T(8,128)(2,1)}), bf16[2048,1792]{1,0:T(8,128)(2,1)}) %all-gather.2.cloned.1.call-update) | async-done | bytes 7340048 | tf_op jit(solution)/shard_map/all_gather | solution.py:169
  143.0 2.9 %fusion.16 = f32[256,768]{1,0:T(8,128)S(1)} fusion(bf16[256,2048]{0,1:T(8,128)(2,1)S(1)} %fusion.15, bf16[2048,1792]{1,0:T(8,128)(2,1)} %all-gather.2.cloned.1.call-done, f32[768]{0:T(1024)} %add.184), kind=kOutput, calls=%fused_computation.26 | convolution fusion | flops 805502976 | bytes 4984832 | tf_op jit(solution)/shard_map/dot_general | solution.py:46
  149.0 12.0 %all-to-all-done.1.kc_ref.vc_ref = bf16[64,2,2,32,256]{4,3,2,1,0:T(8,128)(2,1)} async-done(((bf16[64,2,2,32,256]{4,3,2,1,0:T(8,128)(2,1)}), bf16[64,2,2,32,256]{4,3,2,1,0:T(8,128)(2,1)}, u32[]{:S(2)}, u32[]{:S(2)}) %all-to-all-start.1) | async-done | bytes 4194336 | tf_op jit(solution)/shard_map/all_to_all | solution.py:206
  161.0 13.7 %shard_map.167 = bf16[256,256]{1,0:T(8,128)(2,1)} custom-call(bf16[256,256]{1,0:T(8,128)(2,1)} %copy.59.q_ref, bf16[64,2,2,32,256]{4,3,2,1,0:T(8,128)(2,1)} %all-to-all-done.1.kc_ref.vc_ref, bf16[64,2,2,32,256]{4,3,2,1,0:T(8,128)(2,1)} %all-to-all-done.1.kc_ref.vc_ref, bf16[256,256]{1,0:T(8,128)(2,1)} %copy.60.kn_ref, bf16[256,256]{1,0:T(8,128)(2,1)} %bitcast.112, ...), custom_call_target="tpu_custom_call" | custom-call | tf_op jit(solution)/shard_map/pallas_call | solution.py:121
  174.7 1.8 convolution_convert_fusion
  177.5 6.8 %all-to-all-start.2 = ((bf16[256,8,256]{2,0,1:T(8,128)(2,1)}), bf16[256,8,256]{2,0,1:T(8,128)(2,1)S(1)}, u32[]{:S(2)}, u32[]{:S(2)}) async-start(bf16[256,8,256]{2,0,1:T(8,128)(2,1)} %bitcast.103), calls=%async_computation.2 | async-start | bytes 2097152 | tf_op jit(solution)/shard_map/all_to_all | solution.py:230
  185.1 28.5 %all-to-all-done.2 = bf16[256,8,256]{2,0,1:T(8,128)(2,1)S(1)} async-done(((bf16[256,8,256]{2,0,1:T(8,128)(2,1)}), bf16[256,8,256]{2,0,1:T(8,128)(2,1)S(1)}, u32[]{:S(2)}, u32[]{:S(2)}) %all-to-all-start.2) | async-done | bytes 1048608 | tf_op jit(solution)/shard_map/all_to_all | solution.py:230
  215.9 3.7 %all-to-all-start.3 = ((bf16[8,256,256]{1,2,0:T(8,128)(2,1)}), bf16[8,256,256]{1,2,0:T(8,128)(2,1)S(1)}, u32[]{:S(2)}, u32[]{:S(2)}) async-start(bf16[8,256,256]{1,2,0:T(8,128)(2,1)} %broadcast_in_dim.56), calls=%async_computation.3 | async-start | bytes 2097152 | tf_op jit(solution)/shard_map/all_to_all | solution.py:53
  219.6 29.1 %all-to-all-done.3 = bf16[8,256,256]{1,2,0:T(8,128)(2,1)S(1)} async-done(((bf16[8,256,256]{1,2,0:T(8,128)(2,1)}), bf16[8,256,256]{1,2,0:T(8,128)(2,1)S(1)}, u32[]{:S(2)}, u32[]{:S(2)}) %all-to-all-start.3) | async-done | bytes 1048608 | tf_op jit(solution)/shard_map/all_to_all | solution.py:53
  250.1 2.9 %fusion.22 = bf16[256,768]{1,0:T(8,128)(2,1)S(1)} fusion(bf16[256,2048]{0,1:T(8,128)(2,1)S(1)} %fusion.9, bf16[2048,1792]{1,0:T(8,128)(2,1)} %all-gather.2.cloned.1.call-done, f32[768]{0:T(1024)S(1)} %add.204), kind=kOutput, calls=%fused_computation.28 | convolution fusion | flops 805699584 | bytes 4590592 | tf_op jit(solution)/shard_map/dot_general | solution.py:46
  (110 shorter events, 29.7 us)
Async XLA Ops:
  7.2 30.6 %copy-start = (bf16[48,2,32,256]{3,2,1,0:T(8,128)(2,1)S(1)}, bf16[48,2,32,256]{3,2,1,0:T(8,128)(2,1)}, u32[]{:S(2)}) copy-start(bf16[48,2,32,256]{3,2,1,0:T(8,128)(2,1)} %param.22) | copy-start | bytes 4718596
  7.2 135.9 %all-gather.2.cloned.1.call-start = ((), (), s32[]{:S(2)}) async-start(), calls=%async_computation.4 | async-start | bytes 7454720 | tf_op jit(solution)/shard_map/all_gather | solution.py:169
  40.6 5.9 %copy-start.2 = (bf16[256,256]{1,0:T(8,128)(2,1)S(1)}, bf16[256,256]{1,0:T(8,128)(2,1)}, u32[]{:S(2)}) copy-start(bf16[256,256]{1,0:T(8,128)(2,1)} %param.16) | copy-start | bytes 393220
  40.6 26.4 %copy-start.7 = (s32[256]{0:T(256)S(1)}, s32[256]{0:T(256)}, u32[]{:S(2)}) copy-start(s32[256]{0:T(256)} %param.29) | copy-start | bytes 3076
  40.6 27.1 %copy-start.6 = (s32[4]{0:T(128)S(1)}, s32[4]{0:T(128)}, u32[]{:S(2)}) copy-start(s32[4]{0:T(128)} %param.30) | copy-start | bytes 52
  40.6 31.9 %copy-start.12 = (f32[3,256]{1,0:T(4,128)S(1)}, f32[3,256]{1,0:T(4,128)}, u32[]{:S(2)}) copy-start(f32[3,256]{1,0:T(4,128)} %param.21) | copy-start | bytes 9220
  40.7 120.3 %all-to-all-start.1 = ((bf16[64,2,2,32,256]{4,3,2,1,0:T(8,128)(2,1)}), bf16[64,2,2,32,256]{4,3,2,1,0:T(8,128)(2,1)}, u32[]{:S(2)}, u32[]{:S(2)}) async-start(bf16[64,2,2,32,256]{4,3,2,1,0:T(8,128)(2,1)} %bitcast.102), calls=%async_computation.1 | async-start | bytes 8388608 | tf_op jit(solution)/shard_map/all_to_all | solution.py:206
  46.5 28.1 %collective-permute-start = (bf16[256,256]{1,0:T(8,128)(2,1)S(1)}, bf16[256,256]{1,0:T(8,128)(2,1)S(1)}, u32[]{:S(2)}, u32[]{:S(2)}) collective-permute-start(bf16[256,256]{1,0:T(8,128)(2,1)S(1)} %copy-done.2), channel_id=1, source_target_pairs={{0,1},{1,2},{2,3},{3,4},{4,5},{5,6},{6,7},{7,0},{8,9},{9,10},{10,1... | collective-permute-start | bytes 393224 | tf_op jit(solution)/shard_map/ppermute | solution.py:60
  49.7 30.6 %collective-permute-start.1 = (bf16[256,256]{1,0:T(8,128)(2,1)S(1)}, bf16[256,256]{1,0:T(8,128)(2,1)S(1)}, u32[]{:S(2)}, u32[]{:S(2)}) collective-permute-start(bf16[256,256]{1,0:T(8,128)(2,1)S(1)} %copy-done.2), channel_id=1, source_target_pairs={{0,2},{1,3},{2,4},{3,5},{4,6},{5,7},{6,0},{7,1},{8,10},{9,11},{10,... | collective-permute-start | bytes 393224 | tf_op jit(solution)/shard_map/ppermute | solution.py:60
  53.9 30.2 %collective-permute-start.2 = (bf16[256,256]{1,0:T(8,128)(2,1)S(1)}, bf16[256,256]{1,0:T(8,128)(2,1)S(1)}, u32[]{:S(2)}, u32[]{:S(2)}) collective-permute-start(bf16[256,256]{1,0:T(8,128)(2,1)S(1)} %copy-done.2), channel_id=1, source_target_pairs={{0,3},{1,4},{2,5},{3,6},{4,7},{5,0},{6,1},{7,2},{8,11},{9,12},{10,... | collective-permute-start | bytes 393224 | tf_op jit(solution)/shard_map/ppermute | solution.py:60
  58.6 26.2 %collective-permute-start.3 = (bf16[256,256]{1,0:T(8,128)(2,1)S(1)}, bf16[256,256]{1,0:T(8,128)(2,1)S(1)}, u32[]{:S(2)}, u32[]{:S(2)}) collective-permute-start(bf16[256,256]{1,0:T(8,128)(2,1)S(1)} %copy-done.2), channel_id=1, source_target_pairs={{0,4},{1,5},{2,6},{3,7},{4,0},{5,1},{6,2},{7,3},{8,12},{9,13},{10,... | collective-permute-start | bytes 393224 | tf_op jit(solution)/shard_map/ppermute | solution.py:60
  62.1 23.3 %collective-permute-start.4 = (bf16[256,256]{1,0:T(8,128)(2,1)S(1)}, bf16[256,256]{1,0:T(8,128)(2,1)S(1)}, u32[]{:S(2)}, u32[]{:S(2)}) collective-permute-start(bf16[256,256]{1,0:T(8,128)(2,1)S(1)} %copy-done.2), channel_id=1, source_target_pairs={{0,5},{1,6},{2,7},{3,0},{4,1},{5,2},{6,3},{7,4},{8,13},{9,14},{10,... | collective-permute-start | bytes 393224 | tf_op jit(solution)/shard_map/ppermute | solution.py:60
  68.3 6.3 %copy-start.5 = (s32[256]{0:T(256)}, s32[256]{0:T(256)S(1)}, u32[]{:S(2)}) copy-start(s32[256]{0:T(256)S(1)} %broadcast_subtract_fusion) | copy-start | bytes 3076
  74.6 11.4 %collective-permute-start.5 = (bf16[256,256]{1,0:T(8,128)(2,1)S(1)}, bf16[256,256]{1,0:T(8,128)(2,1)S(1)}, u32[]{:S(2)}, u32[]{:S(2)}) collective-permute-start(bf16[256,256]{1,0:T(8,128)(2,1)S(1)} %copy-done.2), channel_id=1, source_target_pairs={{0,6},{1,7},{2,0},{3,1},{4,2},{5,3},{6,4},{7,5},{8,14},{9,15},{10,... | collective-permute-start | bytes 393224 | tf_op jit(solution)/shard_map/ppermute | solution.py:60
  80.3 7.8 %collective-permute-start.6 = (bf16[256,256]{1,0:T(8,128)(2,1)S(1)}, bf16[256,256]{1,0:T(8,128)(2,1)S(1)}, u32[]{:S(2)}, u32[]{:S(2)}) collective-permute-start(bf16[256,256]{1,0:T(8,128)(2,1)S(1)} %copy-done.2), channel_id=1, source_target_pairs={{0,7},{1,0},{2,1},{3,2},{4,3},{5,4},{6,5},{7,6},{8,15},{9,8},{10,9... | collective-permute-start | bytes 393224 | tf_op jit(solution)/shard_map/ppermute | solution.py:60
  92.2 3.6 %copy-start.8 = (f32[2048]{0:T(1024)S(1)}, f32[2048]{0:T(1024)}, u32[]{:S(2)}) copy-start(f32[2048]{0:T(1024)} %param.19) | copy-start | bytes 24580
  92.2 3.7 %copy-start.9 = (f32[2048]{0:T(1024)S(1)}, f32[2048]{0:T(1024)}, u32[]{:S(2)}) copy-start(f32[2048]{0:T(1024)} %param.18) | copy-start | bytes 24580
  95.2 1.6 copy-start.1
  177.5 36.1 %all-to-all-start.2 = ((bf16[256,8,256]{2,0,1:T(8,128)(2,1)}), bf16[256,8,256]{2,0,1:T(8,128)(2,1)S(1)}, u32[]{:S(2)}, u32[]{:S(2)}) async-start(bf16[256,8,256]{2,0,1:T(8,128)(2,1)} %bitcast.103), calls=%async_computation.2 | async-start | bytes 2097152 | tf_op jit(solution)/shard_map/all_to_all | solution.py:230
  213.8 5.9 %copy-start.13 = (f32[3,256]{1,0:T(4,128)S(1)}, f32[3,256]{1,0:T(4,128)}, u32[]{:S(2)}) copy-start(f32[3,256]{1,0:T(4,128)} %param.28) | copy-start | bytes 9220
  214.7 34.3 %copy-start.3 = (bf16[256,256]{1,0:T(8,128)(2,1)}, bf16[256,256]{1,0:T(8,128)(2,1)S(1)}, u32[]{:S(2)}) copy-start(bf16[256,256]{1,0:T(8,128)(2,1)S(1)} %add_convert_fusion) | copy-start | bytes 393220
  215.9 33.5 %copy-start.10 = (f32[2048]{0:T(1024)S(1)}, f32[2048]{0:T(1024)}, u32[]{:S(2)}) copy-start(f32[2048]{0:T(1024)} %param.26) | copy-start | bytes 24580
  215.9 33.5 %copy-start.11 = (f32[2048]{0:T(1024)S(1)}, f32[2048]{0:T(1024)}, u32[]{:S(2)}) copy-start(f32[2048]{0:T(1024)} %param.25) | copy-start | bytes 24580
  215.9 32.9 %all-to-all-start.3 = ((bf16[8,256,256]{1,2,0:T(8,128)(2,1)}), bf16[8,256,256]{1,2,0:T(8,128)(2,1)S(1)}, u32[]{:S(2)}, u32[]{:S(2)}) async-start(bf16[8,256,256]{1,2,0:T(8,128)(2,1)} %broadcast_in_dim.56), calls=%async_computation.3 | async-start | bytes 2097152 | tf_op jit(solution)/shard_map/all_to_all | solution.py:53
  (1 other events, 0.7 us)
Sparse Core Ops, SparseCore 0:
  11.9 131.0 all-gather.1

commit v8 on v7

--- a/solution.py
+++ b/solution.py
@@ -222,13 +222,16 @@
         local_req.reshape(1, tok_count),
         local_req.reshape(tok_count, 1),
     )
-    partial_out = lax.dot_general(
-        attended, w_dense_t, (((1,), (1,)), ((), ())), preferred_element_type=jnp.float32
+    partial_out = jnp.einsum(
+        "tr,jcr->jtc",
+        attended,
+        w_dense_t.reshape(mp_count, col_width, -1),
+        preferred_element_type=jnp.float32,
     )
     mp_index = lax.axis_index("mp")
-    pieces = partial_out.astype(jnp.bfloat16).reshape(tok_count, mp_count, col_width)
-    arrived_sums = lax.all_to_all(pieces, "mp", split_axis=1, concat_axis=1, tiled=True)
-    dense_total = jnp.sum(arrived_sums.astype(jnp.float32), axis=1)
+    pieces = partial_out.astype(jnp.bfloat16)
+    arrived_sums = lax.all_to_all(pieces, "mp", split_axis=0, concat_axis=0, tiled=True)
+    dense_total = jnp.sum(arrived_sums.astype(jnp.float32), axis=0)
     own_cols = lambda vec: lax.dynamic_slice_in_dim(vec, mp_index * col_width, col_width, 0)
     own_mlp = lax.dynamic_slice_in_dim(mlp_branch, mp_index * col_width, col_width, 1)
     hidden_out = (

time: 262 us -> 261 us (level)
    unnamed x37 -> x38, local copies, waits for them, and re-layouts: 7.58 us -> 8.55 us
  transfers between devices with their start and end apart: 11 -> 11, of which waited for: 5 -> 5; matrix products, arithmetic and copies ran while one was open for 12% -> 13% of each run, Pallas kernels for 0% -> 0%
where the time goes in v8:
time: 261 us; the launch traced here: 260 us
  waiting for transfers between devices  114 us (44%)
  starting transfers between devices  45 us (17%)
  local copies, waits for them, and re-layouts  27.3 us (10%)
  blocking collectives  23.9 us (9%)
  between operations  14.4 us (6%)
  Pallas kernels  13.8 us (5%)
  other arithmetic  12.5 us (5%)
  matrix products  8.16 us (3%)
    all_gather x1, waiting for transfers between devices, local(): gathered = lax.all_gather(joined, 'pool', axis=0, tiled=True)  45.1 us
    ppermute x7, starting transfers between devices, mp_permute_gather(): lax.ppermute(block, 'mp', [(src, (src + shift) % mp_count) for src in ran...  28.6 us
    all_to_all x1, waiting for transfers between devices, mp_gather(): lax.all_to_all(spread, 'mp', split_axis=0, concat_axis=2, tiled=True)  28.4 us
    all_to_all x1, waiting for transfers between devices, local(): lax.all_to_all(pieces, 'mp', split_axis=0, concat_axis=0, tiled=True)  27.3 us
    all_to_all x1, blocking collectives, local(): lax.all_to_all(slot_ids, 'pool', split_axis=0, concat_axis=0, tiled=True)  23.9 us
    pallas_call x1, Pallas kernels, attention_call(): pl.pallas_call(attention_body, grid=grid, in_specs=[pl.BlockSpec((Q_CHUNK...  13.8 us
    all_to_all x1, waiting for transfers between devices, local(): lax.all_to_all(packed, 'pool', split_axis=0, concat_axis=0, tiled=True)  12.3 us
    unnamed x38, local copies, waits for them, and re-layouts  8.55 us
  transfers between devices with their start and end apart: 11, of which 5 were waited for; matrix products, arithmetic and copies ran while one was open for 13% of the time, Pallas kernels for 0%

profile of v8, /device:TPU:1, one launch (start us, length us, event | category | flops | bytes accessed | tf_op | source)
XLA Modules:
  0.0 259.6 jit_solution(16420055373603445723)
XLA Ops:
  12.4 23.9 %all_to_all.28 = s32[64,1,2]{2,1,0:T(1,128)S(1)} all-to-all(s32[64,1,2]{2,1,0:T(1,128)S(1)} %bitcast.118), channel_id=1, replica_groups=mesh['pool'=64,'mp'=8] {'pool'}, dimensions={0} | all-to-all | bytes 1024 | tf_op jit(solution)/shard_map/all_to_all | solution.py:204
  37.8 2.9 %gather_fusion.1 = bf16[128,2,32,256]{3,2,1,0:T(8,128)(2,1)} fusion(bf16[48,2,32,256]{3,2,1,0:T(8,128)(2,1)S(1)} %copy-done, s32[1024]{0:T(1024)S(1)} %pad_clamp_fusion), kind=kCustom, calls=%fused_computation.1 | custom fusion | bytes 8389120 | tf_op jit(solution)/shard_map/gather | solution.py:205
  40.7 5.8 %all-to-all-start.1 = ((bf16[64,2,2,32,256]{4,3,2,1,0:T(8,128)(2,1)}), bf16[64,2,2,32,256]{4,3,2,1,0:T(8,128)(2,1)}, u32[]{:S(2)}, u32[]{:S(2)}) async-start(bf16[64,2,2,32,256]{4,3,2,1,0:T(8,128)(2,1)} %bitcast.104), calls=%async_computation.1 | async-start | bytes 8388608 | tf_op jit(solution)/shard_map/all_to_all | solution.py:206
  46.5 3.2 %collective-permute-start = (bf16[256,256]{1,0:T(8,128)(2,1)S(1)}, bf16[256,256]{1,0:T(8,128)(2,1)S(1)}, u32[]{:S(2)}, u32[]{:S(2)}) collective-permute-start(bf16[256,256]{1,0:T(8,128)(2,1)S(1)} %copy-done.2), channel_id=1, source_target_pairs={{0,1},{1,2},{2,3},{3,4},{4,5},{5,6},{6,7},{7,0},{8,9},{9,10},{10,1... | collective-permute-start | bytes 393224 | tf_op jit(solution)/shard_map/ppermute | solution.py:60
  49.7 4.2 %collective-permute-start.1 = (bf16[256,256]{1,0:T(8,128)(2,1)S(1)}, bf16[256,256]{1,0:T(8,128)(2,1)S(1)}, u32[]{:S(2)}, u32[]{:S(2)}) collective-permute-start(bf16[256,256]{1,0:T(8,128)(2,1)S(1)} %copy-done.2), channel_id=1, source_target_pairs={{0,2},{1,3},{2,4},{3,5},{4,6},{5,7},{6,0},{7,1},{8,10},{9,11},{10,... | collective-permute-start | bytes 393224 | tf_op jit(solution)/shard_map/ppermute | solution.py:60
  53.9 4.6 %collective-permute-start.2 = (bf16[256,256]{1,0:T(8,128)(2,1)S(1)}, bf16[256,256]{1,0:T(8,128)(2,1)S(1)}, u32[]{:S(2)}, u32[]{:S(2)}) collective-permute-start(bf16[256,256]{1,0:T(8,128)(2,1)S(1)} %copy-done.2), channel_id=1, source_target_pairs={{0,3},{1,4},{2,5},{3,6},{4,7},{5,0},{6,1},{7,2},{8,11},{9,12},{10,... | collective-permute-start | bytes 393224 | tf_op jit(solution)/shard_map/ppermute | solution.py:60
  58.6 3.5 %collective-permute-start.3 = (bf16[256,256]{1,0:T(8,128)(2,1)S(1)}, bf16[256,256]{1,0:T(8,128)(2,1)S(1)}, u32[]{:S(2)}, u32[]{:S(2)}) collective-permute-start(bf16[256,256]{1,0:T(8,128)(2,1)S(1)} %copy-done.2), channel_id=1, source_target_pairs={{0,4},{1,5},{2,6},{3,7},{4,0},{5,1},{6,2},{7,3},{8,12},{9,13},{10,... | collective-permute-start | bytes 393224 | tf_op jit(solution)/shard_map/ppermute | solution.py:60
  62.1 4.9 %collective-permute-start.4 = (bf16[256,256]{1,0:T(8,128)(2,1)S(1)}, bf16[256,256]{1,0:T(8,128)(2,1)S(1)}, u32[]{:S(2)}, u32[]{:S(2)}) collective-permute-start(bf16[256,256]{1,0:T(8,128)(2,1)S(1)} %copy-done.2), channel_id=1, source_target_pairs={{0,5},{1,6},{2,7},{3,0},{4,1},{5,2},{6,3},{7,4},{8,13},{9,14},{10,... | collective-permute-start | bytes 393224 | tf_op jit(solution)/shard_map/ppermute | solution.py:60
  68.5 2.5 fusion.32
  74.7 5.0 %collective-permute-start.5 = (bf16[256,256]{1,0:T(8,128)(2,1)S(1)}, bf16[256,256]{1,0:T(8,128)(2,1)S(1)}, u32[]{:S(2)}, u32[]{:S(2)}) collective-permute-start(bf16[256,256]{1,0:T(8,128)(2,1)S(1)} %copy-done.2), channel_id=1, source_target_pairs={{0,6},{1,7},{2,0},{3,1},{4,2},{5,3},{6,4},{7,5},{8,14},{9,15},{10,... | collective-permute-start | bytes 393224 | tf_op jit(solution)/shard_map/ppermute | solution.py:60
  80.4 3.1 %collective-permute-start.6 = (bf16[256,256]{1,0:T(8,128)(2,1)S(1)}, bf16[256,256]{1,0:T(8,128)(2,1)S(1)}, u32[]{:S(2)}, u32[]{:S(2)}) collective-permute-start(bf16[256,256]{1,0:T(8,128)(2,1)S(1)} %copy-done.2), channel_id=1, source_target_pairs={{0,7},{1,0},{2,1},{3,2},{4,3},{5,4},{6,5},{7,6},{8,15},{9,8},{10,9... | collective-permute-start | bytes 393224 | tf_op jit(solution)/shard_map/ppermute | solution.py:60
  88.9 1.8 gather_fusion
  90.7 1.5 convert_bitcast_fusion
  92.2 2.9 %copy.57 = f32[256,8,256]{0,2,1:T(8,128)} copy(f32[256,8,256]{2,0,1:T(8,128)} %convert_bitcast_fusion) | data formatting | bytes 4194304 | tf_op jit(solution)/shard_map/convert_element_type | solution.py:16
  97.6 45.1 %all-gather.2.cloned.1.call-done = bf16[2048,1792]{1,0:T(8,128)(2,1)} async-done(((bf16[32,1792]{1,0:T(8,128)(2,1)}), bf16[2048,1792]{1,0:T(8,128)(2,1)}) %all-gather.2.cloned.1.call-update) | async-done | bytes 7340048 | tf_op jit(solution)/shard_map/all_gather | solution.py:169
  142.7 2.9 %fusion.17 = f32[256,768]{1,0:T(8,128)S(1)} fusion(bf16[256,2048]{0,1:T(8,128)(2,1)S(1)} %fusion.15, bf16[2048,1792]{1,0:T(8,128)(2,1)} %all-gather.2.cloned.1.call-done, f32[768]{0:T(1024)} %add.184), kind=kOutput, calls=%fused_computation.27 | convolution fusion | flops 805502976 | bytes 4984832 | tf_op jit(solution)/shard_map/dot_general | solution.py:46
  148.7 12.3 %all-to-all-done.1.kc_ref.vc_ref = bf16[64,2,2,32,256]{4,3,2,1,0:T(8,128)(2,1)} async-done(((bf16[64,2,2,32,256]{4,3,2,1,0:T(8,128)(2,1)}), bf16[64,2,2,32,256]{4,3,2,1,0:T(8,128)(2,1)}, u32[]{:S(2)}, u32[]{:S(2)}) %all-to-all-start.1) | async-done | bytes 4194336 | tf_op jit(solution)/shard_map/all_to_all | solution.py:206
  161.0 13.8 %shard_map.167 = bf16[256,256]{1,0:T(8,128)(2,1)} custom-call(bf16[256,256]{1,0:T(8,128)(2,1)} %copy.61.q_ref, bf16[64,2,2,32,256]{4,3,2,1,0:T(8,128)(2,1)} %all-to-all-done.1.kc_ref.vc_ref, bf16[64,2,2,32,256]{4,3,2,1,0:T(8,128)(2,1)} %all-to-all-done.1.kc_ref.vc_ref, bf16[256,256]{1,0:T(8,128)(2,1)} %copy.62.kn_ref, bf16[256,256]{1,0:T(8,128)(2,1)} %bitcast.113, ...), custom_call_target="tpu_custom_call" | custom-call | tf_op jit(solution)/shard_map/pallas_call | solution.py:121
  174.8 2.4 fusion.16
  177.1 6.8 %all-to-all-start.2 = ((bf16[8,256,256]{1,2,0:T(8,128)(2,1)}), bf16[8,256,256]{1,2,0:T(8,128)(2,1)S(1)}, u32[]{:S(2)}, u32[]{:S(2)}) async-start(bf16[8,256,256]{1,2,0:T(8,128)(2,1)} %fusion.16), calls=%async_computation.2 | async-start | bytes 2097152 | tf_op jit(solution)/shard_map/all_to_all | solution.py:233
  185.9 27.3 %all-to-all-done.2 = bf16[8,256,256]{1,2,0:T(8,128)(2,1)S(1)} async-done(((bf16[8,256,256]{1,2,0:T(8,128)(2,1)}), bf16[8,256,256]{1,2,0:T(8,128)(2,1)S(1)}, u32[]{:S(2)}, u32[]{:S(2)}) %all-to-all-start.2) | async-done | bytes 1048608 | tf_op jit(solution)/shard_map/all_to_all | solution.py:233
  214.6 3.7 %all-to-all-start.3 = ((bf16[8,256,256]{1,2,0:T(8,128)(2,1)}), bf16[8,256,256]{1,2,0:T(8,128)(2,1)S(1)}, u32[]{:S(2)}, u32[]{:S(2)}) async-start(bf16[8,256,256]{1,2,0:T(8,128)(2,1)} %broadcast_in_dim.56), calls=%async_computation.3 | async-start | bytes 2097152 | tf_op jit(solution)/shard_map/all_to_all | solution.py:53
  219.0 28.4 %all-to-all-done.3 = bf16[8,256,256]{1,2,0:T(8,128)(2,1)S(1)} async-done(((bf16[8,256,256]{1,2,0:T(8,128)(2,1)}), bf16[8,256,256]{1,2,0:T(8,128)(2,1)S(1)}, u32[]{:S(2)}, u32[]{:S(2)}) %all-to-all-start.3) | async-done | bytes 1048608 | tf_op jit(solution)/shard_map/all_to_all | solution.py:53
  248.8 2.9 %fusion.23 = bf16[256,768]{1,0:T(8,128)(2,1)S(1)} fusion(bf16[256,2048]{0,1:T(8,128)(2,1)S(1)} %fusion.9, bf16[2048,1792]{1,0:T(8,128)(2,1)} %all-gather.2.cloned.1.call-done, f32[768]{0:T(1024)S(1)} %add.204), kind=kOutput, calls=%fused_computation.29 | convolution fusion | flops 805699584 | bytes 4590592 | tf_op jit(solution)/shard_map/dot_general | solution.py:46
  (112 shorter events, 29.6 us)
Async XLA Ops:
  7.2 30.6 %copy-start = (bf16[48,2,32,256]{3,2,1,0:T(8,128)(2,1)S(1)}, bf16[48,2,32,256]{3,2,1,0:T(8,128)(2,1)}, u32[]{:S(2)}) copy-start(bf16[48,2,32,256]{3,2,1,0:T(8,128)(2,1)} %param.22) | copy-start | bytes 4718596
  7.2 135.5 %all-gather.2.cloned.1.call-start = ((), (), s32[]{:S(2)}) async-start(), calls=%async_computation.4 | async-start | bytes 7454720 | tf_op jit(solution)/shard_map/all_gather | solution.py:169
  40.6 5.9 %copy-start.2 = (bf16[256,256]{1,0:T(8,128)(2,1)S(1)}, bf16[256,256]{1,0:T(8,128)(2,1)}, u32[]{:S(2)}) copy-start(bf16[256,256]{1,0:T(8,128)(2,1)} %param.16) | copy-start | bytes 393220
  40.6 26.4 %copy-start.6 = (s32[256]{0:T(256)S(1)}, s32[256]{0:T(256)}, u32[]{:S(2)}) copy-start(s32[256]{0:T(256)} %param.29) | copy-start | bytes 3076
  40.6 27.1 %copy-start.5 = (s32[4]{0:T(128)S(1)}, s32[4]{0:T(128)}, u32[]{:S(2)}) copy-start(s32[4]{0:T(128)} %param.30) | copy-start | bytes 52
  40.6 32.0 %copy-start.11 = (f32[3,256]{1,0:T(4,128)S(1)}, f32[3,256]{1,0:T(4,128)}, u32[]{:S(2)}) copy-start(f32[3,256]{1,0:T(4,128)} %param.21) | copy-start | bytes 9220
  40.7 120.3 %all-to-all-start.1 = ((bf16[64,2,2,32,256]{4,3,2,1,0:T(8,128)(2,1)}), bf16[64,2,2,32,256]{4,3,2,1,0:T(8,128)(2,1)}, u32[]{:S(2)}, u32[]{:S(2)}) async-start(bf16[64,2,2,32,256]{4,3,2,1,0:T(8,128)(2,1)} %bitcast.104), calls=%async_computation.1 | async-start | bytes 8388608 | tf_op jit(solution)/shard_map/all_to_all | solution.py:206
  46.5 28.2 %collective-permute-start = (bf16[256,256]{1,0:T(8,128)(2,1)S(1)}, bf16[256,256]{1,0:T(8,128)(2,1)S(1)}, u32[]{:S(2)}, u32[]{:S(2)}) collective-permute-start(bf16[256,256]{1,0:T(8,128)(2,1)S(1)} %copy-done.2), channel_id=1, source_target_pairs={{0,1},{1,2},{2,3},{3,4},{4,5},{5,6},{6,7},{7,0},{8,9},{9,10},{10,1... | collective-permute-start | bytes 393224 | tf_op jit(solution)/shard_map/ppermute | solution.py:60
  49.7 30.7 %collective-permute-start.1 = (bf16[256,256]{1,0:T(8,128)(2,1)S(1)}, bf16[256,256]{1,0:T(8,128)(2,1)S(1)}, u32[]{:S(2)}, u32[]{:S(2)}) collective-permute-start(bf16[256,256]{1,0:T(8,128)(2,1)S(1)} %copy-done.2), channel_id=1, source_target_pairs={{0,2},{1,3},{2,4},{3,5},{4,6},{5,7},{6,0},{7,1},{8,10},{9,11},{10,... | collective-permute-start | bytes 393224 | tf_op jit(solution)/shard_map/ppermute | solution.py:60
  53.9 30.3 %collective-permute-start.2 = (bf16[256,256]{1,0:T(8,128)(2,1)S(1)}, bf16[256,256]{1,0:T(8,128)(2,1)S(1)}, u32[]{:S(2)}, u32[]{:S(2)}) collective-permute-start(bf16[256,256]{1,0:T(8,128)(2,1)S(1)} %copy-done.2), channel_id=1, source_target_pairs={{0,3},{1,4},{2,5},{3,6},{4,7},{5,0},{6,1},{7,2},{8,11},{9,12},{10,... | collective-permute-start | bytes 393224 | tf_op jit(solution)/shard_map/ppermute | solution.py:60
  58.6 26.3 %collective-permute-start.3 = (bf16[256,256]{1,0:T(8,128)(2,1)S(1)}, bf16[256,256]{1,0:T(8,128)(2,1)S(1)}, u32[]{:S(2)}, u32[]{:S(2)}) collective-permute-start(bf16[256,256]{1,0:T(8,128)(2,1)S(1)} %copy-done.2), channel_id=1, source_target_pairs={{0,4},{1,5},{2,6},{3,7},{4,0},{5,1},{6,2},{7,3},{8,12},{9,13},{10,... | collective-permute-start | bytes 393224 | tf_op jit(solution)/shard_map/ppermute | solution.py:60
  62.1 23.4 %collective-permute-start.4 = (bf16[256,256]{1,0:T(8,128)(2,1)S(1)}, bf16[256,256]{1,0:T(8,128)(2,1)S(1)}, u32[]{:S(2)}, u32[]{:S(2)}) collective-permute-start(bf16[256,256]{1,0:T(8,128)(2,1)S(1)} %copy-done.2), channel_id=1, source_target_pairs={{0,5},{1,6},{2,7},{3,0},{4,1},{5,2},{6,3},{7,4},{8,13},{9,14},{10,... | collective-permute-start | bytes 393224 | tf_op jit(solution)/shard_map/ppermute | solution.py:60
  68.4 6.3 %copy-start.4 = (s32[256]{0:T(256)}, s32[256]{0:T(256)S(1)}, u32[]{:S(2)}) copy-start(s32[256]{0:T(256)S(1)} %broadcast_subtract_fusion) | copy-start | bytes 3076
  74.7 11.4 %collective-permute-start.5 = (bf16[256,256]{1,0:T(8,128)(2,1)S(1)}, bf16[256,256]{1,0:T(8,128)(2,1)S(1)}, u32[]{:S(2)}, u32[]{:S(2)}) collective-permute-start(bf16[256,256]{1,0:T(8,128)(2,1)S(1)} %copy-done.2), channel_id=1, source_target_pairs={{0,6},{1,7},{2,0},{3,1},{4,2},{5,3},{6,4},{7,5},{8,14},{9,15},{10,... | collective-permute-start | bytes 393224 | tf_op jit(solution)/shard_map/ppermute | solution.py:60
  80.4 7.8 %collective-permute-start.6 = (bf16[256,256]{1,0:T(8,128)(2,1)S(1)}, bf16[256,256]{1,0:T(8,128)(2,1)S(1)}, u32[]{:S(2)}, u32[]{:S(2)}) collective-permute-start(bf16[256,256]{1,0:T(8,128)(2,1)S(1)} %copy-done.2), channel_id=1, source_target_pairs={{0,7},{1,0},{2,1},{3,2},{4,3},{5,4},{6,5},{7,6},{8,15},{9,8},{10,9... | collective-permute-start | bytes 393224 | tf_op jit(solution)/shard_map/ppermute | solution.py:60
  92.2 3.6 %copy-start.7 = (f32[2048]{0:T(1024)S(1)}, f32[2048]{0:T(1024)}, u32[]{:S(2)}) copy-start(f32[2048]{0:T(1024)} %param.19) | copy-start | bytes 24580
  92.2 3.6 %copy-start.8 = (f32[2048]{0:T(1024)S(1)}, f32[2048]{0:T(1024)}, u32[]{:S(2)}) copy-start(f32[2048]{0:T(1024)} %param.18) | copy-start | bytes 24580
  95.2 1.6 copy-start.1
  161.0 13.8 %slice-start = ((bf16[2048,1792]{1,0:T(8,128)(2,1)}), bf16[2048,256]{1,0:T(8,128)(2,1)S(1)}, s32[]{:S(2)}) async-start(bf16[2048,1792]{1,0:T(8,128)(2,1)} %all-gather.2.cloned.1.call-done), calls=%async_computation.5 | async-start | bytes 2097152 | tf_op jit(solution)/shard_map/slice | solution.py:174
  177.1 36.1 %all-to-all-start.2 = ((bf16[8,256,256]{1,2,0:T(8,128)(2,1)}), bf16[8,256,256]{1,2,0:T(8,128)(2,1)S(1)}, u32[]{:S(2)}, u32[]{:S(2)}) async-start(bf16[8,256,256]{1,2,0:T(8,128)(2,1)} %fusion.16), calls=%async_computation.2 | async-start | bytes 2097152 | tf_op jit(solution)/shard_map/all_to_all | solution.py:233
  213.4 4.9 %copy-start.12 = (f32[3,256]{1,0:T(4,128)S(1)}, f32[3,256]{1,0:T(4,128)}, u32[]{:S(2)}) copy-start(f32[3,256]{1,0:T(4,128)} %param.28) | copy-start | bytes 9220
  214.5 33.5 %copy-start.9 = (f32[2048]{0:T(1024)S(1)}, f32[2048]{0:T(1024)}, u32[]{:S(2)}) copy-start(f32[2048]{0:T(1024)} %param.26) | copy-start | bytes 24580
  214.6 33.5 %copy-start.10 = (f32[2048]{0:T(1024)S(1)}, f32[2048]{0:T(1024)}, u32[]{:S(2)}) copy-start(f32[2048]{0:T(1024)} %param.25) | copy-start | bytes 24580
  214.6 32.9 %all-to-all-start.3 = ((bf16[8,256,256]{1,2,0:T(8,128)(2,1)}), bf16[8,256,256]{1,2,0:T(8,128)(2,1)S(1)}, u32[]{:S(2)}, u32[]{:S(2)}) async-start(bf16[8,256,256]{1,2,0:T(8,128)(2,1)} %broadcast_in_dim.56), calls=%async_computation.3 | async-start | bytes 2097152 | tf_op jit(solution)/shard_map/all_to_all | solution.py:53
  (1 other events, 0.7 us)
Sparse Core Ops, SparseCore 0:
  11.9 130.7 all-gather.1

commit v9 on v7

--- a/solution.py
+++ b/solution.py
@@ -70,7 +70,7 @@
 
 
 def attention_body(q_ref, kc_ref, vc_ref, kn_ref, vn_ref, keyc_ref, keyn_ref, qreq_ref, out_ref):
-    chunk = pl.program_id(0)
+    chunk = pl.program_id(1)
     n_slots = kc_ref.shape[0] * kc_ref.shape[1] * kc_ref.shape[2]
     n_new = kn_ref.shape[0]
     score_scale = HEAD_DIM ** (-0.5)
@@ -81,57 +81,55 @@
     mask_n = (q_req == keyn_ref[...]) & (col_ids <= row_ids)
     lane = lax.broadcasted_iota(jnp.int32, (1, PAIR), 1)
     nt = (((1,), (1,)), ((), ()))
-    for pair in range(out_ref.shape[1] // PAIR):
-        cols = slice(pair * PAIR, (pair + 1) * PAIR)
-        q_pair = q_ref[:, cols]
-        k_pair = kc_ref[:, :, :, cols].reshape(n_slots, PAIR)
-        v_pair = vc_ref[:, :, :, cols].reshape(n_slots, PAIR)
-        kn_pair = kn_ref[:, cols]
-        vn_pair = vn_ref[:, cols]
-        halves = []
-        for half in range(PAIR // HEAD_DIM):
-            in_head = (lane >= half * HEAD_DIM) & (lane < (half + 1) * HEAD_DIM)
-            q_head = jnp.where(in_head, q_pair, jnp.zeros_like(q_pair))
-            s_c = lax.dot_general(q_head, k_pair, nt, preferred_element_type=jnp.float32)
-            s_n = lax.dot_general(q_head, kn_pair, nt, preferred_element_type=jnp.float32)
-            s_c = jnp.where(mask_c, s_c * score_scale, -1e30)
-            s_n = jnp.where(mask_n, s_n * score_scale, -1e30)
-            row_max = jnp.maximum(
-                jnp.max(s_c, axis=1, keepdims=True), jnp.max(s_n, axis=1, keepdims=True)
-            )
-            w_c = jnp.exp(s_c - row_max)
-            w_n = jnp.exp(s_n - row_max)
-            total = jnp.sum(w_c, axis=1, keepdims=True) + jnp.sum(w_n, axis=1, keepdims=True)
-            p_c = (w_c / total).astype(jnp.bfloat16)
-            p_n = (w_n / total).astype(jnp.bfloat16)
-            o = jnp.dot(p_c, v_pair, preferred_element_type=jnp.float32) + jnp.dot(
-                p_n, vn_pair, preferred_element_type=jnp.float32
-            )
-            halves.append((in_head, o))
-        merged = jnp.where(halves[0][0], halves[0][1], halves[1][1])
-        out_ref[:, cols] = merged.astype(out_ref.dtype)
+    q_pair = q_ref[...]
+    k_pair = kc_ref[...].reshape(n_slots, PAIR)
+    v_pair = vc_ref[...].reshape(n_slots, PAIR)
+    kn_pair = kn_ref[...]
+    vn_pair = vn_ref[...]
+    halves = []
+    for half in range(PAIR // HEAD_DIM):
+        in_head = (lane >= half * HEAD_DIM) & (lane < (half + 1) * HEAD_DIM)
+        q_head = jnp.where(in_head, q_pair, jnp.zeros_like(q_pair))
+        s_c = lax.dot_general(q_head, k_pair, nt, preferred_element_type=jnp.float32)
+        s_n = lax.dot_general(q_head, kn_pair, nt, preferred_element_type=jnp.float32)
+        s_c = jnp.where(mask_c, s_c * score_scale, -1e30)
+        s_n = jnp.where(mask_n, s_n * score_scale, -1e30)
+        row_max = jnp.maximum(
+            jnp.max(s_c, axis=1, keepdims=True), jnp.max(s_n, axis=1, keepdims=True)
+        )
+        w_c = jnp.exp(s_c - row_max)
+        w_n = jnp.exp(s_n - row_max)
+        total = jnp.sum(w_c, axis=1, keepdims=True) + jnp.sum(w_n, axis=1, keepdims=True)
+        p_c = (w_c / total).astype(jnp.bfloat16)
+        p_n = (w_n / total).astype(jnp.bfloat16)
+        o = jnp.dot(p_c, v_pair, preferred_element_type=jnp.float32) + jnp.dot(
+            p_n, vn_pair, preferred_element_type=jnp.float32
+        )
+        halves.append((in_head, o))
+    merged = jnp.where(halves[0][0], halves[0][1], halves[1][1])
+    out_ref[...] = merged.astype(out_ref.dtype)
 
 
 def attention_call(query, arrived, key_new, value_new, key_req_c, key_req_n, q_req):
     tok, width = query.shape
     holders, per, _, blk, _ = arrived.shape
     n_slots = holders * per * blk
-    grid = (tok // Q_CHUNK,)
-    full = lambda c: (0, 0)
+    grid = (width // PAIR, tok // Q_CHUNK)
+    full = lambda p, c: (0, 0)
     return pl.pallas_call(
         attention_body,
         grid=grid,
         in_specs=[
-            pl.BlockSpec((Q_CHUNK, width), lambda c: (c, 0)),
-            pl.BlockSpec((holders, per, None, blk, width), lambda c: (0, 0, 0, 0, 0)),
-            pl.BlockSpec((holders, per, None, blk, width), lambda c: (0, 0, 1, 0, 0)),
-            pl.BlockSpec((tok, width), full),
-            pl.BlockSpec((tok, width), full),
+            pl.BlockSpec((Q_CHUNK, PAIR), lambda p, c: (c, p)),
+            pl.BlockSpec((holders, per, None, blk, PAIR), lambda p, c: (0, 0, 0, 0, p)),
+            pl.BlockSpec((holders, per, None, blk, PAIR), lambda p, c: (0, 0, 1, 0, p)),
+            pl.BlockSpec((tok, PAIR), lambda p, c: (0, p)),
+            pl.BlockSpec((tok, PAIR), lambda p, c: (0, p)),
             pl.BlockSpec((1, n_slots), full),
             pl.BlockSpec((1, tok), full),
-            pl.BlockSpec((Q_CHUNK, 1), lambda c: (c, 0)),
+            pl.BlockSpec((Q_CHUNK, 1), lambda p, c: (c, 0)),
         ],
-        out_specs=pl.BlockSpec((Q_CHUNK, width), lambda c: (c, 0)),
+        out_specs=pl.BlockSpec((Q_CHUNK, PAIR), lambda p, c: (c, p)),
         out_shape=jax.ShapeDtypeStruct((tok, width), jnp.bfloat16),
     )(query, arrived, arrived, key_new, value_new, key_req_c, key_req_n, q_req)
 

time: 262 us -> 262 us (level)
  transfers between devices with their start and end apart: 11 -> 11, of which waited for: 5 -> 5; matrix products, arithmetic and copies ran while one was open for 12% -> 13% of each run, Pallas kernels for 0% -> 0%
where the time goes in v9:
time: 262 us; the launch traced here: 261 us
  waiting for transfers between devices  117 us (45%)
  starting transfers between devices  44.8 us (17%)
  local copies, waits for them, and re-layouts  26.6 us (10%)
  blocking collectives  23.9 us (9%)
  between operations  14.4 us (5%)
  other arithmetic  13.3 us (5%)
  Pallas kernels  13.3 us (5%)
  matrix products  7.57 us (3%)
    all_gather x1, waiting for transfers between devices, local(): gathered = lax.all_gather(joined, 'pool', axis=0, tiled=True)  45.4 us
    all_to_all x1, waiting for transfers between devices, mp_gather(): lax.all_to_all(spread, 'mp', split_axis=0, concat_axis=2, tiled=True)  29.1 us
    all_to_all x1, waiting for transfers between devices, local(): lax.all_to_all(pieces, 'mp', split_axis=1, concat_axis=1, tiled=True)  28.5 us
    ppermute x7, starting transfers between devices, mp_permute_gather(): lax.ppermute(block, 'mp', [(src, (src + shift) % mp_count) for src in ran...  28.4 us
    all_to_all x1, blocking collectives, local(): lax.all_to_all(slot_ids, 'pool', split_axis=0, concat_axis=0, tiled=True)  23.9 us
    pallas_call x1, Pallas kernels, attention_call(): pl.pallas_call(attention_body, grid=grid, in_specs=[pl.BlockSpec((Q_CHUNK...  13.3 us
    all_to_all x1, waiting for transfers between devices, local(): lax.all_to_all(packed, 'pool', split_axis=0, concat_axis=0, tiled=True)  12 us
    unnamed x37, local copies, waits for them, and re-layouts  7.58 us
  transfers between devices with their start and end apart: 11, of which 5 were waited for; matrix products, arithmetic and copies ran while one was open for 13% of the time, Pallas kernels for 0%

profile of v9, /device:TPU:1, one launch (start us, length us, event | category | flops | bytes accessed | tf_op | source)
XLA Modules:
  0.0 260.6 jit_solution(1582588318438578487)
XLA Ops:
  12.4 23.9 %all_to_all.28 = s32[64,1,2]{2,1,0:T(1,128)S(1)} all-to-all(s32[64,1,2]{2,1,0:T(1,128)S(1)} %bitcast.117), channel_id=1, replica_groups=mesh['pool'=64,'mp'=8] {'pool'}, dimensions={0} | all-to-all | bytes 1024 | tf_op jit(solution)/shard_map/all_to_all | solution.py:202
  37.8 2.9 %gather_fusion.1 = bf16[128,2,32,256]{3,2,1,0:T(8,128)(2,1)} fusion(bf16[48,2,32,256]{3,2,1,0:T(8,128)(2,1)S(1)} %copy-done, s32[1024]{0:T(1024)S(1)} %pad_clamp_fusion), kind=kCustom, calls=%fused_computation.1 | custom fusion | bytes 8389120 | tf_op jit(solution)/shard_map/gather | solution.py:203
  40.7 5.8 %all-to-all-start.1 = ((bf16[64,2,2,32,256]{4,3,2,1,0:T(8,128)(2,1)}), bf16[64,2,2,32,256]{4,3,2,1,0:T(8,128)(2,1)}, u32[]{:S(2)}, u32[]{:S(2)}) async-start(bf16[64,2,2,32,256]{4,3,2,1,0:T(8,128)(2,1)} %bitcast.102), calls=%async_computation.1 | async-start | bytes 8388608 | tf_op jit(solution)/shard_map/all_to_all | solution.py:204
  46.5 3.2 %collective-permute-start = (bf16[256,256]{1,0:T(8,128)(2,1)S(1)}, bf16[256,256]{1,0:T(8,128)(2,1)S(1)}, u32[]{:S(2)}, u32[]{:S(2)}) collective-permute-start(bf16[256,256]{1,0:T(8,128)(2,1)S(1)} %copy-done.2), channel_id=1, source_target_pairs={{0,1},{1,2},{2,3},{3,4},{4,5},{5,6},{6,7},{7,0},{8,9},{9,10},{10,1... | collective-permute-start | bytes 393224 | tf_op jit(solution)/shard_map/ppermute | solution.py:60
  49.7 4.2 %collective-permute-start.1 = (bf16[256,256]{1,0:T(8,128)(2,1)S(1)}, bf16[256,256]{1,0:T(8,128)(2,1)S(1)}, u32[]{:S(2)}, u32[]{:S(2)}) collective-permute-start(bf16[256,256]{1,0:T(8,128)(2,1)S(1)} %copy-done.2), channel_id=1, source_target_pairs={{0,2},{1,3},{2,4},{3,5},{4,6},{5,7},{6,0},{7,1},{8,10},{9,11},{10,... | collective-permute-start | bytes 393224 | tf_op jit(solution)/shard_map/ppermute | solution.py:60
  53.9 4.6 %collective-permute-start.2 = (bf16[256,256]{1,0:T(8,128)(2,1)S(1)}, bf16[256,256]{1,0:T(8,128)(2,1)S(1)}, u32[]{:S(2)}, u32[]{:S(2)}) collective-permute-start(bf16[256,256]{1,0:T(8,128)(2,1)S(1)} %copy-done.2), channel_id=1, source_target_pairs={{0,3},{1,4},{2,5},{3,6},{4,7},{5,0},{6,1},{7,2},{8,11},{9,12},{10,... | collective-permute-start | bytes 393224 | tf_op jit(solution)/shard_map/ppermute | solution.py:60
  58.6 3.5 %collective-permute-start.3 = (bf16[256,256]{1,0:T(8,128)(2,1)S(1)}, bf16[256,256]{1,0:T(8,128)(2,1)S(1)}, u32[]{:S(2)}, u32[]{:S(2)}) collective-permute-start(bf16[256,256]{1,0:T(8,128)(2,1)S(1)} %copy-done.2), channel_id=1, source_target_pairs={{0,4},{1,5},{2,6},{3,7},{4,0},{5,1},{6,2},{7,3},{8,12},{9,13},{10,... | collective-permute-start | bytes 393224 | tf_op jit(solution)/shard_map/ppermute | solution.py:60
  62.1 4.9 %collective-permute-start.4 = (bf16[256,256]{1,0:T(8,128)(2,1)S(1)}, bf16[256,256]{1,0:T(8,128)(2,1)S(1)}, u32[]{:S(2)}, u32[]{:S(2)}) collective-permute-start(bf16[256,256]{1,0:T(8,128)(2,1)S(1)} %copy-done.2), channel_id=1, source_target_pairs={{0,5},{1,6},{2,7},{3,0},{4,1},{5,2},{6,3},{7,4},{8,13},{9,14},{10,... | collective-permute-start | bytes 393224 | tf_op jit(solution)/shard_map/ppermute | solution.py:60
  68.4 2.5 fusion.31
  74.6 5.0 %collective-permute-start.5 = (bf16[256,256]{1,0:T(8,128)(2,1)S(1)}, bf16[256,256]{1,0:T(8,128)(2,1)S(1)}, u32[]{:S(2)}, u32[]{:S(2)}) collective-permute-start(bf16[256,256]{1,0:T(8,128)(2,1)S(1)} %copy-done.2), channel_id=1, source_target_pairs={{0,6},{1,7},{2,0},{3,1},{4,2},{5,3},{6,4},{7,5},{8,14},{9,15},{10,... | collective-permute-start | bytes 393224 | tf_op jit(solution)/shard_map/ppermute | solution.py:60
  80.3 3.0 %collective-permute-start.6 = (bf16[256,256]{1,0:T(8,128)(2,1)S(1)}, bf16[256,256]{1,0:T(8,128)(2,1)S(1)}, u32[]{:S(2)}, u32[]{:S(2)}) collective-permute-start(bf16[256,256]{1,0:T(8,128)(2,1)S(1)} %copy-done.2), channel_id=1, source_target_pairs={{0,7},{1,0},{2,1},{3,2},{4,3},{5,4},{6,5},{7,6},{8,15},{9,8},{10,9... | collective-permute-start | bytes 393224 | tf_op jit(solution)/shard_map/ppermute | solution.py:60
  86.5 1.6 collective-permute-done.6
  88.8 1.9 gather_fusion
  92.2 3.0 %copy.53 = f32[256,8,256]{0,2,1:T(8,128)} copy(f32[256,8,256]{2,0,1:T(8,128)} %convert_bitcast_fusion) | data formatting | bytes 4194304 | tf_op jit(solution)/shard_map/convert_element_type | solution.py:16
  97.6 45.4 %all-gather.2.cloned.1.call-done = bf16[2048,1792]{1,0:T(8,128)(2,1)} async-done(((bf16[32,1792]{1,0:T(8,128)(2,1)}), bf16[2048,1792]{1,0:T(8,128)(2,1)}) %all-gather.2.cloned.1.call-update) | async-done | bytes 7340048 | tf_op jit(solution)/shard_map/all_gather | solution.py:167
  143.0 2.9 %fusion.16 = f32[256,768]{1,0:T(8,128)S(1)} fusion(bf16[256,2048]{0,1:T(8,128)(2,1)S(1)} %fusion.15, bf16[2048,1792]{1,0:T(8,128)(2,1)} %all-gather.2.cloned.1.call-done, f32[768]{0:T(1024)} %add.184), kind=kOutput, calls=%fused_computation.26 | convolution fusion | flops 805502976 | bytes 4984832 | tf_op jit(solution)/shard_map/dot_general | solution.py:46
  149.0 12.0 %all-to-all-done.1.kc_ref.vc_ref = bf16[64,2,2,32,256]{4,3,2,1,0:T(8,128)(2,1)} async-done(((bf16[64,2,2,32,256]{4,3,2,1,0:T(8,128)(2,1)}), bf16[64,2,2,32,256]{4,3,2,1,0:T(8,128)(2,1)}, u32[]{:S(2)}, u32[]{:S(2)}) %all-to-all-start.1) | async-done | bytes 4194336 | tf_op jit(solution)/shard_map/all_to_all | solution.py:204
  161.0 13.3 %shard_map.167 = bf16[256,256]{1,0:T(8,128)(2,1)} custom-call(bf16[256,256]{1,0:T(8,128)(2,1)} %copy.59.q_ref, bf16[64,2,2,32,256]{4,3,2,1,0:T(8,128)(2,1)} %all-to-all-done.1.kc_ref.vc_ref, bf16[64,2,2,32,256]{4,3,2,1,0:T(8,128)(2,1)} %all-to-all-done.1.kc_ref.vc_ref, bf16[256,256]{1,0:T(8,128)(2,1)} %copy.60.kn_ref, bf16[256,256]{1,0:T(8,128)(2,1)} %bitcast.112, ...), custom_call_target="tpu_custom_call" | custom-call | tf_op jit(solution)/shard_map/pallas_call | solution.py:119
  174.3 1.8 convolution_convert_fusion
  177.1 6.8 %all-to-all-start.2 = ((bf16[256,8,256]{2,0,1:T(8,128)(2,1)}), bf16[256,8,256]{2,0,1:T(8,128)(2,1)S(1)}, u32[]{:S(2)}, u32[]{:S(2)}) async-start(bf16[256,8,256]{2,0,1:T(8,128)(2,1)} %bitcast.103), calls=%async_computation.2 | async-start | bytes 2097152 | tf_op jit(solution)/shard_map/all_to_all | solution.py:228
  184.7 28.5 %all-to-all-done.2 = bf16[256,8,256]{2,0,1:T(8,128)(2,1)S(1)} async-done(((bf16[256,8,256]{2,0,1:T(8,128)(2,1)}), bf16[256,8,256]{2,0,1:T(8,128)(2,1)S(1)}, u32[]{:S(2)}, u32[]{:S(2)}) %all-to-all-start.2) | async-done | bytes 1048608 | tf_op jit(solution)/shard_map/all_to_all | solution.py:228
  215.5 3.7 %all-to-all-start.3 = ((bf16[8,256,256]{1,2,0:T(8,128)(2,1)}), bf16[8,256,256]{1,2,0:T(8,128)(2,1)S(1)}, u32[]{:S(2)}, u32[]{:S(2)}) async-start(bf16[8,256,256]{1,2,0:T(8,128)(2,1)} %broadcast_in_dim.56), calls=%async_computation.3 | async-start | bytes 2097152 | tf_op jit(solution)/shard_map/all_to_all | solution.py:53
  219.2 29.1 %all-to-all-done.3 = bf16[8,256,256]{1,2,0:T(8,128)(2,1)S(1)} async-done(((bf16[8,256,256]{1,2,0:T(8,128)(2,1)}), bf16[8,256,256]{1,2,0:T(8,128)(2,1)S(1)}, u32[]{:S(2)}, u32[]{:S(2)}) %all-to-all-start.3) | async-done | bytes 1048608 | tf_op jit(solution)/shard_map/all_to_all | solution.py:53
  249.8 2.9 %fusion.22 = bf16[256,768]{1,0:T(8,128)(2,1)S(1)} fusion(bf16[256,2048]{0,1:T(8,128)(2,1)S(1)} %fusion.9, bf16[2048,1792]{1,0:T(8,128)(2,1)} %all-gather.2.cloned.1.call-done, f32[768]{0:T(1024)S(1)} %add.204), kind=kOutput, calls=%fused_computation.28 | convolution fusion | flops 805699584 | bytes 4590592 | tf_op jit(solution)/shard_map/dot_general | solution.py:46
  (110 shorter events, 29.8 us)
Async XLA Ops:
  7.2 30.6 %copy-start = (bf16[48,2,32,256]{3,2,1,0:T(8,128)(2,1)S(1)}, bf16[48,2,32,256]{3,2,1,0:T(8,128)(2,1)}, u32[]{:S(2)}) copy-start(bf16[48,2,32,256]{3,2,1,0:T(8,128)(2,1)} %param.22) | copy-start | bytes 4718596
  7.2 135.9 %all-gather.2.cloned.1.call-start = ((), (), s32[]{:S(2)}) async-start(), calls=%async_computation.4 | async-start | bytes 7454720 | tf_op jit(solution)/shard_map/all_gather | solution.py:167
  40.6 5.9 %copy-start.2 = (bf16[256,256]{1,0:T(8,128)(2,1)S(1)}, bf16[256,256]{1,0:T(8,128)(2,1)}, u32[]{:S(2)}) copy-start(bf16[256,256]{1,0:T(8,128)(2,1)} %param.16) | copy-start | bytes 393220
  40.6 26.4 %copy-start.7 = (s32[256]{0:T(256)S(1)}, s32[256]{0:T(256)}, u32[]{:S(2)}) copy-start(s32[256]{0:T(256)} %param.29) | copy-start | bytes 3076
  40.6 27.1 %copy-start.6 = (s32[4]{0:T(128)S(1)}, s32[4]{0:T(128)}, u32[]{:S(2)}) copy-start(s32[4]{0:T(128)} %param.30) | copy-start | bytes 52
  40.6 31.9 %copy-start.12 = (f32[3,256]{1,0:T(4,128)S(1)}, f32[3,256]{1,0:T(4,128)}, u32[]{:S(2)}) copy-start(f32[3,256]{1,0:T(4,128)} %param.21) | copy-start | bytes 9220
  40.7 120.3 %all-to-all-start.1 = ((bf16[64,2,2,32,256]{4,3,2,1,0:T(8,128)(2,1)}), bf16[64,2,2,32,256]{4,3,2,1,0:T(8,128)(2,1)}, u32[]{:S(2)}, u32[]{:S(2)}) async-start(bf16[64,2,2,32,256]{4,3,2,1,0:T(8,128)(2,1)} %bitcast.102), calls=%async_computation.1 | async-start | bytes 8388608 | tf_op jit(solution)/shard_map/all_to_all | solution.py:204
  46.5 28.1 %collective-permute-start = (bf16[256,256]{1,0:T(8,128)(2,1)S(1)}, bf16[256,256]{1,0:T(8,128)(2,1)S(1)}, u32[]{:S(2)}, u32[]{:S(2)}) collective-permute-start(bf16[256,256]{1,0:T(8,128)(2,1)S(1)} %copy-done.2), channel_id=1, source_target_pairs={{0,1},{1,2},{2,3},{3,4},{4,5},{5,6},{6,7},{7,0},{8,9},{9,10},{10,1... | collective-permute-start | bytes 393224 | tf_op jit(solution)/shard_map/ppermute | solution.py:60
  49.7 30.6 %collective-permute-start.1 = (bf16[256,256]{1,0:T(8,128)(2,1)S(1)}, bf16[256,256]{1,0:T(8,128)(2,1)S(1)}, u32[]{:S(2)}, u32[]{:S(2)}) collective-permute-start(bf16[256,256]{1,0:T(8,128)(2,1)S(1)} %copy-done.2), channel_id=1, source_target_pairs={{0,2},{1,3},{2,4},{3,5},{4,6},{5,7},{6,0},{7,1},{8,10},{9,11},{10,... | collective-permute-start | bytes 393224 | tf_op jit(solution)/shard_map/ppermute | solution.py:60
  53.9 30.0 %collective-permute-start.2 = (bf16[256,256]{1,0:T(8,128)(2,1)S(1)}, bf16[256,256]{1,0:T(8,128)(2,1)S(1)}, u32[]{:S(2)}, u32[]{:S(2)}) collective-permute-start(bf16[256,256]{1,0:T(8,128)(2,1)S(1)} %copy-done.2), channel_id=1, source_target_pairs={{0,3},{1,4},{2,5},{3,6},{4,7},{5,0},{6,1},{7,2},{8,11},{9,12},{10,... | collective-permute-start | bytes 393224 | tf_op jit(solution)/shard_map/ppermute | solution.py:60
  58.6 26.0 %collective-permute-start.3 = (bf16[256,256]{1,0:T(8,128)(2,1)S(1)}, bf16[256,256]{1,0:T(8,128)(2,1)S(1)}, u32[]{:S(2)}, u32[]{:S(2)}) collective-permute-start(bf16[256,256]{1,0:T(8,128)(2,1)S(1)} %copy-done.2), channel_id=1, source_target_pairs={{0,4},{1,5},{2,6},{3,7},{4,0},{5,1},{6,2},{7,3},{8,12},{9,13},{10,... | collective-permute-start | bytes 393224 | tf_op jit(solution)/shard_map/ppermute | solution.py:60
  62.1 23.1 %collective-permute-start.4 = (bf16[256,256]{1,0:T(8,128)(2,1)S(1)}, bf16[256,256]{1,0:T(8,128)(2,1)S(1)}, u32[]{:S(2)}, u32[]{:S(2)}) collective-permute-start(bf16[256,256]{1,0:T(8,128)(2,1)S(1)} %copy-done.2), channel_id=1, source_target_pairs={{0,5},{1,6},{2,7},{3,0},{4,1},{5,2},{6,3},{7,4},{8,13},{9,14},{10,... | collective-permute-start | bytes 393224 | tf_op jit(solution)/shard_map/ppermute | solution.py:60
  68.3 6.3 %copy-start.5 = (s32[256]{0:T(256)}, s32[256]{0:T(256)S(1)}, u32[]{:S(2)}) copy-start(s32[256]{0:T(256)S(1)} %broadcast_subtract_fusion) | copy-start | bytes 3076
  74.6 11.3 %collective-permute-start.5 = (bf16[256,256]{1,0:T(8,128)(2,1)S(1)}, bf16[256,256]{1,0:T(8,128)(2,1)S(1)}, u32[]{:S(2)}, u32[]{:S(2)}) collective-permute-start(bf16[256,256]{1,0:T(8,128)(2,1)S(1)} %copy-done.2), channel_id=1, source_target_pairs={{0,6},{1,7},{2,0},{3,1},{4,2},{5,3},{6,4},{7,5},{8,14},{9,15},{10,... | collective-permute-start | bytes 393224 | tf_op jit(solution)/shard_map/ppermute | solution.py:60
  80.3 7.8 %collective-permute-start.6 = (bf16[256,256]{1,0:T(8,128)(2,1)S(1)}, bf16[256,256]{1,0:T(8,128)(2,1)S(1)}, u32[]{:S(2)}, u32[]{:S(2)}) collective-permute-start(bf16[256,256]{1,0:T(8,128)(2,1)S(1)} %copy-done.2), channel_id=1, source_target_pairs={{0,7},{1,0},{2,1},{3,2},{4,3},{5,4},{6,5},{7,6},{8,15},{9,8},{10,9... | collective-permute-start | bytes 393224 | tf_op jit(solution)/shard_map/ppermute | solution.py:60
  92.2 3.6 %copy-start.8 = (f32[2048]{0:T(1024)S(1)}, f32[2048]{0:T(1024)}, u32[]{:S(2)}) copy-start(f32[2048]{0:T(1024)} %param.19) | copy-start | bytes 24580
  92.2 3.7 %copy-start.9 = (f32[2048]{0:T(1024)S(1)}, f32[2048]{0:T(1024)}, u32[]{:S(2)}) copy-start(f32[2048]{0:T(1024)} %param.18) | copy-start | bytes 24580
  95.2 1.6 copy-start.1
  177.1 36.1 %all-to-all-start.2 = ((bf16[256,8,256]{2,0,1:T(8,128)(2,1)}), bf16[256,8,256]{2,0,1:T(8,128)(2,1)S(1)}, u32[]{:S(2)}, u32[]{:S(2)}) async-start(bf16[256,8,256]{2,0,1:T(8,128)(2,1)} %bitcast.103), calls=%async_computation.2 | async-start | bytes 2097152 | tf_op jit(solution)/shard_map/all_to_all | solution.py:228
  213.4 5.9 %copy-start.13 = (f32[3,256]{1,0:T(4,128)S(1)}, f32[3,256]{1,0:T(4,128)}, u32[]{:S(2)}) copy-start(f32[3,256]{1,0:T(4,128)} %param.28) | copy-start | bytes 9220
  214.3 34.3 %copy-start.3 = (bf16[256,256]{1,0:T(8,128)(2,1)}, bf16[256,256]{1,0:T(8,128)(2,1)S(1)}, u32[]{:S(2)}) copy-start(bf16[256,256]{1,0:T(8,128)(2,1)S(1)} %add_convert_fusion) | copy-start | bytes 393220
  215.5 33.5 %copy-start.10 = (f32[2048]{0:T(1024)S(1)}, f32[2048]{0:T(1024)}, u32[]{:S(2)}) copy-start(f32[2048]{0:T(1024)} %param.26) | copy-start | bytes 24580
  215.5 33.5 %copy-start.11 = (f32[2048]{0:T(1024)S(1)}, f32[2048]{0:T(1024)}, u32[]{:S(2)}) copy-start(f32[2048]{0:T(1024)} %param.25) | copy-start | bytes 24580
  215.5 32.9 %all-to-all-start.3 = ((bf16[8,256,256]{1,2,0:T(8,128)(2,1)}), bf16[8,256,256]{1,2,0:T(8,128)(2,1)S(1)}, u32[]{:S(2)}, u32[]{:S(2)}) async-start(bf16[8,256,256]{1,2,0:T(8,128)(2,1)} %broadcast_in_dim.56), calls=%async_computation.3 | async-start | bytes 2097152 | tf_op jit(solution)/shard_map/all_to_all | solution.py:53
  (1 other events, 0.7 us)
Sparse Core Ops, SparseCore 0:
  11.9 131.0 all-gather.1

commit v10 on v9

--- a/solution.py
+++ b/solution.py
@@ -89,19 +89,20 @@
     halves = []
     for half in range(PAIR // HEAD_DIM):
         in_head = (lane >= half * HEAD_DIM) & (lane < (half + 1) * HEAD_DIM)
-        q_head = jnp.where(in_head, q_pair, jnp.zeros_like(q_pair))
+        q_head = jnp.where(in_head, q_pair * jnp.asarray(score_scale, q_pair.dtype), jnp.zeros_like(q_pair))
         s_c = lax.dot_general(q_head, k_pair, nt, preferred_element_type=jnp.float32)
         s_n = lax.dot_general(q_head, kn_pair, nt, preferred_element_type=jnp.float32)
-        s_c = jnp.where(mask_c, s_c * score_scale, -1e30)
-        s_n = jnp.where(mask_n, s_n * score_scale, -1e30)
+        s_c = jnp.where(mask_c, s_c, -1e30)
+        s_n = jnp.where(mask_n, s_n, -1e30)
         row_max = jnp.maximum(
             jnp.max(s_c, axis=1, keepdims=True), jnp.max(s_n, axis=1, keepdims=True)
         )
         w_c = jnp.exp(s_c - row_max)
         w_n = jnp.exp(s_n - row_max)
         total = jnp.sum(w_c, axis=1, keepdims=True) + jnp.sum(w_n, axis=1, keepdims=True)
-        p_c = (w_c / total).astype(jnp.bfloat16)
-        p_n = (w_n / total).astype(jnp.bfloat16)
+        inv_total = 1.0 / total
+        p_c = (w_c * inv_total).astype(jnp.bfloat16)
+        p_n = (w_n * inv_total).astype(jnp.bfloat16)
         o = jnp.dot(p_c, v_pair, preferred_element_type=jnp.float32) + jnp.dot(
             p_n, vn_pair, preferred_element_type=jnp.float32
         )

time: 262 us -> 262 us (level)
  no operation moved by 1% of the time
where the time goes in v10:
time: 262 us; the launch traced here: 261 us
  waiting for transfers between devices  117 us (45%)
  starting transfers between devices  44.8 us (17%)
  local copies, waits for them, and re-layouts  26.6 us (10%)
  blocking collectives  23.9 us (9%)
  between operations  14.4 us (5%)
  Pallas kernels  13.4 us (5%)
  other arithmetic  13.3 us (5%)
  matrix products  7.58 us (3%)
    all_gather x1, waiting for transfers between devices, local(): gathered = lax.all_gather(joined, 'pool', axis=0, tiled=True)  45.4 us
    all_to_all x1, waiting for transfers between devices, mp_gather(): lax.all_to_all(spread, 'mp', split_axis=0, concat_axis=2, tiled=True)  29.1 us
    all_to_all x1, waiting for transfers between devices, local(): lax.all_to_all(pieces, 'mp', split_axis=1, concat_axis=1, tiled=True)  28.5 us
    ppermute x7, starting transfers between devices, mp_permute_gather(): lax.ppermute(block, 'mp', [(src, (src + shift) % mp_count) for src in ran...  28.4 us
    all_to_all x1, blocking collectives, local(): lax.all_to_all(slot_ids, 'pool', split_axis=0, concat_axis=0, tiled=True)  23.9 us
    pallas_call x1, Pallas kernels, attention_call(): pl.pallas_call(attention_body, grid=grid, in_specs=[pl.BlockSpec((Q_CHUNK...  13.4 us
    all_to_all x1, waiting for transfers between devices, local(): lax.all_to_all(packed, 'pool', split_axis=0, concat_axis=0, tiled=True)  12 us
    unnamed x37, local copies, waits for them, and re-layouts  7.58 us
  transfers between devices with their start and end apart: 11, of which 5 were waited for; matrix products, arithmetic and copies ran while one was open for 13% of the time, Pallas kernels for 0%

profile of v10, /device:TPU:1, one launch (start us, length us, event | category | flops | bytes accessed | tf_op | source)
XLA Modules:
  0.0 260.7 jit_solution(14107612475308546074)
XLA Ops:
  12.4 23.9 %all_to_all.28 = s32[64,1,2]{2,1,0:T(1,128)S(1)} all-to-all(s32[64,1,2]{2,1,0:T(1,128)S(1)} %bitcast.117), channel_id=1, replica_groups=mesh['pool'=64,'mp'=8] {'pool'}, dimensions={0} | all-to-all | bytes 1024 | tf_op jit(solution)/shard_map/all_to_all | solution.py:203
  37.8 2.9 %gather_fusion.1 = bf16[128,2,32,256]{3,2,1,0:T(8,128)(2,1)} fusion(bf16[48,2,32,256]{3,2,1,0:T(8,128)(2,1)S(1)} %copy-done, s32[1024]{0:T(1024)S(1)} %pad_clamp_fusion), kind=kCustom, calls=%fused_computation.1 | custom fusion | bytes 8389120 | tf_op jit(solution)/shard_map/gather | solution.py:204
  40.7 5.8 %all-to-all-start.1 = ((bf16[64,2,2,32,256]{4,3,2,1,0:T(8,128)(2,1)}), bf16[64,2,2,32,256]{4,3,2,1,0:T(8,128)(2,1)}, u32[]{:S(2)}, u32[]{:S(2)}) async-start(bf16[64,2,2,32,256]{4,3,2,1,0:T(8,128)(2,1)} %bitcast.102), calls=%async_computation.1 | async-start | bytes 8388608 | tf_op jit(solution)/shard_map/all_to_all | solution.py:205
  46.5 3.2 %collective-permute-start = (bf16[256,256]{1,0:T(8,128)(2,1)S(1)}, bf16[256,256]{1,0:T(8,128)(2,1)S(1)}, u32[]{:S(2)}, u32[]{:S(2)}) collective-permute-start(bf16[256,256]{1,0:T(8,128)(2,1)S(1)} %copy-done.2), channel_id=1, source_target_pairs={{0,1},{1,2},{2,3},{3,4},{4,5},{5,6},{6,7},{7,0},{8,9},{9,10},{10,1... | collective-permute-start | bytes 393224 | tf_op jit(solution)/shard_map/ppermute | solution.py:60
  49.7 4.2 %collective-permute-start.1 = (bf16[256,256]{1,0:T(8,128)(2,1)S(1)}, bf16[256,256]{1,0:T(8,128)(2,1)S(1)}, u32[]{:S(2)}, u32[]{:S(2)}) collective-permute-start(bf16[256,256]{1,0:T(8,128)(2,1)S(1)} %copy-done.2), channel_id=1, source_target_pairs={{0,2},{1,3},{2,4},{3,5},{4,6},{5,7},{6,0},{7,1},{8,10},{9,11},{10,... | collective-permute-start | bytes 393224 | tf_op jit(solution)/shard_map/ppermute | solution.py:60
  53.9 4.6 %collective-permute-start.2 = (bf16[256,256]{1,0:T(8,128)(2,1)S(1)}, bf16[256,256]{1,0:T(8,128)(2,1)S(1)}, u32[]{:S(2)}, u32[]{:S(2)}) collective-permute-start(bf16[256,256]{1,0:T(8,128)(2,1)S(1)} %copy-done.2), channel_id=1, source_target_pairs={{0,3},{1,4},{2,5},{3,6},{4,7},{5,0},{6,1},{7,2},{8,11},{9,12},{10,... | collective-permute-start | bytes 393224 | tf_op jit(solution)/shard_map/ppermute | solution.py:60
  58.6 3.5 %collective-permute-start.3 = (bf16[256,256]{1,0:T(8,128)(2,1)S(1)}, bf16[256,256]{1,0:T(8,128)(2,1)S(1)}, u32[]{:S(2)}, u32[]{:S(2)}) collective-permute-start(bf16[256,256]{1,0:T(8,128)(2,1)S(1)} %copy-done.2), channel_id=1, source_target_pairs={{0,4},{1,5},{2,6},{3,7},{4,0},{5,1},{6,2},{7,3},{8,12},{9,13},{10,... | collective-permute-start | bytes 393224 | tf_op jit(solution)/shard_map/ppermute | solution.py:60
  62.1 4.9 %collective-permute-start.4 = (bf16[256,256]{1,0:T(8,128)(2,1)S(1)}, bf16[256,256]{1,0:T(8,128)(2,1)S(1)}, u32[]{:S(2)}, u32[]{:S(2)}) collective-permute-start(bf16[256,256]{1,0:T(8,128)(2,1)S(1)} %copy-done.2), channel_id=1, source_target_pairs={{0,5},{1,6},{2,7},{3,0},{4,1},{5,2},{6,3},{7,4},{8,13},{9,14},{10,... | collective-permute-start | bytes 393224 | tf_op jit(solution)/shard_map/ppermute | solution.py:60
  68.4 2.5 fusion.31
  74.6 5.0 %collective-permute-start.5 = (bf16[256,256]{1,0:T(8,128)(2,1)S(1)}, bf16[256,256]{1,0:T(8,128)(2,1)S(1)}, u32[]{:S(2)}, u32[]{:S(2)}) collective-permute-start(bf16[256,256]{1,0:T(8,128)(2,1)S(1)} %copy-done.2), channel_id=1, source_target_pairs={{0,6},{1,7},{2,0},{3,1},{4,2},{5,3},{6,4},{7,5},{8,14},{9,15},{10,... | collective-permute-start | bytes 393224 | tf_op jit(solution)/shard_map/ppermute | solution.py:60
  80.3 3.0 %collective-permute-start.6 = (bf16[256,256]{1,0:T(8,128)(2,1)S(1)}, bf16[256,256]{1,0:T(8,128)(2,1)S(1)}, u32[]{:S(2)}, u32[]{:S(2)}) collective-permute-start(bf16[256,256]{1,0:T(8,128)(2,1)S(1)} %copy-done.2), channel_id=1, source_target_pairs={{0,7},{1,0},{2,1},{3,2},{4,3},{5,4},{6,5},{7,6},{8,15},{9,8},{10,9... | collective-permute-start | bytes 393224 | tf_op jit(solution)/shard_map/ppermute | solution.py:60
  86.5 1.6 collective-permute-done.6
  88.8 1.9 gather_fusion
  92.2 3.0 %copy.53 = f32[256,8,256]{0,2,1:T(8,128)} copy(f32[256,8,256]{2,0,1:T(8,128)} %convert_bitcast_fusion) | data formatting | bytes 4194304 | tf_op jit(solution)/shard_map/convert_element_type | solution.py:16
  97.6 45.4 %all-gather.2.cloned.1.call-done = bf16[2048,1792]{1,0:T(8,128)(2,1)} async-done(((bf16[32,1792]{1,0:T(8,128)(2,1)}), bf16[2048,1792]{1,0:T(8,128)(2,1)}) %all-gather.2.cloned.1.call-update) | async-done | bytes 7340048 | tf_op jit(solution)/shard_map/all_gather | solution.py:168
  143.0 2.9 %fusion.16 = f32[256,768]{1,0:T(8,128)S(1)} fusion(bf16[256,2048]{0,1:T(8,128)(2,1)S(1)} %fusion.15, bf16[2048,1792]{1,0:T(8,128)(2,1)} %all-gather.2.cloned.1.call-done, f32[768]{0:T(1024)} %add.184), kind=kOutput, calls=%fused_computation.26 | convolution fusion | flops 805502976 | bytes 4984832 | tf_op jit(solution)/shard_map/dot_general | solution.py:46
  149.0 12.0 %all-to-all-done.1.kc_ref.vc_ref = bf16[64,2,2,32,256]{4,3,2,1,0:T(8,128)(2,1)} async-done(((bf16[64,2,2,32,256]{4,3,2,1,0:T(8,128)(2,1)}), bf16[64,2,2,32,256]{4,3,2,1,0:T(8,128)(2,1)}, u32[]{:S(2)}, u32[]{:S(2)}) %all-to-all-start.1) | async-done | bytes 4194336 | tf_op jit(solution)/shard_map/all_to_all | solution.py:205
  161.0 13.4 %shard_map.167 = bf16[256,256]{1,0:T(8,128)(2,1)} custom-call(bf16[256,256]{1,0:T(8,128)(2,1)} %copy.59.q_ref, bf16[64,2,2,32,256]{4,3,2,1,0:T(8,128)(2,1)} %all-to-all-done.1.kc_ref.vc_ref, bf16[64,2,2,32,256]{4,3,2,1,0:T(8,128)(2,1)} %all-to-all-done.1.kc_ref.vc_ref, bf16[256,256]{1,0:T(8,128)(2,1)} %copy.60.kn_ref, bf16[256,256]{1,0:T(8,128)(2,1)} %bitcast.112, ...), custom_call_target="tpu_custom_call" | custom-call | tf_op jit(solution)/shard_map/pallas_call | solution.py:120
  174.4 1.8 convolution_convert_fusion
  177.2 6.8 %all-to-all-start.2 = ((bf16[256,8,256]{2,0,1:T(8,128)(2,1)}), bf16[256,8,256]{2,0,1:T(8,128)(2,1)S(1)}, u32[]{:S(2)}, u32[]{:S(2)}) async-start(bf16[256,8,256]{2,0,1:T(8,128)(2,1)} %bitcast.103), calls=%async_computation.2 | async-start | bytes 2097152 | tf_op jit(solution)/shard_map/all_to_all | solution.py:229
  184.8 28.5 %all-to-all-done.2 = bf16[256,8,256]{2,0,1:T(8,128)(2,1)S(1)} async-done(((bf16[256,8,256]{2,0,1:T(8,128)(2,1)}), bf16[256,8,256]{2,0,1:T(8,128)(2,1)S(1)}, u32[]{:S(2)}, u32[]{:S(2)}) %all-to-all-start.2) | async-done | bytes 1048608 | tf_op jit(solution)/shard_map/all_to_all | solution.py:229
  215.6 3.7 %all-to-all-start.3 = ((bf16[8,256,256]{1,2,0:T(8,128)(2,1)}), bf16[8,256,256]{1,2,0:T(8,128)(2,1)S(1)}, u32[]{:S(2)}, u32[]{:S(2)}) async-start(bf16[8,256,256]{1,2,0:T(8,128)(2,1)} %broadcast_in_dim.56), calls=%async_computation.3 | async-start | bytes 2097152 | tf_op jit(solution)/shard_map/all_to_all | solution.py:53
  219.3 29.1 %all-to-all-done.3 = bf16[8,256,256]{1,2,0:T(8,128)(2,1)S(1)} async-done(((bf16[8,256,256]{1,2,0:T(8,128)(2,1)}), bf16[8,256,256]{1,2,0:T(8,128)(2,1)S(1)}, u32[]{:S(2)}, u32[]{:S(2)}) %all-to-all-start.3) | async-done | bytes 1048608 | tf_op jit(solution)/shard_map/all_to_all | solution.py:53
  249.8 2.9 %fusion.22 = bf16[256,768]{1,0:T(8,128)(2,1)S(1)} fusion(bf16[256,2048]{0,1:T(8,128)(2,1)S(1)} %fusion.9, bf16[2048,1792]{1,0:T(8,128)(2,1)} %all-gather.2.cloned.1.call-done, f32[768]{0:T(1024)S(1)} %add.204), kind=kOutput, calls=%fused_computation.28 | convolution fusion | flops 805699584 | bytes 4590592 | tf_op jit(solution)/shard_map/dot_general | solution.py:46
  (110 shorter events, 29.8 us)
Async XLA Ops:
  7.2 30.6 %copy-start = (bf16[48,2,32,256]{3,2,1,0:T(8,128)(2,1)S(1)}, bf16[48,2,32,256]{3,2,1,0:T(8,128)(2,1)}, u32[]{:S(2)}) copy-start(bf16[48,2,32,256]{3,2,1,0:T(8,128)(2,1)} %param.22) | copy-start | bytes 4718596
  7.2 135.9 %all-gather.2.cloned.1.call-start = ((), (), s32[]{:S(2)}) async-start(), calls=%async_computation.4 | async-start | bytes 7454720 | tf_op jit(solution)/shard_map/all_gather | solution.py:168
  40.6 5.9 %copy-start.2 = (bf16[256,256]{1,0:T(8,128)(2,1)S(1)}, bf16[256,256]{1,0:T(8,128)(2,1)}, u32[]{:S(2)}) copy-start(bf16[256,256]{1,0:T(8,128)(2,1)} %param.16) | copy-start | bytes 393220
  40.6 26.4 %copy-start.7 = (s32[256]{0:T(256)S(1)}, s32[256]{0:T(256)}, u32[]{:S(2)}) copy-start(s32[256]{0:T(256)} %param.29) | copy-start | bytes 3076
  40.6 27.1 %copy-start.6 = (s32[4]{0:T(128)S(1)}, s32[4]{0:T(128)}, u32[]{:S(2)}) copy-start(s32[4]{0:T(128)} %param.30) | copy-start | bytes 52
  40.6 31.9 %copy-start.12 = (f32[3,256]{1,0:T(4,128)S(1)}, f32[3,256]{1,0:T(4,128)}, u32[]{:S(2)}) copy-start(f32[3,256]{1,0:T(4,128)} %param.21) | copy-start | bytes 9220
  40.7 120.3 %all-to-all-start.1 = ((bf16[64,2,2,32,256]{4,3,2,1,0:T(8,128)(2,1)}), bf16[64,2,2,32,256]{4,3,2,1,0:T(8,128)(2,1)}, u32[]{:S(2)}, u32[]{:S(2)}) async-start(bf16[64,2,2,32,256]{4,3,2,1,0:T(8,128)(2,1)} %bitcast.102), calls=%async_computation.1 | async-start | bytes 8388608 | tf_op jit(solution)/shard_map/all_to_all | solution.py:205
  46.5 28.1 %collective-permute-start = (bf16[256,256]{1,0:T(8,128)(2,1)S(1)}, bf16[256,256]{1,0:T(8,128)(2,1)S(1)}, u32[]{:S(2)}, u32[]{:S(2)}) collective-permute-start(bf16[256,256]{1,0:T(8,128)(2,1)S(1)} %copy-done.2), channel_id=1, source_target_pairs={{0,1},{1,2},{2,3},{3,4},{4,5},{5,6},{6,7},{7,0},{8,9},{9,10},{10,1... | collective-permute-start | bytes 393224 | tf_op jit(solution)/shard_map/ppermute | solution.py:60
  49.7 30.6 %collective-permute-start.1 = (bf16[256,256]{1,0:T(8,128)(2,1)S(1)}, bf16[256,256]{1,0:T(8,128)(2,1)S(1)}, u32[]{:S(2)}, u32[]{:S(2)}) collective-permute-start(bf16[256,256]{1,0:T(8,128)(2,1)S(1)} %copy-done.2), channel_id=1, source_target_pairs={{0,2},{1,3},{2,4},{3,5},{4,6},{5,7},{6,0},{7,1},{8,10},{9,11},{10,... | collective-permute-start | bytes 393224 | tf_op jit(solution)/shard_map/ppermute | solution.py:60
  53.9 30.0 %collective-permute-start.2 = (bf16[256,256]{1,0:T(8,128)(2,1)S(1)}, bf16[256,256]{1,0:T(8,128)(2,1)S(1)}, u32[]{:S(2)}, u32[]{:S(2)}) collective-permute-start(bf16[256,256]{1,0:T(8,128)(2,1)S(1)} %copy-done.2), channel_id=1, source_target_pairs={{0,3},{1,4},{2,5},{3,6},{4,7},{5,0},{6,1},{7,2},{8,11},{9,12},{10,... | collective-permute-start | bytes 393224 | tf_op jit(solution)/shard_map/ppermute | solution.py:60
  58.6 26.0 %collective-permute-start.3 = (bf16[256,256]{1,0:T(8,128)(2,1)S(1)}, bf16[256,256]{1,0:T(8,128)(2,1)S(1)}, u32[]{:S(2)}, u32[]{:S(2)}) collective-permute-start(bf16[256,256]{1,0:T(8,128)(2,1)S(1)} %copy-done.2), channel_id=1, source_target_pairs={{0,4},{1,5},{2,6},{3,7},{4,0},{5,1},{6,2},{7,3},{8,12},{9,13},{10,... | collective-permute-start | bytes 393224 | tf_op jit(solution)/shard_map/ppermute | solution.py:60
  62.1 23.1 %collective-permute-start.4 = (bf16[256,256]{1,0:T(8,128)(2,1)S(1)}, bf16[256,256]{1,0:T(8,128)(2,1)S(1)}, u32[]{:S(2)}, u32[]{:S(2)}) collective-permute-start(bf16[256,256]{1,0:T(8,128)(2,1)S(1)} %copy-done.2), channel_id=1, source_target_pairs={{0,5},{1,6},{2,7},{3,0},{4,1},{5,2},{6,3},{7,4},{8,13},{9,14},{10,... | collective-permute-start | bytes 393224 | tf_op jit(solution)/shard_map/ppermute | solution.py:60
  68.3 6.3 %copy-start.5 = (s32[256]{0:T(256)}, s32[256]{0:T(256)S(1)}, u32[]{:S(2)}) copy-start(s32[256]{0:T(256)S(1)} %broadcast_subtract_fusion) | copy-start | bytes 3076
  74.6 11.3 %collective-permute-start.5 = (bf16[256,256]{1,0:T(8,128)(2,1)S(1)}, bf16[256,256]{1,0:T(8,128)(2,1)S(1)}, u32[]{:S(2)}, u32[]{:S(2)}) collective-permute-start(bf16[256,256]{1,0:T(8,128)(2,1)S(1)} %copy-done.2), channel_id=1, source_target_pairs={{0,6},{1,7},{2,0},{3,1},{4,2},{5,3},{6,4},{7,5},{8,14},{9,15},{10,... | collective-permute-start | bytes 393224 | tf_op jit(solution)/shard_map/ppermute | solution.py:60
  80.3 7.8 %collective-permute-start.6 = (bf16[256,256]{1,0:T(8,128)(2,1)S(1)}, bf16[256,256]{1,0:T(8,128)(2,1)S(1)}, u32[]{:S(2)}, u32[]{:S(2)}) collective-permute-start(bf16[256,256]{1,0:T(8,128)(2,1)S(1)} %copy-done.2), channel_id=1, source_target_pairs={{0,7},{1,0},{2,1},{3,2},{4,3},{5,4},{6,5},{7,6},{8,15},{9,8},{10,9... | collective-permute-start | bytes 393224 | tf_op jit(solution)/shard_map/ppermute | solution.py:60
  92.2 3.6 %copy-start.8 = (f32[2048]{0:T(1024)S(1)}, f32[2048]{0:T(1024)}, u32[]{:S(2)}) copy-start(f32[2048]{0:T(1024)} %param.19) | copy-start | bytes 24580
  92.2 3.7 %copy-start.9 = (f32[2048]{0:T(1024)S(1)}, f32[2048]{0:T(1024)}, u32[]{:S(2)}) copy-start(f32[2048]{0:T(1024)} %param.18) | copy-start | bytes 24580
  95.2 1.6 copy-start.1
  177.2 36.1 %all-to-all-start.2 = ((bf16[256,8,256]{2,0,1:T(8,128)(2,1)}), bf16[256,8,256]{2,0,1:T(8,128)(2,1)S(1)}, u32[]{:S(2)}, u32[]{:S(2)}) async-start(bf16[256,8,256]{2,0,1:T(8,128)(2,1)} %bitcast.103), calls=%async_computation.2 | async-start | bytes 2097152 | tf_op jit(solution)/shard_map/all_to_all | solution.py:229
  213.4 5.9 %copy-start.13 = (f32[3,256]{1,0:T(4,128)S(1)}, f32[3,256]{1,0:T(4,128)}, u32[]{:S(2)}) copy-start(f32[3,256]{1,0:T(4,128)} %param.28) | copy-start | bytes 9220
  214.4 34.3 %copy-start.3 = (bf16[256,256]{1,0:T(8,128)(2,1)}, bf16[256,256]{1,0:T(8,128)(2,1)S(1)}, u32[]{:S(2)}) copy-start(bf16[256,256]{1,0:T(8,128)(2,1)S(1)} %add_convert_fusion) | copy-start | bytes 393220
  215.6 33.5 %copy-start.10 = (f32[2048]{0:T(1024)S(1)}, f32[2048]{0:T(1024)}, u32[]{:S(2)}) copy-start(f32[2048]{0:T(1024)} %param.26) | copy-start | bytes 24580
  215.6 33.5 %copy-start.11 = (f32[2048]{0:T(1024)S(1)}, f32[2048]{0:T(1024)}, u32[]{:S(2)}) copy-start(f32[2048]{0:T(1024)} %param.25) | copy-start | bytes 24580
  215.6 32.9 %all-to-all-start.3 = ((bf16[8,256,256]{1,2,0:T(8,128)(2,1)}), bf16[8,256,256]{1,2,0:T(8,128)(2,1)S(1)}, u32[]{:S(2)}, u32[]{:S(2)}) async-start(bf16[8,256,256]{1,2,0:T(8,128)(2,1)} %broadcast_in_dim.56), calls=%async_computation.3 | async-start | bytes 2097152 | tf_op jit(solution)/shard_map/all_to_all | solution.py:53
  (1 other events, 0.7 us)
Sparse Core Ops, SparseCore 0:
  11.9 131.0 all-gather.1

commit v11 on v9

--- a/solution.py
+++ b/solution.py
@@ -65,7 +65,7 @@
     return by_source.transpose(1, 0, 2).reshape(block.shape[0], mp_count * block.shape[1])
 
 
-Q_CHUNK = 128
+Q_CHUNK = 256
 PAIR = 128
 
 

time: 262 us -> 261 us (level)
  no operation moved by 1% of the time
where the time goes in v11:
time: 261 us; the launch traced here: 260 us
  waiting for transfers between devices  116 us (44%)
  starting transfers between devices  45 us (17%)
  local copies, waits for them, and re-layouts  26.6 us (10%)
  blocking collectives  23.9 us (9%)
  between operations  14.4 us (6%)
  other arithmetic  13.3 us (5%)
  Pallas kernels  12.3 us (5%)
  matrix products  7.57 us (3%)
    all_gather x1, waiting for transfers between devices, local(): gathered = lax.all_gather(joined, 'pool', axis=0, tiled=True)  45.4 us
    all_to_all x1, waiting for transfers between devices, mp_gather(): lax.all_to_all(spread, 'mp', split_axis=0, concat_axis=2, tiled=True)  29.1 us
    ppermute x7, starting transfers between devices, mp_permute_gather(): lax.ppermute(block, 'mp', [(src, (src + shift) % mp_count) for src in ran...  28.6 us
    all_to_all x1, waiting for transfers between devices, local(): lax.all_to_all(pieces, 'mp', split_axis=1, concat_axis=1, tiled=True)  28.5 us
    all_to_all x1, blocking collectives, local(): lax.all_to_all(slot_ids, 'pool', split_axis=0, concat_axis=0, tiled=True)  23.9 us
    pallas_call x1, Pallas kernels, attention_call(): pl.pallas_call(attention_body, grid=grid, in_specs=[pl.BlockSpec((Q_CHUNK...  12.3 us
    all_to_all x1, waiting for transfers between devices, local(): lax.all_to_all(packed, 'pool', split_axis=0, concat_axis=0, tiled=True)  12 us
    unnamed x37, local copies, waits for them, and re-layouts  7.58 us
  transfers between devices with their start and end apart: 11, of which 5 were waited for; matrix products, arithmetic and copies ran while one was open for 13% of the time, Pallas kernels for 0%

profile of v11, /device:TPU:1, one launch (start us, length us, event | category | flops | bytes accessed | tf_op | source)
XLA Modules:
  0.0 259.6 jit_solution(16444328847461544470)
XLA Ops:
  12.4 23.9 %all_to_all.28 = s32[64,1,2]{2,1,0:T(1,128)S(1)} all-to-all(s32[64,1,2]{2,1,0:T(1,128)S(1)} %bitcast.117), channel_id=1, replica_groups=mesh['pool'=64,'mp'=8] {'pool'}, dimensions={0} | all-to-all | bytes 1024 | tf_op jit(solution)/shard_map/all_to_all | solution.py:202
  37.8 2.9 %gather_fusion.1 = bf16[128,2,32,256]{3,2,1,0:T(8,128)(2,1)} fusion(bf16[48,2,32,256]{3,2,1,0:T(8,128)(2,1)S(1)} %copy-done, s32[1024]{0:T(1024)S(1)} %pad_clamp_fusion), kind=kCustom, calls=%fused_computation.1 | custom fusion | bytes 8389120 | tf_op jit(solution)/shard_map/gather | solution.py:203
  40.7 5.8 %all-to-all-start.1 = ((bf16[64,2,2,32,256]{4,3,2,1,0:T(8,128)(2,1)}), bf16[64,2,2,32,256]{4,3,2,1,0:T(8,128)(2,1)}, u32[]{:S(2)}, u32[]{:S(2)}) async-start(bf16[64,2,2,32,256]{4,3,2,1,0:T(8,128)(2,1)} %bitcast.102), calls=%async_computation.1 | async-start | bytes 8388608 | tf_op jit(solution)/shard_map/all_to_all | solution.py:204
  46.5 3.2 %collective-permute-start = (bf16[256,256]{1,0:T(8,128)(2,1)S(1)}, bf16[256,256]{1,0:T(8,128)(2,1)S(1)}, u32[]{:S(2)}, u32[]{:S(2)}) collective-permute-start(bf16[256,256]{1,0:T(8,128)(2,1)S(1)} %copy-done.2), channel_id=1, source_target_pairs={{0,1},{1,2},{2,3},{3,4},{4,5},{5,6},{6,7},{7,0},{8,9},{9,10},{10,1... | collective-permute-start | bytes 393224 | tf_op jit(solution)/shard_map/ppermute | solution.py:60
  49.7 4.2 %collective-permute-start.1 = (bf16[256,256]{1,0:T(8,128)(2,1)S(1)}, bf16[256,256]{1,0:T(8,128)(2,1)S(1)}, u32[]{:S(2)}, u32[]{:S(2)}) collective-permute-start(bf16[256,256]{1,0:T(8,128)(2,1)S(1)} %copy-done.2), channel_id=1, source_target_pairs={{0,2},{1,3},{2,4},{3,5},{4,6},{5,7},{6,0},{7,1},{8,10},{9,11},{10,... | collective-permute-start | bytes 393224 | tf_op jit(solution)/shard_map/ppermute | solution.py:60
  53.9 4.6 %collective-permute-start.2 = (bf16[256,256]{1,0:T(8,128)(2,1)S(1)}, bf16[256,256]{1,0:T(8,128)(2,1)S(1)}, u32[]{:S(2)}, u32[]{:S(2)}) collective-permute-start(bf16[256,256]{1,0:T(8,128)(2,1)S(1)} %copy-done.2), channel_id=1, source_target_pairs={{0,3},{1,4},{2,5},{3,6},{4,7},{5,0},{6,1},{7,2},{8,11},{9,12},{10,... | collective-permute-start | bytes 393224 | tf_op jit(solution)/shard_map/ppermute | solution.py:60
  58.6 3.5 %collective-permute-start.3 = (bf16[256,256]{1,0:T(8,128)(2,1)S(1)}, bf16[256,256]{1,0:T(8,128)(2,1)S(1)}, u32[]{:S(2)}, u32[]{:S(2)}) collective-permute-start(bf16[256,256]{1,0:T(8,128)(2,1)S(1)} %copy-done.2), channel_id=1, source_target_pairs={{0,4},{1,5},{2,6},{3,7},{4,0},{5,1},{6,2},{7,3},{8,12},{9,13},{10,... | collective-permute-start | bytes 393224 | tf_op jit(solution)/shard_map/ppermute | solution.py:60
  62.1 4.9 %collective-permute-start.4 = (bf16[256,256]{1,0:T(8,128)(2,1)S(1)}, bf16[256,256]{1,0:T(8,128)(2,1)S(1)}, u32[]{:S(2)}, u32[]{:S(2)}) collective-permute-start(bf16[256,256]{1,0:T(8,128)(2,1)S(1)} %copy-done.2), channel_id=1, source_target_pairs={{0,5},{1,6},{2,7},{3,0},{4,1},{5,2},{6,3},{7,4},{8,13},{9,14},{10,... | collective-permute-start | bytes 393224 | tf_op jit(solution)/shard_map/ppermute | solution.py:60
  68.4 2.5 fusion.31
  74.6 5.0 %collective-permute-start.5 = (bf16[256,256]{1,0:T(8,128)(2,1)S(1)}, bf16[256,256]{1,0:T(8,128)(2,1)S(1)}, u32[]{:S(2)}, u32[]{:S(2)}) collective-permute-start(bf16[256,256]{1,0:T(8,128)(2,1)S(1)} %copy-done.2), channel_id=1, source_target_pairs={{0,6},{1,7},{2,0},{3,1},{4,2},{5,3},{6,4},{7,5},{8,14},{9,15},{10,... | collective-permute-start | bytes 393224 | tf_op jit(solution)/shard_map/ppermute | solution.py:60
  80.3 3.1 %collective-permute-start.6 = (bf16[256,256]{1,0:T(8,128)(2,1)S(1)}, bf16[256,256]{1,0:T(8,128)(2,1)S(1)}, u32[]{:S(2)}, u32[]{:S(2)}) collective-permute-start(bf16[256,256]{1,0:T(8,128)(2,1)S(1)} %copy-done.2), channel_id=1, source_target_pairs={{0,7},{1,0},{2,1},{3,2},{4,3},{5,4},{6,5},{7,6},{8,15},{9,8},{10,9... | collective-permute-start | bytes 393224 | tf_op jit(solution)/shard_map/ppermute | solution.py:60
  88.8 1.9 gather_fusion
  90.7 1.5 convert_bitcast_fusion
  92.2 3.0 %copy.53 = f32[256,8,256]{0,2,1:T(8,128)} copy(f32[256,8,256]{2,0,1:T(8,128)} %convert_bitcast_fusion) | data formatting | bytes 4194304 | tf_op jit(solution)/shard_map/convert_element_type | solution.py:16
  97.6 45.4 %all-gather.2.cloned.1.call-done = bf16[2048,1792]{1,0:T(8,128)(2,1)} async-done(((bf16[32,1792]{1,0:T(8,128)(2,1)}), bf16[2048,1792]{1,0:T(8,128)(2,1)}) %all-gather.2.cloned.1.call-update) | async-done | bytes 7340048 | tf_op jit(solution)/shard_map/all_gather | solution.py:167
  143.0 2.9 %fusion.16 = f32[256,768]{1,0:T(8,128)S(1)} fusion(bf16[256,2048]{0,1:T(8,128)(2,1)S(1)} %fusion.15, bf16[2048,1792]{1,0:T(8,128)(2,1)} %all-gather.2.cloned.1.call-done, f32[768]{0:T(1024)} %add.184), kind=kOutput, calls=%fused_computation.26 | convolution fusion | flops 805502976 | bytes 4984832 | tf_op jit(solution)/shard_map/dot_general | solution.py:46
  149.0 12.0 %all-to-all-done.1.kc_ref.vc_ref = bf16[64,2,2,32,256]{4,3,2,1,0:T(8,128)(2,1)} async-done(((bf16[64,2,2,32,256]{4,3,2,1,0:T(8,128)(2,1)}), bf16[64,2,2,32,256]{4,3,2,1,0:T(8,128)(2,1)}, u32[]{:S(2)}, u32[]{:S(2)}) %all-to-all-start.1) | async-done | bytes 4194336 | tf_op jit(solution)/shard_map/all_to_all | solution.py:204
  161.0 12.3 %shard_map.167 = bf16[256,256]{1,0:T(8,128)(2,1)} custom-call(bf16[256,256]{1,0:T(8,128)(2,1)} %copy.59.q_ref, bf16[64,2,2,32,256]{4,3,2,1,0:T(8,128)(2,1)} %all-to-all-done.1.kc_ref.vc_ref, bf16[64,2,2,32,256]{4,3,2,1,0:T(8,128)(2,1)} %all-to-all-done.1.kc_ref.vc_ref, bf16[256,256]{1,0:T(8,128)(2,1)} %copy.60.kn_ref, bf16[256,256]{1,0:T(8,128)(2,1)} %bitcast.112, ...), custom_call_target="tpu_custom_call" | custom-call | tf_op jit(solution)/shard_map/pallas_call | solution.py:119
  173.3 1.8 convolution_convert_fusion
  176.1 6.8 %all-to-all-start.2 = ((bf16[256,8,256]{2,0,1:T(8,128)(2,1)}), bf16[256,8,256]{2,0,1:T(8,128)(2,1)S(1)}, u32[]{:S(2)}, u32[]{:S(2)}) async-start(bf16[256,8,256]{2,0,1:T(8,128)(2,1)} %bitcast.103), calls=%async_computation.2 | async-start | bytes 2097152 | tf_op jit(solution)/shard_map/all_to_all | solution.py:228
  183.7 28.5 %all-to-all-done.2 = bf16[256,8,256]{2,0,1:T(8,128)(2,1)S(1)} async-done(((bf16[256,8,256]{2,0,1:T(8,128)(2,1)}), bf16[256,8,256]{2,0,1:T(8,128)(2,1)S(1)}, u32[]{:S(2)}, u32[]{:S(2)}) %all-to-all-start.2) | async-done | bytes 1048608 | tf_op jit(solution)/shard_map/all_to_all | solution.py:228
  214.5 3.7 %all-to-all-start.3 = ((bf16[8,256,256]{1,2,0:T(8,128)(2,1)}), bf16[8,256,256]{1,2,0:T(8,128)(2,1)S(1)}, u32[]{:S(2)}, u32[]{:S(2)}) async-start(bf16[8,256,256]{1,2,0:T(8,128)(2,1)} %broadcast_in_dim.56), calls=%async_computation.3 | async-start | bytes 2097152 | tf_op jit(solution)/shard_map/all_to_all | solution.py:53
  218.2 29.1 %all-to-all-done.3 = bf16[8,256,256]{1,2,0:T(8,128)(2,1)S(1)} async-done(((bf16[8,256,256]{1,2,0:T(8,128)(2,1)}), bf16[8,256,256]{1,2,0:T(8,128)(2,1)S(1)}, u32[]{:S(2)}, u32[]{:S(2)}) %all-to-all-start.3) | async-done | bytes 1048608 | tf_op jit(solution)/shard_map/all_to_all | solution.py:53
  248.7 2.9 %fusion.22 = bf16[256,768]{1,0:T(8,128)(2,1)S(1)} fusion(bf16[256,2048]{0,1:T(8,128)(2,1)S(1)} %fusion.9, bf16[2048,1792]{1,0:T(8,128)(2,1)} %all-gather.2.cloned.1.call-done, f32[768]{0:T(1024)S(1)} %add.204), kind=kOutput, calls=%fused_computation.28 | convolution fusion | flops 805699584 | bytes 4590592 | tf_op jit(solution)/shard_map/dot_general | solution.py:46
  (110 shorter events, 29.7 us)
Async XLA Ops:
  7.2 30.6 %copy-start = (bf16[48,2,32,256]{3,2,1,0:T(8,128)(2,1)S(1)}, bf16[48,2,32,256]{3,2,1,0:T(8,128)(2,1)}, u32[]{:S(2)}) copy-start(bf16[48,2,32,256]{3,2,1,0:T(8,128)(2,1)} %param.22) | copy-start | bytes 4718596
  7.2 135.9 %all-gather.2.cloned.1.call-start = ((), (), s32[]{:S(2)}) async-start(), calls=%async_computation.4 | async-start | bytes 7454720 | tf_op jit(solution)/shard_map/all_gather | solution.py:167
  40.6 5.9 %copy-start.2 = (bf16[256,256]{1,0:T(8,128)(2,1)S(1)}, bf16[256,256]{1,0:T(8,128)(2,1)}, u32[]{:S(2)}) copy-start(bf16[256,256]{1,0:T(8,128)(2,1)} %param.16) | copy-start | bytes 393220
  40.6 26.4 %copy-start.7 = (s32[256]{0:T(256)S(1)}, s32[256]{0:T(256)}, u32[]{:S(2)}) copy-start(s32[256]{0:T(256)} %param.29) | copy-start | bytes 3076
  40.6 27.1 %copy-start.6 = (s32[4]{0:T(128)S(1)}, s32[4]{0:T(128)}, u32[]{:S(2)}) copy-start(s32[4]{0:T(128)} %param.30) | copy-start | bytes 52
  40.6 31.9 %copy-start.12 = (f32[3,256]{1,0:T(4,128)S(1)}, f32[3,256]{1,0:T(4,128)}, u32[]{:S(2)}) copy-start(f32[3,256]{1,0:T(4,128)} %param.21) | copy-start | bytes 9220
  40.7 120.3 %all-to-all-start.1 = ((bf16[64,2,2,32,256]{4,3,2,1,0:T(8,128)(2,1)}), bf16[64,2,2,32,256]{4,3,2,1,0:T(8,128)(2,1)}, u32[]{:S(2)}, u32[]{:S(2)}) async-start(bf16[64,2,2,32,256]{4,3,2,1,0:T(8,128)(2,1)} %bitcast.102), calls=%async_computation.1 | async-start | bytes 8388608 | tf_op jit(solution)/shard_map/all_to_all | solution.py:204
  46.5 28.1 %collective-permute-start = (bf16[256,256]{1,0:T(8,128)(2,1)S(1)}, bf16[256,256]{1,0:T(8,128)(2,1)S(1)}, u32[]{:S(2)}, u32[]{:S(2)}) collective-permute-start(bf16[256,256]{1,0:T(8,128)(2,1)S(1)} %copy-done.2), channel_id=1, source_target_pairs={{0,1},{1,2},{2,3},{3,4},{4,5},{5,6},{6,7},{7,0},{8,9},{9,10},{10,1... | collective-permute-start | bytes 393224 | tf_op jit(solution)/shard_map/ppermute | solution.py:60
  49.7 30.6 %collective-permute-start.1 = (bf16[256,256]{1,0:T(8,128)(2,1)S(1)}, bf16[256,256]{1,0:T(8,128)(2,1)S(1)}, u32[]{:S(2)}, u32[]{:S(2)}) collective-permute-start(bf16[256,256]{1,0:T(8,128)(2,1)S(1)} %copy-done.2), channel_id=1, source_target_pairs={{0,2},{1,3},{2,4},{3,5},{4,6},{5,7},{6,0},{7,1},{8,10},{9,11},{10,... | collective-permute-start | bytes 393224 | tf_op jit(solution)/shard_map/ppermute | solution.py:60
  53.9 30.2 %collective-permute-start.2 = (bf16[256,256]{1,0:T(8,128)(2,1)S(1)}, bf16[256,256]{1,0:T(8,128)(2,1)S(1)}, u32[]{:S(2)}, u32[]{:S(2)}) collective-permute-start(bf16[256,256]{1,0:T(8,128)(2,1)S(1)} %copy-done.2), channel_id=1, source_target_pairs={{0,3},{1,4},{2,5},{3,6},{4,7},{5,0},{6,1},{7,2},{8,11},{9,12},{10,... | collective-permute-start | bytes 393224 | tf_op jit(solution)/shard_map/ppermute | solution.py:60
  58.6 26.2 %collective-permute-start.3 = (bf16[256,256]{1,0:T(8,128)(2,1)S(1)}, bf16[256,256]{1,0:T(8,128)(2,1)S(1)}, u32[]{:S(2)}, u32[]{:S(2)}) collective-permute-start(bf16[256,256]{1,0:T(8,128)(2,1)S(1)} %copy-done.2), channel_id=1, source_target_pairs={{0,4},{1,5},{2,6},{3,7},{4,0},{5,1},{6,2},{7,3},{8,12},{9,13},{10,... | collective-permute-start | bytes 393224 | tf_op jit(solution)/shard_map/ppermute | solution.py:60
  62.1 23.3 %collective-permute-start.4 = (bf16[256,256]{1,0:T(8,128)(2,1)S(1)}, bf16[256,256]{1,0:T(8,128)(2,1)S(1)}, u32[]{:S(2)}, u32[]{:S(2)}) collective-permute-start(bf16[256,256]{1,0:T(8,128)(2,1)S(1)} %copy-done.2), channel_id=1, source_target_pairs={{0,5},{1,6},{2,7},{3,0},{4,1},{5,2},{6,3},{7,4},{8,13},{9,14},{10,... | collective-permute-start | bytes 393224 | tf_op jit(solution)/shard_map/ppermute | solution.py:60
  68.3 6.3 %copy-start.5 = (s32[256]{0:T(256)}, s32[256]{0:T(256)S(1)}, u32[]{:S(2)}) copy-start(s32[256]{0:T(256)S(1)} %broadcast_subtract_fusion) | copy-start | bytes 3076
  74.6 11.4 %collective-permute-start.5 = (bf16[256,256]{1,0:T(8,128)(2,1)S(1)}, bf16[256,256]{1,0:T(8,128)(2,1)S(1)}, u32[]{:S(2)}, u32[]{:S(2)}) collective-permute-start(bf16[256,256]{1,0:T(8,128)(2,1)S(1)} %copy-done.2), channel_id=1, source_target_pairs={{0,6},{1,7},{2,0},{3,1},{4,2},{5,3},{6,4},{7,5},{8,14},{9,15},{10,... | collective-permute-start | bytes 393224 | tf_op jit(solution)/shard_map/ppermute | solution.py:60
  80.3 7.8 %collective-permute-start.6 = (bf16[256,256]{1,0:T(8,128)(2,1)S(1)}, bf16[256,256]{1,0:T(8,128)(2,1)S(1)}, u32[]{:S(2)}, u32[]{:S(2)}) collective-permute-start(bf16[256,256]{1,0:T(8,128)(2,1)S(1)} %copy-done.2), channel_id=1, source_target_pairs={{0,7},{1,0},{2,1},{3,2},{4,3},{5,4},{6,5},{7,6},{8,15},{9,8},{10,9... | collective-permute-start | bytes 393224 | tf_op jit(solution)/shard_map/ppermute | solution.py:60
  92.2 3.6 %copy-start.8 = (f32[2048]{0:T(1024)S(1)}, f32[2048]{0:T(1024)}, u32[]{:S(2)}) copy-start(f32[2048]{0:T(1024)} %param.19) | copy-start | bytes 24580
  92.2 3.7 %copy-start.9 = (f32[2048]{0:T(1024)S(1)}, f32[2048]{0:T(1024)}, u32[]{:S(2)}) copy-start(f32[2048]{0:T(1024)} %param.18) | copy-start | bytes 24580
  95.2 1.6 copy-start.1
  176.1 36.1 %all-to-all-start.2 = ((bf16[256,8,256]{2,0,1:T(8,128)(2,1)}), bf16[256,8,256]{2,0,1:T(8,128)(2,1)S(1)}, u32[]{:S(2)}, u32[]{:S(2)}) async-start(bf16[256,8,256]{2,0,1:T(8,128)(2,1)} %bitcast.103), calls=%async_computation.2 | async-start | bytes 2097152 | tf_op jit(solution)/shard_map/all_to_all | solution.py:228
  212.3 5.9 %copy-start.13 = (f32[3,256]{1,0:T(4,128)S(1)}, f32[3,256]{1,0:T(4,128)}, u32[]{:S(2)}) copy-start(f32[3,256]{1,0:T(4,128)} %param.28) | copy-start | bytes 9220
  213.3 34.3 %copy-start.3 = (bf16[256,256]{1,0:T(8,128)(2,1)}, bf16[256,256]{1,0:T(8,128)(2,1)S(1)}, u32[]{:S(2)}) copy-start(bf16[256,256]{1,0:T(8,128)(2,1)S(1)} %add_convert_fusion) | copy-start | bytes 393220
  214.5 33.5 %copy-start.10 = (f32[2048]{0:T(1024)S(1)}, f32[2048]{0:T(1024)}, u32[]{:S(2)}) copy-start(f32[2048]{0:T(1024)} %param.26) | copy-start | bytes 24580
  214.5 33.5 %copy-start.11 = (f32[2048]{0:T(1024)S(1)}, f32[2048]{0:T(1024)}, u32[]{:S(2)}) copy-start(f32[2048]{0:T(1024)} %param.25) | copy-start | bytes 24580
  214.5 32.9 %all-to-all-start.3 = ((bf16[8,256,256]{1,2,0:T(8,128)(2,1)}), bf16[8,256,256]{1,2,0:T(8,128)(2,1)S(1)}, u32[]{:S(2)}, u32[]{:S(2)}) async-start(bf16[8,256,256]{1,2,0:T(8,128)(2,1)} %broadcast_in_dim.56), calls=%async_computation.3 | async-start | bytes 2097152 | tf_op jit(solution)/shard_map/all_to_all | solution.py:53
  (1 other events, 0.7 us)
Sparse Core Ops, SparseCore 0:
  11.9 131.0 all-gather.1

commit v12 on v11

--- a/solution.py
+++ b/solution.py
@@ -69,7 +69,7 @@
 PAIR = 128
 
 
-def attention_body(q_ref, kc_ref, vc_ref, kn_ref, vn_ref, keyc_ref, keyn_ref, qreq_ref, out_ref):
+def attention_body(q_ref, kc_ref, vc_ref, kn_ref, vn_ref, keyc_ref, keyn_ref, qreq_ref, wd_ref, out_ref, acc_ref):
     chunk = pl.program_id(1)
     n_slots = kc_ref.shape[0] * kc_ref.shape[1] * kc_ref.shape[2]
     n_new = kn_ref.shape[0]
@@ -106,11 +106,20 @@
             p_n, vn_pair, preferred_element_type=jnp.float32
         )
         halves.append((in_head, o))
-    merged = jnp.where(halves[0][0], halves[0][1], halves[1][1])
-    out_ref[...] = merged.astype(out_ref.dtype)
-
-
-def attention_call(query, arrived, key_new, value_new, key_req_c, key_req_n, q_req):
+    merged = jnp.where(halves[0][0], halves[0][1], halves[1][1]).astype(jnp.bfloat16)
+    dense_part = lax.dot_general(merged, wd_ref[...], nt, preferred_element_type=jnp.float32)
+    pair = pl.program_id(0)
+
+    @pl.when(pair == 0)
+    def _():
+        acc_ref[...] = dense_part
+
+    @pl.when(pair == pl.num_programs(0) - 1)
+    def _():
+        out_ref[...] = (acc_ref[...] + dense_part).astype(out_ref.dtype)
+
+
+def attention_call(query, arrived, key_new, value_new, key_req_c, key_req_n, q_req, w_dense_t):
     tok, width = query.shape
     holders, per, _, blk, _ = arrived.shape
     n_slots = holders * per * blk
@@ -128,10 +137,12 @@
             pl.BlockSpec((1, n_slots), full),
             pl.BlockSpec((1, tok), full),
             pl.BlockSpec((Q_CHUNK, 1), lambda p, c: (c, 0)),
+            pl.BlockSpec((w_dense_t.shape[0], PAIR), lambda p, c: (0, p)),
         ],
-        out_specs=pl.BlockSpec((Q_CHUNK, PAIR), lambda p, c: (c, p)),
-        out_shape=jax.ShapeDtypeStruct((tok, width), jnp.bfloat16),
-    )(query, arrived, arrived, key_new, value_new, key_req_c, key_req_n, q_req)
+        out_specs=pl.BlockSpec((Q_CHUNK, w_dense_t.shape[0]), lambda p, c: (c, 0)),
+        out_shape=jax.ShapeDtypeStruct((tok, w_dense_t.shape[0]), jnp.bfloat16),
+        scratch_shapes=[pltpu.VMEM((Q_CHUNK, w_dense_t.shape[0]), jnp.float32)],
+    )(query, arrived, arrived, key_new, value_new, key_req_c, key_req_n, q_req, w_dense_t)
 
 
 def local(
@@ -219,12 +230,10 @@
         key_req_c,
         local_req.reshape(1, tok_count),
         local_req.reshape(tok_count, 1),
-    )
-    partial_out = lax.dot_general(
-        attended, w_dense_t, (((1,), (1,)), ((), ())), preferred_element_type=jnp.float32
+        w_dense_t,
     )
     mp_index = lax.axis_index("mp")
-    pieces = partial_out.astype(jnp.bfloat16).reshape(tok_count, mp_count, col_width)
+    pieces = attended.reshape(tok_count, mp_count, col_width)
     arrived_sums = lax.all_to_all(pieces, "mp", split_axis=1, concat_axis=1, tiled=True)
     dense_total = jnp.sum(arrived_sums.astype(jnp.float32), axis=1)
     own_cols = lambda vec: lax.dynamic_slice_in_dim(vec, mp_index * col_width, col_width, 0)

time: 261 us -> 262 us (level)
  local copies, waits for them, and re-layouts: 26.6 us -> 30.2 us
where the time goes in v12:
time: 262 us; the launch traced here: 260 us
  waiting for transfers between devices  114 us (44%)
  starting transfers between devices  45 us (17%)
  local copies, waits for them, and re-layouts  30.2 us (12%)
  blocking collectives  23.9 us (9%)
  between operations  14.4 us (5%)
  Pallas kernels  13.8 us (5%)
  other arithmetic  13.3 us (5%)
  matrix products  5.81 us (2%)
    all_gather x1, waiting for transfers between devices, local(): gathered = lax.all_gather(joined, 'pool', axis=0, tiled=True)  45.4 us
    all_to_all x1, waiting for transfers between devices, mp_gather(): lax.all_to_all(spread, 'mp', split_axis=0, concat_axis=2, tiled=True)  29.1 us
    ppermute x7, starting transfers between devices, mp_permute_gather(): lax.ppermute(block, 'mp', [(src, (src + shift) % mp_count) for src in ran...  28.6 us
    all_to_all x1, waiting for transfers between devices, local(): lax.all_to_all(pieces, 'mp', split_axis=1, concat_axis=1, tiled=True)  28.5 us
    all_to_all x1, blocking collectives, local(): lax.all_to_all(slot_ids, 'pool', split_axis=0, concat_axis=0, tiled=True)  23.9 us
    pallas_call x1, Pallas kernels, attention_call(): pl.pallas_call(attention_body, grid=grid, in_specs=[pl.BlockSpec((Q_CHUNK...  13.8 us
    all_to_all x1, waiting for transfers between devices, local(): lax.all_to_all(packed, 'pool', split_axis=0, concat_axis=0, tiled=True)  9.68 us
    unnamed x37, local copies, waits for them, and re-layouts  7.58 us
  transfers between devices with their start and end apart: 11, of which 5 were waited for; matrix products, arithmetic and copies ran while one was open for 13% of the time, Pallas kernels for 0%

profile of v12, /device:TPU:1, one launch (start us, length us, event | category | flops | bytes accessed | tf_op | source)
XLA Modules:
  0.0 260.5 jit_solution(4182861310123890987)
XLA Ops:
  12.4 23.9 %all_to_all.28 = s32[64,1,2]{2,1,0:T(1,128)S(1)} all-to-all(s32[64,1,2]{2,1,0:T(1,128)S(1)} %bitcast.116), channel_id=1, replica_groups=mesh['pool'=64,'mp'=8] {'pool'}, dimensions={0} | all-to-all | bytes 1024 | tf_op jit(solution)/shard_map/all_to_all | solution.py:213
  37.8 2.9 %gather_fusion.1 = bf16[128,2,32,256]{3,2,1,0:T(8,128)(2,1)} fusion(bf16[48,2,32,256]{3,2,1,0:T(8,128)(2,1)S(1)} %copy-done, s32[1024]{0:T(1024)S(1)} %pad_clamp_fusion), kind=kCustom, calls=%fused_computation.1 | custom fusion | bytes 8389120 | tf_op jit(solution)/shard_map/gather | solution.py:214
  40.7 5.8 %all-to-all-start.1 = ((bf16[64,2,2,32,256]{4,3,2,1,0:T(8,128)(2,1)}), bf16[64,2,2,32,256]{4,3,2,1,0:T(8,128)(2,1)}, u32[]{:S(2)}, u32[]{:S(2)}) async-start(bf16[64,2,2,32,256]{4,3,2,1,0:T(8,128)(2,1)} %bitcast.101), calls=%async_computation.1 | async-start | bytes 8388608 | tf_op jit(solution)/shard_map/all_to_all | solution.py:215
  46.5 3.2 %collective-permute-start = (bf16[256,256]{1,0:T(8,128)(2,1)S(1)}, bf16[256,256]{1,0:T(8,128)(2,1)S(1)}, u32[]{:S(2)}, u32[]{:S(2)}) collective-permute-start(bf16[256,256]{1,0:T(8,128)(2,1)S(1)} %copy-done.2), channel_id=1, source_target_pairs={{0,1},{1,2},{2,3},{3,4},{4,5},{5,6},{6,7},{7,0},{8,9},{9,10},{10,1... | collective-permute-start | bytes 393224 | tf_op jit(solution)/shard_map/ppermute | solution.py:60
  49.7 4.2 %collective-permute-start.1 = (bf16[256,256]{1,0:T(8,128)(2,1)S(1)}, bf16[256,256]{1,0:T(8,128)(2,1)S(1)}, u32[]{:S(2)}, u32[]{:S(2)}) collective-permute-start(bf16[256,256]{1,0:T(8,128)(2,1)S(1)} %copy-done.2), channel_id=1, source_target_pairs={{0,2},{1,3},{2,4},{3,5},{4,6},{5,7},{6,0},{7,1},{8,10},{9,11},{10,... | collective-permute-start | bytes 393224 | tf_op jit(solution)/shard_map/ppermute | solution.py:60
  53.9 4.6 %collective-permute-start.2 = (bf16[256,256]{1,0:T(8,128)(2,1)S(1)}, bf16[256,256]{1,0:T(8,128)(2,1)S(1)}, u32[]{:S(2)}, u32[]{:S(2)}) collective-permute-start(bf16[256,256]{1,0:T(8,128)(2,1)S(1)} %copy-done.2), channel_id=1, source_target_pairs={{0,3},{1,4},{2,5},{3,6},{4,7},{5,0},{6,1},{7,2},{8,11},{9,12},{10,... | collective-permute-start | bytes 393224 | tf_op jit(solution)/shard_map/ppermute | solution.py:60
  58.6 3.5 %collective-permute-start.3 = (bf16[256,256]{1,0:T(8,128)(2,1)S(1)}, bf16[256,256]{1,0:T(8,128)(2,1)S(1)}, u32[]{:S(2)}, u32[]{:S(2)}) collective-permute-start(bf16[256,256]{1,0:T(8,128)(2,1)S(1)} %copy-done.2), channel_id=1, source_target_pairs={{0,4},{1,5},{2,6},{3,7},{4,0},{5,1},{6,2},{7,3},{8,12},{9,13},{10,... | collective-permute-start | bytes 393224 | tf_op jit(solution)/shard_map/ppermute | solution.py:60
  62.1 4.9 %collective-permute-start.4 = (bf16[256,256]{1,0:T(8,128)(2,1)S(1)}, bf16[256,256]{1,0:T(8,128)(2,1)S(1)}, u32[]{:S(2)}, u32[]{:S(2)}) collective-permute-start(bf16[256,256]{1,0:T(8,128)(2,1)S(1)} %copy-done.2), channel_id=1, source_target_pairs={{0,5},{1,6},{2,7},{3,0},{4,1},{5,2},{6,3},{7,4},{8,13},{9,14},{10,... | collective-permute-start | bytes 393224 | tf_op jit(solution)/shard_map/ppermute | solution.py:60
  68.4 2.5 fusion.30
  74.6 5.0 %collective-permute-start.5 = (bf16[256,256]{1,0:T(8,128)(2,1)S(1)}, bf16[256,256]{1,0:T(8,128)(2,1)S(1)}, u32[]{:S(2)}, u32[]{:S(2)}) collective-permute-start(bf16[256,256]{1,0:T(8,128)(2,1)S(1)} %copy-done.2), channel_id=1, source_target_pairs={{0,6},{1,7},{2,0},{3,1},{4,2},{5,3},{6,4},{7,5},{8,14},{9,15},{10,... | collective-permute-start | bytes 393224 | tf_op jit(solution)/shard_map/ppermute | solution.py:60
  80.3 3.1 %collective-permute-start.6 = (bf16[256,256]{1,0:T(8,128)(2,1)S(1)}, bf16[256,256]{1,0:T(8,128)(2,1)S(1)}, u32[]{:S(2)}, u32[]{:S(2)}) collective-permute-start(bf16[256,256]{1,0:T(8,128)(2,1)S(1)} %copy-done.2), channel_id=1, source_target_pairs={{0,7},{1,0},{2,1},{3,2},{4,3},{5,4},{6,5},{7,6},{8,15},{9,8},{10,9... | collective-permute-start | bytes 393224 | tf_op jit(solution)/shard_map/ppermute | solution.py:60
  88.8 1.9 gather_fusion
  92.2 3.0 %copy.55 = f32[256,8,256]{0,2,1:T(8,128)} copy(f32[256,8,256]{2,0,1:T(8,128)} %convert_bitcast_fusion) | data formatting | bytes 4194304 | tf_op jit(solution)/shard_map/convert_element_type | solution.py:16
  97.6 45.4 %all-gather.2.cloned.1.call-done = bf16[2048,1792]{1,0:T(8,128)(2,1)} async-done(((bf16[32,1792]{1,0:T(8,128)(2,1)}), bf16[2048,1792]{1,0:T(8,128)(2,1)}) %all-gather.2.cloned.1.call-update) | async-done | bytes 7340048 | tf_op jit(solution)/shard_map/all_gather | solution.py:178
  143.0 2.9 %fusion.16 = f32[256,768]{1,0:T(8,128)S(1)} fusion(bf16[256,2048]{0,1:T(8,128)(2,1)S(1)} %fusion.15, bf16[2048,1792]{1,0:T(8,128)(2,1)} %all-gather.2.cloned.1.call-done, f32[768]{0:T(1024)} %add.184), kind=kOutput, calls=%fused_computation.25 | convolution fusion | flops 805502976 | bytes 4984832 | tf_op jit(solution)/shard_map/dot_general | solution.py:46
  149.0 2.3 slice.87.wd_ref
  151.3 9.7 %all-to-all-done.1.kc_ref.vc_ref = bf16[64,2,2,32,256]{4,3,2,1,0:T(8,128)(2,1)} async-done(((bf16[64,2,2,32,256]{4,3,2,1,0:T(8,128)(2,1)}), bf16[64,2,2,32,256]{4,3,2,1,0:T(8,128)(2,1)}, u32[]{:S(2)}, u32[]{:S(2)}) %all-to-all-start.1) | async-done | bytes 4194336 | tf_op jit(solution)/shard_map/all_to_all | solution.py:215
  161.0 13.8 %shard_map.167 = bf16[256,2048]{1,0:T(8,128)(2,1)} custom-call(bf16[256,256]{1,0:T(8,128)(2,1)} %copy.61.q_ref, bf16[64,2,2,32,256]{4,3,2,1,0:T(8,128)(2,1)} %all-to-all-done.1.kc_ref.vc_ref, bf16[64,2,2,32,256]{4,3,2,1,0:T(8,128)(2,1)} %all-to-all-done.1.kc_ref.vc_ref, bf16[256,256]{1,0:T(8,128)(2,1)} %copy.62.kn_ref, bf16[256,256]{1,0:T(8,128)(2,1)} %bitcast.111, ...), custom_call_target="tpu_custom_call" | custom-call | tf_op jit(solution)/shard_map/pallas_call | solution.py:128
  174.7 2.3 copy.73
  177.0 6.8 %all-to-all-start.2 = ((bf16[256,8,256]{2,0,1:T(8,128)(2,1)}), bf16[256,8,256]{2,0,1:T(8,128)(2,1)S(1)}, u32[]{:S(2)}, u32[]{:S(2)}) async-start(bf16[256,8,256]{2,0,1:T(8,128)(2,1)} %bitcast.102), calls=%async_computation.2 | async-start | bytes 2097152 | tf_op jit(solution)/shard_map/all_to_all | solution.py:237
  184.6 28.5 %all-to-all-done.2 = bf16[256,8,256]{2,0,1:T(8,128)(2,1)S(1)} async-done(((bf16[256,8,256]{2,0,1:T(8,128)(2,1)}), bf16[256,8,256]{2,0,1:T(8,128)(2,1)S(1)}, u32[]{:S(2)}, u32[]{:S(2)}) %all-to-all-start.2) | async-done | bytes 1048608 | tf_op jit(solution)/shard_map/all_to_all | solution.py:237
  215.4 3.7 %all-to-all-start.3 = ((bf16[8,256,256]{1,2,0:T(8,128)(2,1)}), bf16[8,256,256]{1,2,0:T(8,128)(2,1)S(1)}, u32[]{:S(2)}, u32[]{:S(2)}) async-start(bf16[8,256,256]{1,2,0:T(8,128)(2,1)} %broadcast_in_dim.56), calls=%async_computation.3 | async-start | bytes 2097152 | tf_op jit(solution)/shard_map/all_to_all | solution.py:53
  219.1 29.1 %all-to-all-done.3 = bf16[8,256,256]{1,2,0:T(8,128)(2,1)S(1)} async-done(((bf16[8,256,256]{1,2,0:T(8,128)(2,1)}), bf16[8,256,256]{1,2,0:T(8,128)(2,1)S(1)}, u32[]{:S(2)}, u32[]{:S(2)}) %all-to-all-start.3) | async-done | bytes 1048608 | tf_op jit(solution)/shard_map/all_to_all | solution.py:53
  249.6 2.9 %fusion.22 = bf16[256,768]{1,0:T(8,128)(2,1)S(1)} fusion(bf16[256,2048]{0,1:T(8,128)(2,1)S(1)} %fusion.9, bf16[2048,1792]{1,0:T(8,128)(2,1)} %all-gather.2.cloned.1.call-done, f32[768]{0:T(1024)S(1)} %add.204), kind=kOutput, calls=%fused_computation.27 | convolution fusion | flops 805699584 | bytes 4590592 | tf_op jit(solution)/shard_map/dot_general | solution.py:46
  (110 shorter events, 30.1 us)
Async XLA Ops:
  7.2 30.6 %copy-start = (bf16[48,2,32,256]{3,2,1,0:T(8,128)(2,1)S(1)}, bf16[48,2,32,256]{3,2,1,0:T(8,128)(2,1)}, u32[]{:S(2)}) copy-start(bf16[48,2,32,256]{3,2,1,0:T(8,128)(2,1)} %param.22) | copy-start | bytes 4718596
  7.2 135.9 %all-gather.2.cloned.1.call-start = ((), (), s32[]{:S(2)}) async-start(), calls=%async_computation.4 | async-start | bytes 7454720 | tf_op jit(solution)/shard_map/all_gather | solution.py:178
  40.6 5.9 %copy-start.2 = (bf16[256,256]{1,0:T(8,128)(2,1)S(1)}, bf16[256,256]{1,0:T(8,128)(2,1)}, u32[]{:S(2)}) copy-start(bf16[256,256]{1,0:T(8,128)(2,1)} %param.16) | copy-start | bytes 393220
  40.6 26.4 %copy-start.7 = (s32[256]{0:T(256)S(1)}, s32[256]{0:T(256)}, u32[]{:S(2)}) copy-start(s32[256]{0:T(256)} %param.29) | copy-start | bytes 3076
  40.6 27.1 %copy-start.6 = (s32[4]{0:T(128)S(1)}, s32[4]{0:T(128)}, u32[]{:S(2)}) copy-start(s32[4]{0:T(128)} %param.30) | copy-start | bytes 52
  40.6 31.9 %copy-start.12 = (f32[3,256]{1,0:T(4,128)S(1)}, f32[3,256]{1,0:T(4,128)}, u32[]{:S(2)}) copy-start(f32[3,256]{1,0:T(4,128)} %param.21) | copy-start | bytes 9220
  40.7 120.3 %all-to-all-start.1 = ((bf16[64,2,2,32,256]{4,3,2,1,0:T(8,128)(2,1)}), bf16[64,2,2,32,256]{4,3,2,1,0:T(8,128)(2,1)}, u32[]{:S(2)}, u32[]{:S(2)}) async-start(bf16[64,2,2,32,256]{4,3,2,1,0:T(8,128)(2,1)} %bitcast.101), calls=%async_computation.1 | async-start | bytes 8388608 | tf_op jit(solution)/shard_map/all_to_all | solution.py:215
  46.5 28.1 %collective-permute-start = (bf16[256,256]{1,0:T(8,128)(2,1)S(1)}, bf16[256,256]{1,0:T(8,128)(2,1)S(1)}, u32[]{:S(2)}, u32[]{:S(2)}) collective-permute-start(bf16[256,256]{1,0:T(8,128)(2,1)S(1)} %copy-done.2), channel_id=1, source_target_pairs={{0,1},{1,2},{2,3},{3,4},{4,5},{5,6},{6,7},{7,0},{8,9},{9,10},{10,1... | collective-permute-start | bytes 393224 | tf_op jit(solution)/shard_map/ppermute | solution.py:60
  49.7 30.6 %collective-permute-start.1 = (bf16[256,256]{1,0:T(8,128)(2,1)S(1)}, bf16[256,256]{1,0:T(8,128)(2,1)S(1)}, u32[]{:S(2)}, u32[]{:S(2)}) collective-permute-start(bf16[256,256]{1,0:T(8,128)(2,1)S(1)} %copy-done.2), channel_id=1, source_target_pairs={{0,2},{1,3},{2,4},{3,5},{4,6},{5,7},{6,0},{7,1},{8,10},{9,11},{10,... | collective-permute-start | bytes 393224 | tf_op jit(solution)/shard_map/ppermute | solution.py:60
  53.9 30.2 %collective-permute-start.2 = (bf16[256,256]{1,0:T(8,128)(2,1)S(1)}, bf16[256,256]{1,0:T(8,128)(2,1)S(1)}, u32[]{:S(2)}, u32[]{:S(2)}) collective-permute-start(bf16[256,256]{1,0:T(8,128)(2,1)S(1)} %copy-done.2), channel_id=1, source_target_pairs={{0,3},{1,4},{2,5},{3,6},{4,7},{5,0},{6,1},{7,2},{8,11},{9,12},{10,... | collective-permute-start | bytes 393224 | tf_op jit(solution)/shard_map/ppermute | solution.py:60
  58.6 26.2 %collective-permute-start.3 = (bf16[256,256]{1,0:T(8,128)(2,1)S(1)}, bf16[256,256]{1,0:T(8,128)(2,1)S(1)}, u32[]{:S(2)}, u32[]{:S(2)}) collective-permute-start(bf16[256,256]{1,0:T(8,128)(2,1)S(1)} %copy-done.2), channel_id=1, source_target_pairs={{0,4},{1,5},{2,6},{3,7},{4,0},{5,1},{6,2},{7,3},{8,12},{9,13},{10,... | collective-permute-start | bytes 393224 | tf_op jit(solution)/shard_map/ppermute | solution.py:60
  62.1 23.3 %collective-permute-start.4 = (bf16[256,256]{1,0:T(8,128)(2,1)S(1)}, bf16[256,256]{1,0:T(8,128)(2,1)S(1)}, u32[]{:S(2)}, u32[]{:S(2)}) collective-permute-start(bf16[256,256]{1,0:T(8,128)(2,1)S(1)} %copy-done.2), channel_id=1, source_target_pairs={{0,5},{1,6},{2,7},{3,0},{4,1},{5,2},{6,3},{7,4},{8,13},{9,14},{10,... | collective-permute-start | bytes 393224 | tf_op jit(solution)/shard_map/ppermute | solution.py:60
  68.3 6.3 %copy-start.5 = (s32[256]{0:T(256)}, s32[256]{0:T(256)S(1)}, u32[]{:S(2)}) copy-start(s32[256]{0:T(256)S(1)} %broadcast_subtract_fusion) | copy-start | bytes 3076
  74.6 11.4 %collective-permute-start.5 = (bf16[256,256]{1,0:T(8,128)(2,1)S(1)}, bf16[256,256]{1,0:T(8,128)(2,1)S(1)}, u32[]{:S(2)}, u32[]{:S(2)}) collective-permute-start(bf16[256,256]{1,0:T(8,128)(2,1)S(1)} %copy-done.2), channel_id=1, source_target_pairs={{0,6},{1,7},{2,0},{3,1},{4,2},{5,3},{6,4},{7,5},{8,14},{9,15},{10,... | collective-permute-start | bytes 393224 | tf_op jit(solution)/shard_map/ppermute | solution.py:60
  80.3 7.8 %collective-permute-start.6 = (bf16[256,256]{1,0:T(8,128)(2,1)S(1)}, bf16[256,256]{1,0:T(8,128)(2,1)S(1)}, u32[]{:S(2)}, u32[]{:S(2)}) collective-permute-start(bf16[256,256]{1,0:T(8,128)(2,1)S(1)} %copy-done.2), channel_id=1, source_target_pairs={{0,7},{1,0},{2,1},{3,2},{4,3},{5,4},{6,5},{7,6},{8,15},{9,8},{10,9... | collective-permute-start | bytes 393224 | tf_op jit(solution)/shard_map/ppermute | solution.py:60
  92.2 3.6 %copy-start.8 = (f32[2048]{0:T(1024)S(1)}, f32[2048]{0:T(1024)}, u32[]{:S(2)}) copy-start(f32[2048]{0:T(1024)} %param.19) | copy-start | bytes 24580
  92.2 3.7 %copy-start.9 = (f32[2048]{0:T(1024)S(1)}, f32[2048]{0:T(1024)}, u32[]{:S(2)}) copy-start(f32[2048]{0:T(1024)} %param.18) | copy-start | bytes 24580
  95.2 1.6 copy-start.1
  177.0 36.1 %all-to-all-start.2 = ((bf16[256,8,256]{2,0,1:T(8,128)(2,1)}), bf16[256,8,256]{2,0,1:T(8,128)(2,1)S(1)}, u32[]{:S(2)}, u32[]{:S(2)}) async-start(bf16[256,8,256]{2,0,1:T(8,128)(2,1)} %bitcast.102), calls=%async_computation.2 | async-start | bytes 2097152 | tf_op jit(solution)/shard_map/all_to_all | solution.py:237
  213.2 5.9 %copy-start.13 = (f32[3,256]{1,0:T(4,128)S(1)}, f32[3,256]{1,0:T(4,128)}, u32[]{:S(2)}) copy-start(f32[3,256]{1,0:T(4,128)} %param.28) | copy-start | bytes 9220
  214.2 34.3 %copy-start.3 = (bf16[256,256]{1,0:T(8,128)(2,1)}, bf16[256,256]{1,0:T(8,128)(2,1)S(1)}, u32[]{:S(2)}) copy-start(bf16[256,256]{1,0:T(8,128)(2,1)S(1)} %add_convert_fusion) | copy-start | bytes 393220
  215.4 33.5 %copy-start.10 = (f32[2048]{0:T(1024)S(1)}, f32[2048]{0:T(1024)}, u32[]{:S(2)}) copy-start(f32[2048]{0:T(1024)} %param.26) | copy-start | bytes 24580
  215.4 33.5 %copy-start.11 = (f32[2048]{0:T(1024)S(1)}, f32[2048]{0:T(1024)}, u32[]{:S(2)}) copy-start(f32[2048]{0:T(1024)} %param.25) | copy-start | bytes 24580
  215.4 32.9 %all-to-all-start.3 = ((bf16[8,256,256]{1,2,0:T(8,128)(2,1)}), bf16[8,256,256]{1,2,0:T(8,128)(2,1)S(1)}, u32[]{:S(2)}, u32[]{:S(2)}) async-start(bf16[8,256,256]{1,2,0:T(8,128)(2,1)} %broadcast_in_dim.56), calls=%async_computation.3 | async-start | bytes 2097152 | tf_op jit(solution)/shard_map/all_to_all | solution.py:53
  (1 other events, 0.7 us)
Sparse Core Ops, SparseCore 0:
  11.9 131.0 all-gather.1
